TPU v7x, 256 devices: a whole 4x4x8 slice. The times are simulated.
256 devices in a mesh: oi: 16 (over y, x_hi, core), oj: 16 (over z, x_lo).
Axes of the slice: x: 4 (x_hi: 2, x_lo: 2; x = x_hi * 2 + x_lo), y: 4, z: 8, core: 2. Of those that a mesh axis runs over, the one named last changes fastest.
Arguments:
- amps: bfloat16 [64, 64, 32768], P('oi', 'oj'), may hold values from -6 to 6
- ladder_w: bfloat16 [2016, 2016], P('oj'), may hold values from -0.125 to 0.125
- fock: bfloat16 [64, 64], replicated, may hold values from -0.75 to 0.75
- eps_occ: float32 [64], replicated, may hold values from -2 to -0.3
- eps_pair: float32 [32768], replicated, may hold values from 0.5 to 4
Outputs:
- update: bfloat16 [64, 64, 32768], P('oi', 'oj')
All inputs are finite; a program needn't handle non-finite values.
Results may differ from a plain program's by a relative error of at most 0.0054.
Values may be sent and summed in bfloat16 or wider, within the bound.
No kernel may reach another device: no remote copies, remote signals or barrier semaphores. Data moves between devices by JAX's collectives and lax.ppermute only.
A program may use at most 128 MiB of HBM per device.

v0:
```python
import jax
import jax.numpy as jnp
import numpy as np
from jax import lax
from jax.sharding import PartitionSpec as P


def pair_tables(occ):
    first, second = np.triu_indices(occ, 1)
    upper = (first * occ + second).astype(np.int32)
    lower = (second * occ + first).astype(np.int32)
    npairs = upper.shape[0]
    expand = np.full((occ * occ,), 2 * npairs, dtype=np.int32)
    expand[upper] = np.arange(npairs, dtype=np.int32)
    expand[lower] = npairs + np.arange(npairs, dtype=np.int32)
    return (upper, lower, expand)


def divide_out(resid, energies, first_eps, second_eps):
    denom = energies[None, None, :] - first_eps[:, None, None] - second_eps[None, :, None]
    held = lax.optimization_barrier(resid)
    return (held.astype(jnp.float32) / denom).astype(jnp.bfloat16)


def on_device(amps, ladder_w, fock, eps_occ, eps_pair):
    pair_amps = lax.all_to_all(
        lax.all_to_all(amps, "oi", split_axis=2, concat_axis=0, tiled=True),
        "oj",
        split_axis=2,
        concat_axis=1,
        tiled=True,
    )
    occ = pair_amps.shape[0]
    width = pair_amps.shape[2]
    upper, lower, expand = pair_tables(occ)
    flat = pair_amps.reshape(occ * occ, width)
    anti = (flat[upper].astype(jnp.float32) - flat[lower].astype(jnp.float32)).astype(jnp.bfloat16)
    contract = (((0,), (0,)), ((), ()))
    whole_w = lax.all_gather(ladder_w, "oj", axis=0, tiled=True)
    ladder = lax.dot_general(
        whole_w, anti[:, 0 : 0 + width], contract, preferred_element_type=jnp.float32
    )
    mixed = jnp.einsum("ikp,kj->ijp", pair_amps, fock, preferred_element_type=jnp.float32)
    filler = jnp.zeros((1, width), jnp.float32)
    full = jnp.concatenate([ladder, -ladder, filler], axis=0)[expand].reshape(occ, occ, width)
    resid = (full - (mixed - jnp.transpose(mixed, (1, 0, 2)))).astype(jnp.bfloat16)
    outgoing = resid.reshape(occ, occ, 1, 1, width)
    landed = lax.all_to_all(
        lax.all_to_all(outgoing, "oi", split_axis=0, concat_axis=2, tiled=True),
        "oj",
        split_axis=1,
        concat_axis=3,
        tiled=True,
    )
    rows_i = landed.shape[0]
    rows_j = landed.shape[1]
    arrived = landed.reshape(rows_i, rows_j, landed.shape[2] * landed.shape[3] * width)
    first_eps = lax.dynamic_slice_in_dim(eps_occ, lax.axis_index("oi") * rows_i, rows_i, 0)
    second_eps = lax.dynamic_slice_in_dim(eps_occ, lax.axis_index("oj") * rows_j, rows_j, 0)
    return divide_out(arrived, eps_pair, first_eps, second_eps)


def solution(mesh):
    in_specs = (P("oi", "oj", None), P("oj", None), P(), P(), P())
    out_specs = P("oi", "oj", None)
    return jax.shard_map(
        on_device, mesh=mesh, in_specs=in_specs, out_specs=out_specs, check_vma=False
    )
```

profile of v0, /device:TPU:1, one launch (start us, length us, event | category | flops | bytes accessed | tf_op | source)
XLA Modules:
  0.0 458.2 jit_solution(2015257166413810704)
XLA Ops:
  6.5 0.0 copy-start
  6.5 0.0 all-gather.3.cloned.1.call-start
  6.5 0.7 all-gather.3.cloned.1.call-update
  7.3 34.9 %copy.33 = bf16[4,4,32768]{1,0,2:T(4,128)(2,1)} copy(bf16[4,4,32768]{2,1,0:T(4,128)(2,1)} %param.11) | data formatting | bytes 2097152 | tf_op args[0]
  42.1 67.6 %reshape.75 = bf16[16,2,16384]{2,1,0:T(2,128)(2,1)S(1)} reshape(bf16[32768,4,4]{2,1,0:T(4,128)(2,1)} %bitcast.50) | data formatting | bytes 2097152
  109.8 49.6 %all_to_all.69 = bf16[16,2,16384]{2,1,0:T(2,128)(2,1)S(1)} all-to-all(bf16[16,2,16384]{2,1,0:T(2,128)(2,1)S(1)} %reshape.75), channel_id=1, replica_groups=mesh['oi'=16,'oj'=16] {'oi'}, dimensions={0} | all-to-all | bytes 2097152 | tf_op jit(solution)/shard_map/all_to_all | solution.py:27
  159.4 73.1 %reshape.76 = bf16[32768,4,4]{2,1,0:T(4,128)(2,1)} reshape(bf16[16,2,16384]{2,1,0:T(2,128)(2,1)S(1)} %all_to_all.69) | data formatting | bytes 2097152
  232.5 47.0 %copy.34 = bf16[4,4,16,2048]{3,1,0,2:T(4,128)(2,1)S(1)} copy(bf16[4,4,16,2048]{1,0,3,2:T(4,128)(2,1)} %bitcast.49) | data formatting | bytes 2097152 | tf_op jit(solution)/shard_map/all_to_all | solution.py:27
  279.4 1.7 copy.35
  281.1 0.0 copy-start.4
  281.2 0.0 copy-start.3
  281.2 0.0 copy-start.2
  281.2 2.2 reshape.77
  283.4 7.1 %all-to-all-start.1 = ((bf16[16,2,16384]{2,1,0:T(2,128)(2,1)}), bf16[16,2,16384]{2,1,0:T(2,128)(2,1)S(1)}, u32[]{:S(2)}, u32[]{:S(2)}) async-start(bf16[16,2,16384]{2,1,0:T(2,128)(2,1)} %reshape.77), calls=%async_computation.1 | async-start | bytes 2097152 | tf_op jit(solution)/shard_map/all_to_all | solution.py:26
  290.5 0.1 pad.2.clone
  290.6 0.0 copy-done.4
  290.6 0.0 copy-done.3
  290.6 0.0 copy-done.2
  290.7 25.0 %all-to-all-done.1 = bf16[16,2,16384]{2,1,0:T(2,128)(2,1)S(1)} async-done(((bf16[16,2,16384]{2,1,0:T(2,128)(2,1)}), bf16[16,2,16384]{2,1,0:T(2,128)(2,1)S(1)}, u32[]{:S(2)}, u32[]{:S(2)}) %all-to-all-start.1) | async-done | bytes 1048608 | tf_op jit(solution)/shard_map/all_to_all | solution.py:26
  315.7 1.3 reshape.78
  317.0 1.4 copy.36
  318.4 6.3 %gather_fusion.1 = bf16[2016,128]{1,0:T(8,128)(2,1)S(1)} fusion(bf16[4096,128]{1,0:T(8,128)(2,1)S(1)} %bitcast.51, s32[2048]{0:T(1024)S(1)} %pad_clamp_fusion), kind=kCustom, calls=%fused_computation.1 | custom fusion | bytes 1040256 | tf_op jit(solution)/shard_map/gather | solution.py:37
  324.8 6.3 %gather_fusion = bf16[2016,128]{1,0:T(8,128)(2,1)S(1)} fusion(bf16[4096,128]{1,0:T(8,128)(2,1)S(1)} %bitcast.52, s32[2048]{0:T(1024)S(1)} %pad_clamp_fusion.1), kind=kCustom, calls=%fused_computation | custom fusion | bytes 1040256 | tf_op jit(solution)/shard_map/gather | solution.py:37
  331.1 0.0 copy-done
  331.1 1.8 fusion.4
  332.9 0.0 all-gather.3.cloned.1.call-done
  332.9 14.1 %copy.37 = bf16[16,126,2016]{1,0,2:T(8,128)(2,1)} copy(bf16[16,126,2016]{1,2,0:T(8,128)(2,1)} %all-gather.3.cloned.1.call-done) | data formatting | bytes 16257024 | tf_op jit(solution)/shard_map/all_gather | solution.py:39
  347.1 15.7 %reshape.72 = bf16[2016,2016]{0,1:T(8,128)(2,1)} reshape(bf16[16,126,2016]{1,0,2:T(8,128)(2,1)} %copy.37) | data formatting | bytes 16257024
  362.8 5.7 %fusion.7 = (f32[2016,128]{1,0:T(8,128)S(1)}, f32[2016,128]{1,0:T(8,128)S(1)}) fusion(bf16[2016,2016]{0,1:T(8,128)(2,1)} %reshape.72, bf16[2016,128]{1,0:T(8,128)(2,1)S(1)} %gather_fusion.1, bf16[2016,128]{1,0:T(8,128)(2,1)S(1)} %gather_fusion), kind=kOutput, calls=%fused_computation.20 | convolution fusion | flops 1041739776 | bytes 11225088 | tf_op jit(solution)/shard_map/dot_general | solution.py:40
  368.5 3.1 maximum_maximum_fusion
  371.6 14.2 %gather_fusion.2 = f32[4096,128]{1,0:T(8,128)} fusion(f32[4033,128]{1,0:T(8,128)S(1)} %maximum_maximum_fusion, s32[4096]{0:T(1024)S(1)} %broadcast_clamp_fusion), kind=kCustom, calls=%fused_computation.2 | custom fusion | bytes 4210688 | tf_op jit(solution)/shard_map/gather | solution.py:45
  385.8 5.2 %fusion.3 = bf16[64,64,1,1,128]{4,0,1,3,2:T(8,128)(2,1)S(1)} fusion(f32[64,64,128]{2,0,1:T(8,128)} %fusion.4, f32[64,64,128]{2,1,0:T(8,128)} %bitcast.56), kind=kLoop, calls=%fused_computation.10 | loop fusion | flops 1572864 | bytes 5242880 | tf_op jit(solution)/shard_map/reshape | solution.py:47
  391.1 0.0 copy-start.5
  391.1 1.6 copy.41
  392.7 8.0 %all-to-all-start.2 = ((bf16[64,64,1,1,128]{4,1,3,2,0:T(8,128)(2,1)}), bf16[64,64,1,1,128]{4,1,3,2,0:T(8,128)(2,1)S(1)}, u32[]{:S(2)}, u32[]{:S(2)}) async-start(bf16[64,64,1,1,128]{4,1,3,2,0:T(8,128)(2,1)} %copy.41), calls=%async_computation.2 | async-start | bytes 2097152 | tf_op jit(solution)/shard_map/all_to_all | solution.py:49
  400.7 0.0 copy-done.5
  400.7 0.1 fusion.6
  400.8 17.0 %all-to-all-done.2 = bf16[64,64,1,1,128]{4,1,3,2,0:T(8,128)(2,1)S(1)} async-done(((bf16[64,64,1,1,128]{4,1,3,2,0:T(8,128)(2,1)}), bf16[64,64,1,1,128]{4,1,3,2,0:T(8,128)(2,1)S(1)}, u32[]{:S(2)}, u32[]{:S(2)}) %all-to-all-start.2) | async-done | bytes 1048608 | tf_op jit(solution)/shard_map/all_to_all | solution.py:49
  417.8 0.0 copy-start.1
  417.8 1.8 copy.53
  419.6 3.7 all-to-all-start.3
  423.2 0.0 copy-done.1
  423.2 0.2 broadcast_subtract_fusion
  423.4 25.2 %all-to-all-done.3 = bf16[4,64,16,1,128]{4,0,2,3,1:T(4,128)(2,1)S(1)} async-done(((bf16[4,64,16,1,128]{4,0,2,3,1:T(4,128)(2,1)}), bf16[4,64,16,1,128]{4,0,2,3,1:T(4,128)(2,1)S(1)}, u32[]{:S(2)}, u32[]{:S(2)}) %all-to-all-start.3) | async-done | bytes 1048608 | tf_op jit(solution)/shard_map/all_to_all | solution.py:48
  448.6 0.7 copy.43
  449.2 0.4 reshape.46
  449.6 1.8 fusion.2
  (3 shorter events, 0.0 us)
Async XLA Ops:
  6.5 324.6 %copy-start = (bf16[64,64]{1,0:T(8,128)(2,1)S(1)}, bf16[64,64]{1,0:T(8,128)(2,1)}, u32[]{:S(2)}) copy-start(bf16[64,64]{1,0:T(8,128)(2,1)} %param.13) | copy-start | bytes 24580
  6.5 326.4 %all-gather.3.cloned.1.call-start = ((), (), s32[]{:S(2)}) async-start(), calls=%async_computation.4 | async-start | bytes 8773632 | tf_op jit(solution)/shard_map/all_gather | solution.py:39
  281.1 9.5 %copy-start.4 = (s32[2016]{0:T(1024)S(1)}, s32[2016]{0:T(1024)}, u32[]{:S(2)}) copy-start(s32[2016]{0:T(1024)} %constant.39) | copy-start | bytes 24196
  281.2 9.5 %copy-start.3 = (s32[2016]{0:T(1024)S(1)}, s32[2016]{0:T(1024)}, u32[]{:S(2)}) copy-start(s32[2016]{0:T(1024)} %constant.38) | copy-start | bytes 24196
  281.2 9.5 %copy-start.2 = (s32[4096]{0:T(1024)S(1)}, s32[4096]{0:T(1024)}, u32[]{:S(2)}) copy-start(s32[4096]{0:T(1024)} %constant.40) | copy-start | bytes 49156
  283.4 32.3 %all-to-all-start.1 = ((bf16[16,2,16384]{2,1,0:T(2,128)(2,1)}), bf16[16,2,16384]{2,1,0:T(2,128)(2,1)S(1)}, u32[]{:S(2)}, u32[]{:S(2)}) async-start(bf16[16,2,16384]{2,1,0:T(2,128)(2,1)} %reshape.77), calls=%async_computation.1 | async-start | bytes 2097152 | tf_op jit(solution)/shard_map/all_to_all | solution.py:26
  391.1 9.7 %copy-start.5 = (f32[64]{0:T(128)S(1)}, f32[64]{0:T(128)}, u32[]{:S(2)}) copy-start(f32[64]{0:T(128)} %param.14) | copy-start | bytes 772
  392.7 25.1 %all-to-all-start.2 = ((bf16[64,64,1,1,128]{4,1,3,2,0:T(8,128)(2,1)}), bf16[64,64,1,1,128]{4,1,3,2,0:T(8,128)(2,1)S(1)}, u32[]{:S(2)}, u32[]{:S(2)}) async-start(bf16[64,64,1,1,128]{4,1,3,2,0:T(8,128)(2,1)} %copy.41), calls=%async_computation.2 | async-start | bytes 2097152 | tf_op jit(solution)/shard_map/all_to_all | solution.py:49
  417.8 5.5 %copy-start.1 = (f32[32768]{0:T(1024)S(1)}, f32[32768]{0:T(1024)}, u32[]{:S(2)}) copy-start(f32[32768]{0:T(1024)} %param.15) | copy-start | bytes 393220
  419.6 29.0 %all-to-all-start.3 = ((bf16[4,64,16,1,128]{4,0,2,3,1:T(4,128)(2,1)}), bf16[4,64,16,1,128]{4,0,2,3,1:T(4,128)(2,1)S(1)}, u32[]{:S(2)}, u32[]{:S(2)}) async-start(bf16[4,64,16,1,128]{4,0,2,3,1:T(4,128)(2,1)} %bitcast.48), calls=%async_computation.3 | async-start | bytes 2097152 | tf_op jit(solution)/shard_map/all_to_all | solution.py:48
Sparse Core Ops, SparseCore 0:
  9.1 194.0 all-gather.2
where the time goes:
time: 465 us; the launch traced here: 458 us
  local copies, waits for them, and re-layouts  291 us (63%)
  waiting for transfers between devices  67.9 us (15%)
  blocking collectives  49.6 us (11%)
  starting transfers between devices  18.7 us (4%)
  between operations  13.6 us (3%)
  other arithmetic  10.3 us (2%)
  matrix products  7.52 us (2%)
    unnamed x18, local copies, waits for them, and re-layouts  195 us
    all_to_all x1, blocking collectives, on_device(): lax.all_to_all(amps, 'oi', split_axis=2, concat_axis=0, tiled=True)  49.6 us
    all_to_all x2, local copies, waits for them, and re-layouts, on_device(): lax.all_to_all(amps, 'oi', split_axis=2, concat_axis=0, tiled=True)  48.7 us
    all_to_all x1, waiting for transfers between devices, on_device(): lax.all_to_all(lax.all_to_all(outgoing, 'oi', split_axis=0, concat_axis=2...  25.2 us
    all_to_all x1, waiting for transfers between devices, on_device(): lax.all_to_all(lax.all_to_all(amps, 'oi', split_axis=2, concat_axis=0, ti...  25 us
    all_to_all x1, waiting for transfers between devices, on_device(): lax.all_to_all(outgoing, 'oi', split_axis=0, concat_axis=2, tiled=True)  17 us
    gather x1, local copies, waits for them, and re-layouts, on_device(): jnp.concatenate([ladder, -ladder, filler], axis=0)[expand]  14.2 us
    all_gather x1, local copies, waits for them, and re-layouts, on_device(): whole_w = lax.all_gather(ladder_w, 'oj', axis=0, tiled=True)  14.1 us
  transfers between devices with their start and end apart: 4, of which 3 were waited for; matrix products, arithmetic and copies ran while one was open for 53% of the time, Pallas kernels for 0%

commit v1 on v0

v1 whole, which is shorter than its diff:
```python
import jax
import jax.numpy as jnp
import numpy as np
from jax import lax
from jax.sharding import PartitionSpec as P


def pair_tables(occ):
    first, second = np.triu_indices(occ, 1)
    upper = (first * occ + second).astype(np.int32)
    lower = (second * occ + first).astype(np.int32)
    npairs = upper.shape[0]
    spread = np.full((occ * occ,), npairs, dtype=np.int32)
    spread[upper] = np.arange(npairs, dtype=np.int32)
    return (upper, lower, spread)


def on_device(amps, ladder_w, fock, eps_occ, eps_pair):
    rows_i, rows_j, total = amps.shape
    n_oi = lax.axis_size("oi")
    n_oj = lax.axis_size("oj")
    ndev = n_oi * n_oj
    width = total // ndev
    occ = rows_i * n_oi
    me_i = lax.axis_index("oi")
    me_j = lax.axis_index("oj")
    me = me_i * n_oj + me_j
    core = me_i % 2
    partner = [(a, a ^ 1) for a in range(n_oi)]

    send = amps.reshape(rows_i, rows_j, ndev, width).transpose(2, 0, 1, 3)
    recv = lax.all_to_all(send, ("oi", "oj"), 0, 0, tiled=True)
    pair_amps = (
        recv.reshape(n_oi, n_oj, rows_i, rows_j, width)
        .transpose(0, 2, 1, 3, 4)
        .reshape(occ, occ, width)
    )

    upper, lower, spread = pair_tables(occ)
    npairs = upper.shape[0]
    half = npairs // 2
    flat = pair_amps.reshape(occ * occ, width)
    anti = (flat[upper].astype(jnp.float32) - flat[lower].astype(jnp.float32)).astype(jnp.bfloat16)

    anti_other = lax.ppermute(anti, "oi", partner)
    w_part = lax.dynamic_slice_in_dim(ladder_w, core * half, half, 1)
    w_half = lax.all_gather(w_part, "oj", axis=0, tiled=True)
    both = jnp.concatenate([anti, anti_other], axis=1)
    contract = (((0,), (0,)), ((), ()))
    lad = lax.dot_general(w_half, both, contract, preferred_element_type=jnp.float32)
    lad_mine = lad[:, :width]
    lad_other = lax.ppermute(lad[:, width:], "oi", partner)
    first = jnp.where(core == 0, lad_mine, lad_other)
    second = jnp.where(core == 0, lad_other, lad_mine)
    ladder = jnp.concatenate([first, second, jnp.zeros((1, width), jnp.float32)], axis=0)

    upper_part = ladder[spread].reshape(occ, occ, width)
    mixed = jnp.einsum("ikp,kj->ijp", pair_amps, fock, preferred_element_type=jnp.float32)
    x = upper_part - mixed
    resid = x - jnp.transpose(x, (1, 0, 2))
    resid = lax.reduce_precision(resid, exponent_bits=8, mantissa_bits=7)
    energies = lax.dynamic_slice_in_dim(eps_pair, me * width, width, 0)
    denom = energies[None, None, :] - eps_occ[:, None, None] - eps_occ[None, :, None]
    upd = (resid / denom).astype(jnp.bfloat16)

    out_send = (
        upd.reshape(n_oi, rows_i, n_oj, rows_j, width)
        .transpose(0, 2, 1, 3, 4)
        .reshape(ndev, rows_i, rows_j, width)
    )
    out_recv = lax.all_to_all(out_send, ("oi", "oj"), 0, 0, tiled=True)
    return out_recv.transpose(1, 2, 0, 3).reshape(rows_i, rows_j, total)


def solution(mesh):
    in_specs = (P("oi", "oj", None), P("oj", None), P(), P(), P())
    out_specs = P("oi", "oj", None)
    return jax.shard_map(
        on_device, mesh=mesh, in_specs=in_specs, out_specs=out_specs, check_vma=False
    )
```

time: 465 us -> 214 us (0.46); the launches traced: 458 us -> 213 us
  local copies, waits for them, and re-layouts: 291 us -> 51.7 us
  waiting for transfers between devices: 67.9 us -> 79.6 us
  other arithmetic: 10.3 us -> 2.01 us
  blocking collectives: 49.6 us -> 43.5 us
    unnamed x18 -> x14, local copies, waits for them, and re-layouts: 195 us -> 10.2 us
    all_to_all x5 -> x1, local copies, waits for them, and re-layouts: 52.5 us -> 0.27 us  [on_device(): recv = lax.all_to_all(send, ('oi', 'oj'), 0, 0, tiled=True)]
    all_gather x1, waiting for transfers between devices: 0.01 us -> 40.7 us  [on_device(): w_half = lax.all_gather(w_part, 'oj', axis=0, tiled=True)]
    all_to_all x3 -> x1, waiting for transfers between devices: 67.2 us -> 38.1 us  [on_device(): recv = lax.all_to_all(send, ('oi', 'oj'), 0, 0, tiled=True)]
    all_gather x1, local copies, waits for them, and re-layouts: 14.1 us -> 5.19 us  [on_device(): w_half = lax.all_gather(w_part, 'oj', axis=0, tiled=True)]
    all_to_all x1, blocking collectives: 49.6 us -> 43.5 us  [on_device(): out_recv = lax.all_to_all(out_send, ('oi', 'oj'), 0, 0, tiled=True)]
    reshape x1 -> x0, other arithmetic: 5.23 us -> none  [on_device(): outgoing = resid.reshape(occ, occ, 1, 1, width)]
    all_to_all x3 -> x1, starting transfers between devices: 18.7 us -> 15.6 us  [on_device(): recv = lax.all_to_all(send, ('oi', 'oj'), 0, 0, tiled=True)]
  transfers between devices with their start and end apart: 4 -> 4, of which waited for: 3 -> 3; matrix products, arithmetic and copies ran while one was open for 53% -> 15% of each run, Pallas kernels for 0% -> 0%
where the time goes in v1:
time: 214 us; the launch traced here: 213 us
  waiting for transfers between devices  79.6 us (37%)
  local copies, waits for them, and re-layouts  51.7 us (24%)
  blocking collectives  43.5 us (20%)
  starting transfers between devices  17.5 us (8%)
  between operations  13.6 us (6%)
  matrix products  5.61 us (3%)
    all_to_all x1, blocking collectives, on_device(): out_recv = lax.all_to_all(out_send, ('oi', 'oj'), 0, 0, tiled=True)  43.5 us
    all_gather x1, waiting for transfers between devices, on_device(): w_half = lax.all_gather(w_part, 'oj', axis=0, tiled=True)  40.7 us
    all_to_all x1, waiting for transfers between devices, on_device(): recv = lax.all_to_all(send, ('oi', 'oj'), 0, 0, tiled=True)  38.1 us
    all_to_all x1, starting transfers between devices, on_device(): recv = lax.all_to_all(send, ('oi', 'oj'), 0, 0, tiled=True)  15.6 us
    gather x1, local copies, waits for them, and re-layouts, on_device(): upper_part = ladder[spread].reshape(occ, occ, width)  14.1 us
    unnamed x14, local copies, waits for them, and re-layouts  10.2 us
    gather x1, local copies, waits for them, and re-layouts, on_device(): flat[upper].astype(jnp.float32) - flat[lower].astype(jnp.float32)  6.34 us
    gather x1, local copies, waits for them, and re-layouts, on_device(): flat[lower].astype(jnp.float32)  6.34 us
  transfers between devices with their start and end apart: 4, of which 3 were waited for; matrix products, arithmetic and copies ran while one was open for 15% of the time, Pallas kernels for 0%

profile of v1, /device:TPU:1, one launch (start us, length us, event | category | flops | bytes accessed | tf_op | source)
XLA Modules:
  0.0 213.4 jit_solution(14065660140634274733)
XLA Ops:
  6.5 0.0 copy-start
  6.5 0.0 all-gather.3.cloned.1.call-start
  6.5 1.0 copy-done
  7.6 0.7 dynamic-slice_bitcast_fusion
  8.3 0.0 all-gather.3.cloned.1.call-update
  8.3 2.1 %reshape.50 = bf16[4,4,256,128]{3,2,1,0:T(8,128)(2,1)S(1)} reshape(bf16[4,4,32768]{2,1,0:T(4,128)(2,1)} %param.11) | data formatting | bytes 2097152 | tf_op jit(solution)/shard_map/reshape | solution.py:31
  10.5 0.0 copy-start.4
  10.5 0.0 copy-start.3
  10.5 1.8 copy.34
  12.3 15.6 %all-to-all-start = ((bf16[256,4,4,128]{3,2,1,0:T(4,128)(2,1)}), bf16[256,4,4,128]{3,2,1,0:T(4,128)(2,1)S(1)}, u32[]{:S(2)}, u32[]{:S(2)}) async-start(bf16[256,4,4,128]{3,2,1,0:T(4,128)(2,1)} %copy.34), calls=%async_computation | async-start | bytes 2097152 | tf_op jit(solution)/shard_map/all_to_all | solution.py:32
  27.9 0.0 copy-done.4
  28.0 0.0 copy-done.3
  28.0 38.1 %all-to-all-done = bf16[256,4,4,128]{3,2,1,0:T(4,128)(2,1)S(1)} async-done(((bf16[256,4,4,128]{3,2,1,0:T(4,128)(2,1)}), bf16[256,4,4,128]{3,2,1,0:T(4,128)(2,1)S(1)}, u32[]{:S(2)}, u32[]{:S(2)}) %all-to-all-start) | async-done | bytes 1048608 | tf_op jit(solution)/shard_map/all_to_all | solution.py:32
  66.0 0.3 copy.35
  66.3 1.4 copy.36
  67.7 6.3 %gather_fusion = bf16[2016,128]{1,0:T(8,128)(2,1)S(1)} fusion(bf16[4096,128]{1,0:T(8,128)(2,1)S(1)} %bitcast.37, s32[2048]{0:T(1024)S(1)} %pad_clamp_fusion.1), kind=kCustom, calls=%fused_computation | custom fusion | bytes 1040256 | tf_op jit(solution)/shard_map/gather | solution.py:43
  74.0 6.3 %gather_fusion.1 = bf16[2016,128]{1,0:T(8,128)(2,1)S(1)} fusion(bf16[4096,128]{1,0:T(8,128)(2,1)S(1)} %bitcast.38, s32[2048]{0:T(1024)S(1)} %pad_clamp_fusion), kind=kCustom, calls=%fused_computation.1 | custom fusion | bytes 1040256 | tf_op jit(solution)/shard_map/gather | solution.py:43
  80.4 0.1 subtract_convert_fusion
  80.5 1.0 collective-permute-start
  81.6 40.7 %all-gather.3.cloned.1.call-done = bf16[16,126,1008]{1,2,0:T(8,128)(2,1)} async-done(((bf16[1,126,1008]{1,2,0:T(8,128)(2,1)}), bf16[16,126,1008]{1,2,0:T(8,128)(2,1)}) %all-gather.3.cloned.1.call-update) | async-done | bytes 4064272 | tf_op jit(solution)/shard_map/all_gather | solution.py:47
  122.2 5.2 %copy.33 = bf16[16,126,1008]{1,0,2:T(8,128)(2,1)} copy(bf16[16,126,1008]{1,2,0:T(8,128)(2,1)} %all-gather.3.cloned.1.call-done) | data formatting | bytes 8128512 | tf_op jit(solution)/shard_map/all_gather | solution.py:47
  127.4 8.4 %reshape.82 = bf16[2016,1008]{0,1:T(8,128)(2,1)} reshape(bf16[16,126,1008]{1,0,2:T(8,128)(2,1)} %copy.33) | data formatting | bytes 8128512
  135.8 0.0 copy-start.2
  135.8 0.0 copy-start.5
  135.8 0.0 collective-permute-done
  135.8 3.6 %fusion.3 = f32[1008,256]{1,0:T(8,128)S(1)} fusion(bf16[2016,1008]{0,1:T(8,128)(2,1)} %reshape.82, bf16[2016,128]{1,0:T(8,128)(2,1)} %collective-permute-done, bf16[2016,128]{1,0:T(8,128)(2,1)S(1)} %subtract_convert_fusion), kind=kOutput, calls=%fused_computation.10 | convolution fusion | flops 1042513920 | bytes 6128640 | tf_op jit(solution)/shard_map/dot_general | solution.py:50
  139.4 0.8 slice.15
  140.2 0.8 collective-permute-start.1
  141.0 0.1 pad.2.clone
  141.1 0.8 dynamic_slice.7
  141.9 0.0 copy-done.2
  141.9 0.0 copy-done.5
  141.9 0.1 broadcast_subtract_fusion
  141.9 0.8 collective-permute-done.1
  142.8 0.1 slice_select_fusion.1
  142.8 0.3 maximum_maximum_fusion
  143.2 0.0 copy-start.1
  143.2 14.1 %gather_fusion.2 = f32[4096,128]{1,0:T(8,128)} fusion(f32[2017,128]{1,0:T(8,128)S(1)} %maximum_maximum_fusion, s32[4096]{0:T(1024)S(1)} %broadcast_clamp_fusion), kind=kCustom, calls=%fused_computation.2 | custom fusion | bytes 4210688 | tf_op jit(solution)/shard_map/gather | solution.py:57
  157.3 0.0 copy-done.1
  157.3 2.1 bitcast_subtract_fusion.1
  159.4 1.4 fusion.2
  160.7 0.2 copy.40
  161.0 0.8 copy.41
  161.8 43.5 %all_to_all.10 = bf16[256,4,4,128]{3,2,1,0:T(4,128)(2,1)S(1)} all-to-all(bf16[256,4,4,128]{3,2,1,0:T(4,128)(2,1)S(1)} %copy.41), channel_id=1, replica_groups=mesh['oi'=16,'oj'=16] {'oi','oj'}, dimensions={0} | all-to-all | bytes 2097152 | tf_op jit(solution)/shard_map/all_to_all | solution.py:71
  205.2 1.3 copy_bitcast_fusion
  (3 shorter events, 0.0 us)
Async XLA Ops:
  6.5 1.0 copy-start
  6.5 115.7 %all-gather.3.cloned.1.call-start = ((), (), s32[]{:S(2)}) async-start(), calls=%async_computation.2 | async-start | bytes 4386816 | tf_op jit(solution)/shard_map/all_gather | solution.py:47
  10.5 17.5 %copy-start.4 = (s32[2016]{0:T(1024)S(1)}, s32[2016]{0:T(1024)}, u32[]{:S(2)}) copy-start(s32[2016]{0:T(1024)} %constant.56) | copy-start | bytes 24196
  10.5 17.5 %copy-start.3 = (s32[2016]{0:T(1024)S(1)}, s32[2016]{0:T(1024)}, u32[]{:S(2)}) copy-start(s32[2016]{0:T(1024)} %constant.57) | copy-start | bytes 24196
  12.3 53.8 %all-to-all-start = ((bf16[256,4,4,128]{3,2,1,0:T(4,128)(2,1)}), bf16[256,4,4,128]{3,2,1,0:T(4,128)(2,1)S(1)}, u32[]{:S(2)}, u32[]{:S(2)}) async-start(bf16[256,4,4,128]{3,2,1,0:T(4,128)(2,1)} %copy.34), calls=%async_computation | async-start | bytes 2097152 | tf_op jit(solution)/shard_map/all_to_all | solution.py:32
  80.5 55.3 %collective-permute-start = (bf16[2016,128]{1,0:T(8,128)(2,1)S(1)}, bf16[2016,128]{1,0:T(8,128)(2,1)}, u32[]{:S(2)}, u32[]{:S(2)}) collective-permute-start(bf16[2016,128]{1,0:T(8,128)(2,1)S(1)} %subtract_convert_fusion), channel_id=1, source_target_pairs={{0,16},{16,0},{32,48},{48,32},{64,80},{80,64},{96,112},{112,96},{1... | collective-permute-start | bytes 1548296 | tf_op jit(solution)/shard_map/ppermute | solution.py:45
  135.8 6.0 %copy-start.2 = (s32[4096]{0:T(1024)S(1)}, s32[4096]{0:T(1024)}, u32[]{:S(2)}) copy-start(s32[4096]{0:T(1024)} %constant.58) | copy-start | bytes 49156
  135.8 6.0 %copy-start.5 = (f32[64]{0:T(128)S(1)}, f32[64]{0:T(128)}, u32[]{:S(2)}) copy-start(f32[64]{0:T(128)} %param.14) | copy-start | bytes 772
  140.2 2.5 %collective-permute-start.1 = (f32[1008,128]{1,0:T(8,128)}, f32[1008,128]{1,0:T(8,128)S(1)}, u32[]{:S(2)}, u32[]{:S(2)}) collective-permute-start(f32[1008,128]{1,0:T(8,128)} %slice.15), channel_id=1, source_target_pairs={{0,16},{16,0},{32,48},{48,32},{64,80},{80,64},{96,112},{112,96},{1... | collective-permute-start | bytes 1548296 | tf_op jit(solution)/shard_map/ppermute | solution.py:52
  143.2 14.1 %copy-start.1 = (bf16[64,64]{1,0:T(8,128)(2,1)S(1)}, bf16[64,64]{1,0:T(8,128)(2,1)}, u32[]{:S(2)}) copy-start(bf16[64,64]{1,0:T(8,128)(2,1)} %param.13) | copy-start | bytes 24580
Sparse Core Ops, SparseCore 0:
  9.1 113.0 all-gather.2

commit v2 on v1

--- a/solution.py
+++ b/solution.py
@@ -15,6 +15,9 @@
     return (upper, lower, spread)
 
 
+FLIPS = (1, 4, 5)
+
+
 def on_device(amps, ladder_w, fock, eps_occ, eps_pair):
     rows_i, rows_j, total = amps.shape
     n_oi = lax.axis_size("oi")
@@ -25,8 +28,8 @@
     me_i = lax.axis_index("oi")
     me_j = lax.axis_index("oj")
     me = me_i * n_oj + me_j
-    core = me_i % 2
-    partner = [(a, a ^ 1) for a in range(n_oi)]
+    q = ((me_i >> 2) & 1) * 2 + (me_i & 1)
+    perms = [[(a, a ^ f) for a in range(n_oi)] for f in FLIPS]
 
     send = amps.reshape(rows_i, rows_j, ndev, width).transpose(2, 0, 1, 3)
     recv = lax.all_to_all(send, ("oi", "oj"), 0, 0, tiled=True)
@@ -38,21 +41,24 @@
 
     upper, lower, spread = pair_tables(occ)
     npairs = upper.shape[0]
-    half = npairs // 2
+    part = npairs // 4
     flat = pair_amps.reshape(occ * occ, width)
     anti = (flat[upper].astype(jnp.float32) - flat[lower].astype(jnp.float32)).astype(jnp.bfloat16)
 
-    anti_other = lax.ppermute(anti, "oi", partner)
-    w_part = lax.dynamic_slice_in_dim(ladder_w, core * half, half, 1)
-    w_half = lax.all_gather(w_part, "oj", axis=0, tiled=True)
-    both = jnp.concatenate([anti, anti_other], axis=1)
-    contract = (((0,), (0,)), ((), ()))
-    lad = lax.dot_general(w_half, both, contract, preferred_element_type=jnp.float32)
-    lad_mine = lad[:, :width]
-    lad_other = lax.ppermute(lad[:, width:], "oi", partner)
-    first = jnp.where(core == 0, lad_mine, lad_other)
-    second = jnp.where(core == 0, lad_other, lad_mine)
-    ladder = jnp.concatenate([first, second, jnp.zeros((1, width), jnp.float32)], axis=0)
+    anti_all = [anti] + [lax.ppermute(anti, "oi", p) for p in perms]
+    w_part = lax.dynamic_slice_in_dim(ladder_w, q * part, part, 1)
+    w_blocks = lax.all_gather(w_part, "oj", axis=0, tiled=False)
+    both = jnp.concatenate(anti_all, axis=1).reshape(n_oj, npairs // n_oj, 4 * width)
+    contract = (((0, 1), (0, 1)), ((), ()))
+    lad = lax.dot_general(w_blocks, both, contract, preferred_element_type=jnp.float32)
+    pieces = [lad[:, :width]] + [
+        lax.ppermute(lad[:, (n + 1) * width : (n + 2) * width], "oi", p)
+        for n, p in enumerate(perms)
+    ]
+    stack = jnp.stack(pieces)
+    order = jnp.bitwise_xor(q, jnp.arange(4, dtype=q.dtype))
+    ladder = jnp.take(stack, order, axis=0).reshape(npairs, width)
+    ladder = jnp.concatenate([ladder, jnp.zeros((1, width), jnp.float32)], axis=0)
 
     upper_part = ladder[spread].reshape(occ, occ, width)
     mixed = jnp.einsum("ikp,kj->ijp", pair_amps, fock, preferred_element_type=jnp.float32)

time: 214 us -> 197 us (0.921)
  local copies, waits for them, and re-layouts: 51.7 us -> 42.1 us
  blocking collectives: 43.5 us -> 36.9 us
  waiting for transfers between devices: 79.6 us -> 73.8 us
  starting transfers between devices: 17.5 us -> 20.1 us
  other arithmetic: 2.01 us -> 4.53 us
    all_gather x1, waiting for transfers between devices: 40.7 us -> 0.01 us  [on_device(): w_blocks = lax.all_gather(w_part, 'oj', axis=0, tiled=False)]
    ppermute x2 -> x6, waiting for transfers between devices: 0.82 us -> 32.9 us  [the longest x3 22.4 us: on_device(): anti_all = [anti] + [lax.ppermute(anti, 'oi', p) for p in perms]]
    unnamed x14 -> x13, local copies, waits for them, and re-layouts: 10.2 us -> 1.72 us
    all_to_all x1, blocking collectives: 43.5 us -> 36.9 us  [on_device(): out_recv = lax.all_to_all(out_send, ('oi', 'oj'), 0, 0, tiled=True)]
    all_gather x1 -> x0, local copies, waits for them, and re-layouts: 5.19 us -> none  [on_device(): w_half = lax.all_gather(w_part, 'oj', axis=0, tiled=True)]
    all_to_all x1, waiting for transfers between devices: 38.1 us -> 40.9 us  [on_device(): recv = lax.all_to_all(send, ('oi', 'oj'), 0, 0, tiled=True)]
    reshape x0 -> x1, local copies, waits for them, and re-layouts: none -> 2.83 us  [on_device(): jnp.concatenate(anti_all, axis=1).reshape(n_oj, npairs // n_oj, 4 * width)]
    ppermute x2 -> x6, starting transfers between devices: 1.83 us -> 4.45 us  [the longest x3 2.23 us: on_device(): anti_all = [anti] + [lax.ppermute(anti, 'oi', p) for p in perms]]
  transfers between devices with their start and end apart: 4 -> 8, of which waited for: 3 -> 5; matrix products, arithmetic and copies ran while one was open for 15% -> 12% of each run, Pallas kernels for 0% -> 0%
where the time goes in v2:
time: 197 us
  waiting for transfers between devices  73.8 us (37%)
  local copies, waits for them, and re-layouts  42.1 us (21%)
  blocking collectives  36.9 us (19%)
  starting transfers between devices  20.1 us (10%)
  between operations  13.6 us (7%)
  matrix products  5.51 us (3%)
  other arithmetic  4.53 us (2%)
    all_to_all x1, waiting for transfers between devices, on_device(): recv = lax.all_to_all(send, ('oi', 'oj'), 0, 0, tiled=True)  40.9 us
    all_to_all x1, blocking collectives, on_device(): out_recv = lax.all_to_all(out_send, ('oi', 'oj'), 0, 0, tiled=True)  36.9 us
    ppermute x3, waiting for transfers between devices, on_device(): anti_all = [anti] + [lax.ppermute(anti, 'oi', p) for p in perms]  22.4 us
    all_to_all x1, starting transfers between devices, on_device(): recv = lax.all_to_all(send, ('oi', 'oj'), 0, 0, tiled=True)  15.6 us
    gather x1, local copies, waits for them, and re-layouts, on_device(): upper_part = ladder[spread].reshape(occ, occ, width)  14.1 us
    ppermute x3, waiting for transfers between devices, on_device(): lax.ppermute(lad[:, (n + 1) * width:(n + 2) * width], 'oi', p)  10.4 us
    gather x1, local copies, waits for them, and re-layouts, on_device(): flat[upper].astype(jnp.float32) - flat[lower].astype(jnp.float32)  6.34 us
    gather x1, local copies, waits for them, and re-layouts, on_device(): flat[lower].astype(jnp.float32)  6.34 us
  transfers between devices with their start and end apart: 8, of which 5 were waited for; matrix products, arithmetic and copies ran while one was open for 12% of the time, Pallas kernels for 0%

profile of v2, /device:TPU:1, one launch (start us, length us, event | category | flops | bytes accessed | tf_op | source)
XLA Modules:
  0.0 196.5 jit_solution(3884457506577957532)
XLA Ops:
  6.5 0.0 copy-start
  6.5 0.0 all-gather.4.cloned.1.call-start
  6.5 1.0 copy-done
  7.6 0.6 dynamic-slice_bitcast_fusion
  8.2 0.0 all-gather.4.cloned.1.call-update
  8.2 2.1 %reshape.77 = bf16[4,4,256,128]{3,2,1,0:T(8,128)(2,1)S(1)} reshape(bf16[4,4,32768]{2,1,0:T(4,128)(2,1)} %param.11) | data formatting | bytes 2097152 | tf_op jit(solution)/shard_map/reshape | solution.py:34
  10.4 0.0 copy-start.4
  10.4 0.0 copy-start.3
  10.4 1.8 copy.26
  12.2 15.6 %all-to-all-start = ((bf16[256,4,4,128]{3,2,1,0:T(4,128)(2,1)}), bf16[256,4,4,128]{3,2,1,0:T(4,128)(2,1)S(1)}, u32[]{:S(2)}, u32[]{:S(2)}) async-start(bf16[256,4,4,128]{3,2,1,0:T(4,128)(2,1)} %copy.26), calls=%async_computation | async-start | bytes 2097152 | tf_op jit(solution)/shard_map/all_to_all | solution.py:35
  27.9 0.0 copy-done.4
  27.9 0.0 copy-done.3
  27.9 40.9 %all-to-all-done = bf16[256,4,4,128]{3,2,1,0:T(4,128)(2,1)S(1)} async-done(((bf16[256,4,4,128]{3,2,1,0:T(4,128)(2,1)}), bf16[256,4,4,128]{3,2,1,0:T(4,128)(2,1)S(1)}, u32[]{:S(2)}, u32[]{:S(2)}) %all-to-all-start) | async-done | bytes 1048608 | tf_op jit(solution)/shard_map/all_to_all | solution.py:35
  68.8 0.3 copy.27
  69.1 1.4 copy.28
  70.4 6.3 %gather_fusion = bf16[2016,128]{1,0:T(8,128)(2,1)S(1)} fusion(bf16[4096,128]{1,0:T(8,128)(2,1)S(1)} %bitcast.46, s32[2048]{0:T(1024)S(1)} %pad_clamp_fusion.1), kind=kCustom, calls=%fused_computation | custom fusion | bytes 1040256 | tf_op jit(solution)/shard_map/gather | solution.py:46
  76.8 0.0 copy-start.2
  76.8 6.3 %gather_fusion.1 = bf16[2016,128]{1,0:T(8,128)(2,1)S(1)} fusion(bf16[4096,128]{1,0:T(8,128)(2,1)S(1)} %bitcast.47, s32[2048]{0:T(1024)S(1)} %pad_clamp_fusion), kind=kCustom, calls=%fused_computation.1 | custom fusion | bytes 1040256 | tf_op jit(solution)/shard_map/gather | solution.py:46
  83.2 0.1 subtract_convert_fusion
  83.3 0.1 collective-permute-start
  83.4 0.3 collective-permute-start.1
  83.7 1.8 collective-permute-start.2
  85.5 0.0 copy-done.2
  85.6 0.0 collective-permute-done
  85.6 10.8 %collective-permute-done.1 = bf16[2016,128]{1,0:T(8,128)(2,1)S(1)} collective-permute-done((bf16[2016,128]{1,0:T(8,128)(2,1)S(1)}, bf16[2016,128]{1,0:T(8,128)(2,1)S(1)}, u32[]{:S(2)}, u32[]{:S(2)}) %collective-permute-start.1) | collective-permute-done | bytes 516128 | tf_op jit(solution)/shard_map/ppermute | solution.py:48
  96.4 11.6 %collective-permute-done.2 = bf16[2016,128]{1,0:T(8,128)(2,1)S(1)} collective-permute-done((bf16[2016,128]{1,0:T(8,128)(2,1)S(1)}, bf16[2016,128]{1,0:T(8,128)(2,1)S(1)}, u32[]{:S(2)}, u32[]{:S(2)}) %collective-permute-start.2) | collective-permute-done | bytes 516128 | tf_op jit(solution)/shard_map/ppermute | solution.py:48
  108.0 1.6 pad_maximum_fusion
  109.6 2.8 %reshape.79 = bf16[16,126,512]{2,1,0:T(8,128)(2,1)} reshape(bf16[2016,512]{1,0:T(8,128)(2,1)} %pad_maximum_fusion) | data formatting | bytes 4128768 | tf_op jit(solution)/shard_map/reshape | solution.py:51
  112.4 0.0 copy-start.5
  112.4 0.0 all-gather.4.cloned.1.call-done
  112.4 3.5 %convolution_bitcast_fusion = f32[504,512]{1,0:T(8,128)S(1)} fusion(bf16[16,126,504]{1,2,0:T(8,128)(2,1)} %all-gather.4.cloned.1.call-done, bf16[16,126,512]{2,1,0:T(8,128)(2,1)} %reshape.79), kind=kOutput, calls=%fused_computation.10 | convolution fusion | flops 1040449536 | bytes 5128704 | tf_op jit(solution)/shard_map/dot_general | solution.py:53
  115.9 0.1 slice_bitcast_fusion
  116.0 0.1 collective-permute-start.3
  116.1 0.3 collective-permute-start.4
  116.4 1.8 collective-permute-start.5
  118.2 0.1 broadcast_in_dim.27
  118.3 0.1 broadcast_in_dim.28
  118.4 0.8 dynamic_slice.7
  119.1 0.0 copy-done.5
  119.1 0.1 broadcast_subtract_fusion
  119.2 0.0 collective-permute-done.3
  119.2 4.3 %collective-permute-done.4 = f32[504,128]{1,0:T(8,128)S(1)} collective-permute-done((f32[504,128]{1,0:T(8,128)S(1)}, f32[504,128]{1,0:T(8,128)S(1)}, u32[]{:S(2)}, u32[]{:S(2)}) %collective-permute-start.4) | collective-permute-done | bytes 258080 | tf_op jit(solution)/shard_map/ppermute | solution.py:55
  123.5 6.1 %collective-permute-done.5 = f32[504,128]{1,0:T(8,128)S(1)} collective-permute-done((f32[504,128]{1,0:T(8,128)S(1)}, f32[504,128]{1,0:T(8,128)S(1)}, u32[]{:S(2)}, u32[]{:S(2)}) %collective-permute-start.5) | collective-permute-done | bytes 258080 | tf_op jit(solution)/shard_map/ppermute | solution.py:55
  129.6 1.0 pad_maximum_fusion.1
  130.6 1.8 gather_fusion.2
  132.5 0.3 bitcast_select_fusion
  132.8 0.1 concatenate.7
  132.9 0.0 copy-start.1
  132.9 14.1 %gather_fusion.3 = f32[4096,128]{1,0:T(8,128)} fusion(f32[2017,128]{1,0:T(8,128)S(1)} %concatenate.7, s32[4096]{0:T(1024)S(1)} %broadcast_clamp_fusion), kind=kCustom, calls=%fused_computation.3 | custom fusion | bytes 4210688 | tf_op jit(solution)/shard_map/gather | solution.py:63
  147.0 0.0 copy-done.1
  147.0 2.1 %bitcast_subtract_fusion.1 = f32[64,64,128]{2,1,0:T(8,128)S(1)} fusion(f32[64,64,128]{2,1,0:T(8,128)} %bitcast.49, bf16[64,64,128]{2,1,0:T(8,128)(2,1)S(1)} %bitcast.48, bf16[64,64]{1,0:T(8,128)(2,1)S(1)} %copy-done.1), kind=kOutput, calls=%fused_computation.8 | convolution fusion | flops 67633152 | bytes 5251072 | tf_op jit(solution)/shard_map/ikp,kj->ijp/dot_general | solution.py:64
  149.1 1.4 fusion.2
  150.5 0.2 copy.32
  150.7 0.8 copy.33
  151.5 36.9 %all_to_all.10 = bf16[256,4,4,128]{3,2,1,0:T(4,128)(2,1)S(1)} all-to-all(bf16[256,4,4,128]{3,2,1,0:T(4,128)(2,1)S(1)} %copy.33), channel_id=1, replica_groups=mesh['oi'=16,'oj'=16] {'oi','oj'}, dimensions={0} | all-to-all | bytes 2097152 | tf_op jit(solution)/shard_map/all_to_all | solution.py:77
  188.4 1.3 copy_bitcast_fusion
  (6 shorter events, 0.0 us)
Async XLA Ops:
  6.5 1.0 copy-start
  6.5 105.9 %all-gather.4.cloned.1.call-start = ((), (), s32[]{:S(2)}) async-start(), calls=%async_computation.2 | async-start | bytes 2193408 | tf_op jit(solution)/shard_map/all_gather | solution.py:50
  10.4 17.5 %copy-start.4 = (s32[2016]{0:T(1024)S(1)}, s32[2016]{0:T(1024)}, u32[]{:S(2)}) copy-start(s32[2016]{0:T(1024)} %constant.65) | copy-start | bytes 24196
  10.4 17.5 %copy-start.3 = (s32[2016]{0:T(1024)S(1)}, s32[2016]{0:T(1024)}, u32[]{:S(2)}) copy-start(s32[2016]{0:T(1024)} %constant.66) | copy-start | bytes 24196
  12.2 56.6 %all-to-all-start = ((bf16[256,4,4,128]{3,2,1,0:T(4,128)(2,1)}), bf16[256,4,4,128]{3,2,1,0:T(4,128)(2,1)S(1)}, u32[]{:S(2)}, u32[]{:S(2)}) async-start(bf16[256,4,4,128]{3,2,1,0:T(4,128)(2,1)} %copy.26), calls=%async_computation | async-start | bytes 2097152 | tf_op jit(solution)/shard_map/all_to_all | solution.py:35
  76.8 8.8 %copy-start.2 = (s32[4096]{0:T(1024)S(1)}, s32[4096]{0:T(1024)}, u32[]{:S(2)}) copy-start(s32[4096]{0:T(1024)} %constant.67) | copy-start | bytes 49156
  83.3 2.3 %collective-permute-start = (bf16[2016,128]{1,0:T(8,128)(2,1)S(1)}, bf16[2016,128]{1,0:T(8,128)(2,1)S(1)}, u32[]{:S(2)}, u32[]{:S(2)}) collective-permute-start(bf16[2016,128]{1,0:T(8,128)(2,1)S(1)} %subtract_convert_fusion), channel_id=1, source_target_pairs={{0,16},{16,0},{32,48},{48,32},{64,80},{80,64},{96,112},{112,96},{1... | collective-permute-start | bytes 1548296 | tf_op jit(solution)/shard_map/ppermute | solution.py:48
  83.4 13.0 %collective-permute-start.1 = (bf16[2016,128]{1,0:T(8,128)(2,1)S(1)}, bf16[2016,128]{1,0:T(8,128)(2,1)S(1)}, u32[]{:S(2)}, u32[]{:S(2)}) collective-permute-start(bf16[2016,128]{1,0:T(8,128)(2,1)S(1)} %subtract_convert_fusion), channel_id=1, source_target_pairs={{0,64},{16,80},{32,96},{48,112},{64,0},{80,16},{96,32},{112,48},{1... | collective-permute-start | bytes 1548296 | tf_op jit(solution)/shard_map/ppermute | solution.py:48
  83.7 24.3 %collective-permute-start.2 = (bf16[2016,128]{1,0:T(8,128)(2,1)S(1)}, bf16[2016,128]{1,0:T(8,128)(2,1)S(1)}, u32[]{:S(2)}, u32[]{:S(2)}) collective-permute-start(bf16[2016,128]{1,0:T(8,128)(2,1)S(1)} %subtract_convert_fusion), channel_id=1, source_target_pairs={{0,80},{16,64},{32,112},{48,96},{64,16},{80,0},{96,48},{112,32},{1... | collective-permute-start | bytes 1548296 | tf_op jit(solution)/shard_map/ppermute | solution.py:48
  112.4 6.7 %copy-start.5 = (f32[64]{0:T(128)S(1)}, f32[64]{0:T(128)}, u32[]{:S(2)}) copy-start(f32[64]{0:T(128)} %param.14) | copy-start | bytes 772
  116.0 3.2 %collective-permute-start.3 = (f32[504,128]{1,0:T(8,128)S(1)}, f32[504,128]{1,0:T(8,128)S(1)}, u32[]{:S(2)}, u32[]{:S(2)}) collective-permute-start(f32[504,128]{1,0:T(8,128)S(1)} %get-tuple-element.8), channel_id=1, source_target_pairs={{0,16},{16,0},{32,48},{48,32},{64,80},{80,64},{96,112},{112,96},{1... | collective-permute-start | bytes 774152 | tf_op jit(solution)/shard_map/ppermute | solution.py:55
  116.1 7.5 %collective-permute-start.4 = (f32[504,128]{1,0:T(8,128)S(1)}, f32[504,128]{1,0:T(8,128)S(1)}, u32[]{:S(2)}, u32[]{:S(2)}) collective-permute-start(f32[504,128]{1,0:T(8,128)S(1)} %get-tuple-element.7), channel_id=1, source_target_pairs={{0,64},{16,80},{32,96},{48,112},{64,0},{80,16},{96,32},{112,48},{1... | collective-permute-start | bytes 774152 | tf_op jit(solution)/shard_map/ppermute | solution.py:55
  116.4 13.2 %collective-permute-start.5 = (f32[504,128]{1,0:T(8,128)S(1)}, f32[504,128]{1,0:T(8,128)S(1)}, u32[]{:S(2)}, u32[]{:S(2)}) collective-permute-start(f32[504,128]{1,0:T(8,128)S(1)} %get-tuple-element.6), channel_id=1, source_target_pairs={{0,80},{16,64},{32,112},{48,96},{64,16},{80,0},{96,48},{112,32},{1... | collective-permute-start | bytes 774152 | tf_op jit(solution)/shard_map/ppermute | solution.py:55
  132.9 14.1 %copy-start.1 = (bf16[64,64]{1,0:T(8,128)(2,1)S(1)}, bf16[64,64]{1,0:T(8,128)(2,1)}, u32[]{:S(2)}) copy-start(bf16[64,64]{1,0:T(8,128)(2,1)} %param.13) | copy-start | bytes 24580
Sparse Core Ops, SparseCore 0:
  9.1 76.8 all-gather.3

commit v3 on v2

--- a/solution.py
+++ b/solution.py
@@ -45,7 +45,10 @@
     flat = pair_amps.reshape(occ * occ, width)
     anti = (flat[upper].astype(jnp.float32) - flat[lower].astype(jnp.float32)).astype(jnp.bfloat16)
 
-    anti_all = [anti] + [lax.ppermute(anti, "oi", p) for p in perms]
+    from_core = lax.ppermute(anti, "oi", perms[0])
+    from_y = lax.ppermute(anti, "oi", perms[1])
+    from_diag = lax.ppermute(from_y, "oi", perms[0])
+    anti_all = [anti, from_core, from_y, from_diag]
     w_part = lax.dynamic_slice_in_dim(ladder_w, q * part, part, 1)
     w_blocks = lax.all_gather(w_part, "oj", axis=0, tiled=False)
     both = jnp.concatenate(anti_all, axis=1).reshape(n_oj, npairs // n_oj, 4 * width)

time: 197 us -> 194 us (0.985)
  waiting for transfers between devices: 73.8 us -> 57.9 us
  starting transfers between devices: 20.1 us -> 29.3 us
  blocking collectives: 36.9 us -> 41.8 us
    ppermute x3, starting transfers between devices: 2.22 us -> 11.4 us  [on_device(): lax.ppermute(lad[:, (n + 1) * width:(n + 2) * width], 'oi', p)]
    ppermute x3, waiting for transfers between devices: 22.4 us -> 13.5 us  [the longest x1 12 us: on_device(): from_y = lax.ppermute(anti, 'oi', perms[1])]
    all_to_all x1, waiting for transfers between devices: 40.9 us -> 33.5 us  [on_device(): recv = lax.all_to_all(send, ('oi', 'oj'), 0, 0, tiled=True)]
    all_to_all x1, blocking collectives: 36.9 us -> 41.8 us  [on_device(): out_recv = lax.all_to_all(out_send, ('oi', 'oj'), 0, 0, tiled=True)]
  transfers between devices with their start and end apart: 8 -> 8, of which waited for: 5 -> 6; matrix products, arithmetic and copies ran while one was open for 12% -> 11% of each run, Pallas kernels for 0% -> 0%
where the time goes in v3:
time: 194 us
  waiting for transfers between devices  57.9 us (30%)
  blocking collectives  41.8 us (22%)
  local copies, waits for them, and re-layouts  41.2 us (21%)
  starting transfers between devices  29.3 us (15%)
  between operations  13.6 us (7%)
  matrix products  5.51 us (3%)
  other arithmetic  4.54 us (2%)
    all_to_all x1, blocking collectives, on_device(): out_recv = lax.all_to_all(out_send, ('oi', 'oj'), 0, 0, tiled=True)  41.8 us
    all_to_all x1, waiting for transfers between devices, on_device(): recv = lax.all_to_all(send, ('oi', 'oj'), 0, 0, tiled=True)  33.5 us
    all_to_all x1, starting transfers between devices, on_device(): recv = lax.all_to_all(send, ('oi', 'oj'), 0, 0, tiled=True)  15.6 us
    gather x1, local copies, waits for them, and re-layouts, on_device(): upper_part = ladder[spread].reshape(occ, occ, width)  14.1 us
    ppermute x1, waiting for transfers between devices, on_device(): from_y = lax.ppermute(anti, 'oi', perms[1])  12 us
    ppermute x3, starting transfers between devices, on_device(): lax.ppermute(lad[:, (n + 1) * width:(n + 2) * width], 'oi', p)  11.4 us
    ppermute x3, waiting for transfers between devices, on_device(): lax.ppermute(lad[:, (n + 1) * width:(n + 2) * width], 'oi', p)  10.7 us
    gather x1, local copies, waits for them, and re-layouts, on_device(): flat[upper].astype(jnp.float32) - flat[lower].astype(jnp.float32)  6.34 us
  transfers between devices with their start and end apart: 8, of which 6 were waited for; matrix products, arithmetic and copies ran while one was open for 11% of the time, Pallas kernels for 0%

profile of v3, /device:TPU:1, one launch (start us, length us, event | category | flops | bytes accessed | tf_op | source)
XLA Modules:
  0.0 193.8 jit_solution(18165145650088242372)
XLA Ops:
  6.5 0.0 copy-start
  6.5 2.2 %reshape.77 = bf16[4,4,256,128]{3,2,1,0:T(8,128)(2,1)S(1)} reshape(bf16[4,4,32768]{2,1,0:T(4,128)(2,1)} %param.11) | data formatting | bytes 2097152 | tf_op jit(solution)/shard_map/reshape | solution.py:34
  8.7 0.0 copy-start.4
  8.8 0.0 copy-start.3
  8.8 1.8 copy.26
  10.6 15.6 %all-to-all-start = ((bf16[256,4,4,128]{3,2,1,0:T(4,128)(2,1)}), bf16[256,4,4,128]{3,2,1,0:T(4,128)(2,1)S(1)}, u32[]{:S(2)}, u32[]{:S(2)}) async-start(bf16[256,4,4,128]{3,2,1,0:T(4,128)(2,1)} %copy.26), calls=%async_computation | async-start | bytes 2097152 | tf_op jit(solution)/shard_map/all_to_all | solution.py:35
  26.2 0.0 all-gather.4.cloned.1.call-start
  26.3 0.0 copy-done
  26.3 0.7 dynamic-slice_bitcast_fusion
  26.9 0.0 all-gather.4.cloned.1.call-update
  27.0 0.0 copy-done.4
  27.0 0.0 copy-done.3
  27.0 33.5 %all-to-all-done = bf16[256,4,4,128]{3,2,1,0:T(4,128)(2,1)S(1)} async-done(((bf16[256,4,4,128]{3,2,1,0:T(4,128)(2,1)}), bf16[256,4,4,128]{3,2,1,0:T(4,128)(2,1)S(1)}, u32[]{:S(2)}, u32[]{:S(2)}) %all-to-all-start) | async-done | bytes 1048608 | tf_op jit(solution)/shard_map/all_to_all | solution.py:35
  60.5 0.3 copy.27
  60.8 1.4 copy.28
  62.2 6.3 %gather_fusion = bf16[2016,128]{1,0:T(8,128)(2,1)S(1)} fusion(bf16[4096,128]{1,0:T(8,128)(2,1)S(1)} %bitcast.46, s32[2048]{0:T(1024)S(1)} %pad_clamp_fusion.1), kind=kCustom, calls=%fused_computation | custom fusion | bytes 1040256 | tf_op jit(solution)/shard_map/gather | solution.py:46
  68.5 0.0 copy-start.2
  68.5 6.3 %gather_fusion.1 = bf16[2016,128]{1,0:T(8,128)(2,1)S(1)} fusion(bf16[4096,128]{1,0:T(8,128)(2,1)S(1)} %bitcast.47, s32[2048]{0:T(1024)S(1)} %pad_clamp_fusion), kind=kCustom, calls=%fused_computation.1 | custom fusion | bytes 1040256 | tf_op jit(solution)/shard_map/gather | solution.py:46
  74.9 0.1 subtract_convert_fusion
  75.0 0.1 collective-permute-start.1
  75.1 1.0 collective-permute-start
  76.1 12.0 %collective-permute-done.1 = bf16[2016,128]{1,0:T(8,128)(2,1)S(1)} collective-permute-done((bf16[2016,128]{1,0:T(8,128)(2,1)S(1)}, bf16[2016,128]{1,0:T(8,128)(2,1)S(1)}, u32[]{:S(2)}, u32[]{:S(2)}) %collective-permute-start.1) | collective-permute-done | bytes 516128 | tf_op jit(solution)/shard_map/ppermute | solution.py:49
  88.1 1.2 collective-permute-start.2
  89.3 0.0 copy-done.2
  89.3 0.0 collective-permute-done
  89.3 1.5 collective-permute-done.2
  90.8 1.6 pad_maximum_fusion
  92.4 2.8 %reshape.79 = bf16[16,126,512]{2,1,0:T(8,128)(2,1)} reshape(bf16[2016,512]{1,0:T(8,128)(2,1)} %pad_maximum_fusion) | data formatting | bytes 4128768 | tf_op jit(solution)/shard_map/reshape | solution.py:54
  95.2 0.0 copy-start.5
  95.2 0.1 all-gather.4.cloned.1.call-done
  95.3 3.4 %convolution_bitcast_fusion = f32[504,512]{1,0:T(8,128)S(1)} fusion(bf16[16,126,504]{1,2,0:T(8,128)(2,1)} %all-gather.4.cloned.1.call-done, bf16[16,126,512]{2,1,0:T(8,128)(2,1)} %reshape.79), kind=kOutput, calls=%fused_computation.10 | convolution fusion | flops 1040449536 | bytes 5128704 | tf_op jit(solution)/shard_map/dot_general | solution.py:56
  98.7 0.1 slice_bitcast_fusion
  98.8 9.6 %collective-permute-start.3 = (f32[504,128]{1,0:T(8,128)S(1)}, f32[504,128]{1,0:T(8,128)S(1)}, u32[]{:S(2)}, u32[]{:S(2)}) collective-permute-start(f32[504,128]{1,0:T(8,128)S(1)} %get-tuple-element.8), channel_id=1, source_target_pairs={{0,16},{16,0},{32,48},{48,32},{64,80},{80,64},{96,112},{112,96},{1... | collective-permute-start | bytes 774152 | tf_op jit(solution)/shard_map/ppermute | solution.py:58
  108.4 1.2 collective-permute-start.4
  109.6 0.6 collective-permute-start.5
  110.2 0.1 broadcast_in_dim.27
  110.2 0.1 broadcast_in_dim.28
  110.3 0.8 dynamic_slice.7
  111.1 0.0 copy-done.5
  111.1 0.1 broadcast_subtract_fusion
  111.2 0.0 collective-permute-done.3
  111.2 4.9 %collective-permute-done.4 = f32[504,128]{1,0:T(8,128)S(1)} collective-permute-done((f32[504,128]{1,0:T(8,128)S(1)}, f32[504,128]{1,0:T(8,128)S(1)}, u32[]{:S(2)}, u32[]{:S(2)}) %collective-permute-start.4) | collective-permute-done | bytes 258080 | tf_op jit(solution)/shard_map/ppermute | solution.py:58
  116.1 5.8 %collective-permute-done.5 = f32[504,128]{1,0:T(8,128)S(1)} collective-permute-done((f32[504,128]{1,0:T(8,128)S(1)}, f32[504,128]{1,0:T(8,128)S(1)}, u32[]{:S(2)}, u32[]{:S(2)}) %collective-permute-start.5) | collective-permute-done | bytes 258080 | tf_op jit(solution)/shard_map/ppermute | solution.py:58
  121.9 1.0 pad_maximum_fusion.1
  122.9 1.8 gather_fusion.2
  124.8 0.3 bitcast_select_fusion
  125.1 0.1 concatenate.7
  125.2 0.0 copy-start.1
  125.2 14.1 %gather_fusion.3 = f32[4096,128]{1,0:T(8,128)} fusion(f32[2017,128]{1,0:T(8,128)S(1)} %concatenate.7, s32[4096]{0:T(1024)S(1)} %broadcast_clamp_fusion), kind=kCustom, calls=%fused_computation.3 | custom fusion | bytes 4210688 | tf_op jit(solution)/shard_map/gather | solution.py:66
  139.3 0.0 copy-done.1
  139.3 2.1 %bitcast_subtract_fusion.1 = f32[64,64,128]{2,1,0:T(8,128)S(1)} fusion(f32[64,64,128]{2,1,0:T(8,128)} %bitcast.49, bf16[64,64,128]{2,1,0:T(8,128)(2,1)S(1)} %bitcast.48, bf16[64,64]{1,0:T(8,128)(2,1)S(1)} %copy-done.1), kind=kOutput, calls=%fused_computation.8 | convolution fusion | flops 67633152 | bytes 5251072 | tf_op jit(solution)/shard_map/ikp,kj->ijp/dot_general | solution.py:67
  141.4 1.4 fusion.2
  142.8 0.2 copy.32
  143.0 0.8 copy.33
  143.8 41.8 %all_to_all.10 = bf16[256,4,4,128]{3,2,1,0:T(4,128)(2,1)S(1)} all-to-all(bf16[256,4,4,128]{3,2,1,0:T(4,128)(2,1)S(1)} %copy.33), channel_id=1, replica_groups=mesh['oi'=16,'oj'=16] {'oi','oj'}, dimensions={0} | all-to-all | bytes 2097152 | tf_op jit(solution)/shard_map/all_to_all | solution.py:80
  185.6 1.3 copy_bitcast_fusion
  (6 shorter events, 0.0 us)
Async XLA Ops:
  6.5 19.7 %copy-start = (bf16[126,2016]{0,1:T(8,128)(2,1)S(1)}, bf16[126,2016]{0,1:T(8,128)(2,1)}, u32[]{:S(2)}) copy-start(bf16[126,2016]{0,1:T(8,128)(2,1)} %param.12) | copy-start | bytes 1524100
  8.7 18.2 %copy-start.4 = (s32[2016]{0:T(1024)S(1)}, s32[2016]{0:T(1024)}, u32[]{:S(2)}) copy-start(s32[2016]{0:T(1024)} %constant.65) | copy-start | bytes 24196
  8.8 18.2 %copy-start.3 = (s32[2016]{0:T(1024)S(1)}, s32[2016]{0:T(1024)}, u32[]{:S(2)}) copy-start(s32[2016]{0:T(1024)} %constant.66) | copy-start | bytes 24196
  10.6 50.0 %all-to-all-start = ((bf16[256,4,4,128]{3,2,1,0:T(4,128)(2,1)}), bf16[256,4,4,128]{3,2,1,0:T(4,128)(2,1)S(1)}, u32[]{:S(2)}, u32[]{:S(2)}) async-start(bf16[256,4,4,128]{3,2,1,0:T(4,128)(2,1)} %copy.26), calls=%async_computation | async-start | bytes 2097152 | tf_op jit(solution)/shard_map/all_to_all | solution.py:35
  26.2 69.0 %all-gather.4.cloned.1.call-start = ((), (), s32[]{:S(2)}) async-start(), calls=%async_computation.2 | async-start | bytes 2193408 | tf_op jit(solution)/shard_map/all_gather | solution.py:53
  68.5 20.8 %copy-start.2 = (s32[4096]{0:T(1024)S(1)}, s32[4096]{0:T(1024)}, u32[]{:S(2)}) copy-start(s32[4096]{0:T(1024)} %constant.67) | copy-start | bytes 49156
  75.0 13.1 %collective-permute-start.1 = (bf16[2016,128]{1,0:T(8,128)(2,1)S(1)}, bf16[2016,128]{1,0:T(8,128)(2,1)S(1)}, u32[]{:S(2)}, u32[]{:S(2)}) collective-permute-start(bf16[2016,128]{1,0:T(8,128)(2,1)S(1)} %subtract_convert_fusion), channel_id=1, source_target_pairs={{0,64},{16,80},{32,96},{48,112},{64,0},{80,16},{96,32},{112,48},{1... | collective-permute-start | bytes 1548296 | tf_op jit(solution)/shard_map/ppermute | solution.py:49
  75.1 14.2 %collective-permute-start = (bf16[2016,128]{1,0:T(8,128)(2,1)S(1)}, bf16[2016,128]{1,0:T(8,128)(2,1)S(1)}, u32[]{:S(2)}, u32[]{:S(2)}) collective-permute-start(bf16[2016,128]{1,0:T(8,128)(2,1)S(1)} %subtract_convert_fusion), channel_id=1, source_target_pairs={{0,16},{16,0},{32,48},{48,32},{64,80},{80,64},{96,112},{112,96},{1... | collective-permute-start | bytes 1548296 | tf_op jit(solution)/shard_map/ppermute | solution.py:48
  88.1 2.7 %collective-permute-start.2 = (bf16[2016,128]{1,0:T(8,128)(2,1)S(1)}, bf16[2016,128]{1,0:T(8,128)(2,1)S(1)}, u32[]{:S(2)}, u32[]{:S(2)}) collective-permute-start(bf16[2016,128]{1,0:T(8,128)(2,1)S(1)} %collective-permute-done.1), channel_id=1, source_target_pairs={{0,16},{16,0},{32,48},{48,32},{64,80},{80,64},{96,112},{112,96},{1... | collective-permute-start | bytes 1548296 | tf_op jit(solution)/shard_map/ppermute | solution.py:50
  95.2 15.9 %copy-start.5 = (f32[64]{0:T(128)S(1)}, f32[64]{0:T(128)}, u32[]{:S(2)}) copy-start(f32[64]{0:T(128)} %param.14) | copy-start | bytes 772
  98.8 12.4 %collective-permute-start.3 = (f32[504,128]{1,0:T(8,128)S(1)}, f32[504,128]{1,0:T(8,128)S(1)}, u32[]{:S(2)}, u32[]{:S(2)}) collective-permute-start(f32[504,128]{1,0:T(8,128)S(1)} %get-tuple-element.8), channel_id=1, source_target_pairs={{0,16},{16,0},{32,48},{48,32},{64,80},{80,64},{96,112},{112,96},{1... | collective-permute-start | bytes 774152 | tf_op jit(solution)/shard_map/ppermute | solution.py:58
  108.4 7.7 %collective-permute-start.4 = (f32[504,128]{1,0:T(8,128)S(1)}, f32[504,128]{1,0:T(8,128)S(1)}, u32[]{:S(2)}, u32[]{:S(2)}) collective-permute-start(f32[504,128]{1,0:T(8,128)S(1)} %get-tuple-element.7), channel_id=1, source_target_pairs={{0,64},{16,80},{32,96},{48,112},{64,0},{80,16},{96,32},{112,48},{1... | collective-permute-start | bytes 774152 | tf_op jit(solution)/shard_map/ppermute | solution.py:58
  109.6 12.3 %collective-permute-start.5 = (f32[504,128]{1,0:T(8,128)S(1)}, f32[504,128]{1,0:T(8,128)S(1)}, u32[]{:S(2)}, u32[]{:S(2)}) collective-permute-start(f32[504,128]{1,0:T(8,128)S(1)} %get-tuple-element.6), channel_id=1, source_target_pairs={{0,80},{16,64},{32,112},{48,96},{64,16},{80,0},{96,48},{112,32},{1... | collective-permute-start | bytes 774152 | tf_op jit(solution)/shard_map/ppermute | solution.py:58
  125.2 14.1 %copy-start.1 = (bf16[64,64]{1,0:T(8,128)(2,1)S(1)}, bf16[64,64]{1,0:T(8,128)(2,1)}, u32[]{:S(2)}) copy-start(bf16[64,64]{1,0:T(8,128)(2,1)} %param.13) | copy-start | bytes 24580
Sparse Core Ops, SparseCore 0:
  28.8 66.3 all-gather.3

commit v4 on v3

--- a/solution.py
+++ b/solution.py
@@ -2,6 +2,8 @@
 import jax.numpy as jnp
 import numpy as np
 from jax import lax
+from jax.experimental import pallas as pl
+from jax.experimental.pallas import tpu as pltpu
 from jax.sharding import PartitionSpec as P
 
 
@@ -16,6 +18,51 @@
 
 
 FLIPS = (1, 4, 5)
+
+
+def row_starts(occ):
+    return [i * (occ - 1) - i * (i - 1) // 2 - i for i in range(occ)]
+
+
+def anti_kernel(d_ref, o_ref, tmp_ref):
+    occ = d_ref.shape[0]
+    off = 0
+    for k in range(occ - 1):
+        n = occ - 1 - k
+        tmp_ref[off : off + n, :] = d_ref[k, k + 1 : occ, :]
+        off += n
+    blocks, rows = o_ref.shape[0], o_ref.shape[1]
+    for b in range(blocks):
+        o_ref[b] = tmp_ref[b * rows : (b + 1) * rows, :].astype(o_ref.dtype)
+
+
+def spread_kernel(q_ref, p0, p1, p2, p3, o_ref, lad_ref):
+    pieces = (p0, p1, p2, p3)
+    part = p0.shape[0]
+    q = q_ref[0]
+    lad_ref[0:8, :] = jnp.zeros((8, lad_ref.shape[1]), lad_ref.dtype)
+    for r in range(4):
+        for n in range(4):
+
+            @pl.when(jnp.bitwise_xor(q, r) == n)
+            def _():
+                lad_ref[8 + r * part : 8 + (r + 1) * part, :] = pieces[n][...]
+
+    occ, width = o_ref.shape[0], o_ref.shape[2]
+    col = lax.broadcasted_iota(jnp.int32, (occ, width), 0)
+    for i, s in enumerate(row_starts(occ)):
+        o_ref[i] = jnp.where(col > i, lad_ref[7 + s : 7 + s + occ, :], 0.0)
+
+
+def vmem_call(kernel, out_shape, scratch, *args, smem=0):
+    spaces = [pltpu.SMEM] * smem + [pltpu.VMEM] * (len(args) - smem)
+    return pl.pallas_call(
+        kernel,
+        out_shape=out_shape,
+        in_specs=[pl.BlockSpec(memory_space=s) for s in spaces],
+        out_specs=pl.BlockSpec(memory_space=pltpu.VMEM),
+        scratch_shapes=scratch,
+    )(*args)
 
 
 def on_device(amps, ladder_w, fock, eps_occ, eps_pair):
@@ -42,28 +89,39 @@
     upper, lower, spread = pair_tables(occ)
     npairs = upper.shape[0]
     part = npairs // 4
-    flat = pair_amps.reshape(occ * occ, width)
-    anti = (flat[upper].astype(jnp.float32) - flat[lower].astype(jnp.float32)).astype(jnp.bfloat16)
+    swapped = jnp.transpose(pair_amps, (1, 0, 2))
+    diff = pair_amps.astype(jnp.float32) - swapped.astype(jnp.float32)
+    anti = vmem_call(
+        anti_kernel,
+        jax.ShapeDtypeStruct((n_oj, npairs // n_oj, width), jnp.bfloat16),
+        [pltpu.VMEM((npairs, width), jnp.float32)],
+        diff,
+    )
 
     from_core = lax.ppermute(anti, "oi", perms[0])
     from_y = lax.ppermute(anti, "oi", perms[1])
     from_diag = lax.ppermute(from_y, "oi", perms[0])
-    anti_all = [anti, from_core, from_y, from_diag]
     w_part = lax.dynamic_slice_in_dim(ladder_w, q * part, part, 1)
     w_blocks = lax.all_gather(w_part, "oj", axis=0, tiled=False)
-    both = jnp.concatenate(anti_all, axis=1).reshape(n_oj, npairs // n_oj, 4 * width)
     contract = (((0, 1), (0, 1)), ((), ()))
-    lad = lax.dot_general(w_blocks, both, contract, preferred_element_type=jnp.float32)
-    pieces = [lad[:, :width]] + [
-        lax.ppermute(lad[:, (n + 1) * width : (n + 2) * width], "oi", p)
-        for n, p in enumerate(perms)
+
+    def quarter(block):
+        return lax.dot_general(w_blocks, block, contract, preferred_element_type=jnp.float32)
+
+    own = quarter(anti)
+    back = [
+        lax.ppermute(quarter(block), "oi", p)
+        for block, p in zip((from_core, from_y, from_diag), perms)
     ]
-    stack = jnp.stack(pieces)
-    order = jnp.bitwise_xor(q, jnp.arange(4, dtype=q.dtype))
-    ladder = jnp.take(stack, order, axis=0).reshape(npairs, width)
-    ladder = jnp.concatenate([ladder, jnp.zeros((1, width), jnp.float32)], axis=0)
-
-    upper_part = ladder[spread].reshape(occ, occ, width)
+    upper_part = vmem_call(
+        spread_kernel,
+        jax.ShapeDtypeStruct((occ, occ, width), jnp.float32),
+        [pltpu.VMEM((8 + npairs, width), jnp.float32)],
+        q.astype(jnp.int32).reshape(1),
+        own,
+        *back,
+        smem=1,
+    )
     mixed = jnp.einsum("ikp,kj->ijp", pair_amps, fock, preferred_element_type=jnp.float32)
     x = upper_part - mixed
     resid = x - jnp.transpose(x, (1, 0, 2))

time: 194 us -> 167 us (0.86)
  blocking collectives: 41.8 us -> 97.2 us
  waiting for transfers between devices: 57.9 us -> 20.4 us
  local copies, waits for them, and re-layouts: 41.2 us -> 9.58 us
  starting transfers between devices: 29.3 us -> 7.14 us
  Pallas kernels: 0 us -> 5.45 us
  matrix products: 5.51 us -> 7.55 us
    all_to_all x0 -> x1, blocking collectives: none -> 55.4 us  [on_device(): recv = lax.all_to_all(send, ('oi', 'oj'), 0, 0, tiled=True)]
    all_to_all x1 -> x0, waiting for transfers between devices: 33.5 us -> none  [on_device(): recv = lax.all_to_all(send, ('oi', 'oj'), 0, 0, tiled=True)]
    gather x4 -> x0, local copies, waits for them, and re-layouts: 28.6 us -> none  [the longest x1 14.1 us: on_device(): upper_part = ladder[spread].reshape(occ, occ, width)]
    all_to_all x1 -> x0, starting transfers between devices: 15.6 us -> none  [on_device(): recv = lax.all_to_all(send, ('oi', 'oj'), 0, 0, tiled=True)]
    pallas_call x0 -> x2, Pallas kernels: none -> 5.45 us  [vmem_call(): pl.pallas_call(kernel, out_shape=out_shape, in_specs=[pl.BlockSpec(memory...]
    ppermute x3, starting transfers between devices: 11.4 us -> 5.98 us  [on_device(): lax.ppermute(quarter(block), 'oi', p)]
    sub x0 -> x2, other arithmetic: none -> 4.65 us  [the longest x1 2.58 us: on_device(): diff = pair_amps.astype(jnp.float32) - swapped.astype(jnp.float32)]
    ppermute x3, waiting for transfers between devices: 10.7 us -> 6.25 us  [on_device(): lax.ppermute(quarter(block), 'oi', p)]
  transfers between devices with their start and end apart: 8 -> 7, of which waited for: 6 -> 4; matrix products, arithmetic and copies ran while one was open for 11% -> 9% of each run, Pallas kernels for 0% -> 2%
where the time goes in v4:
time: 167 us
  blocking collectives  97.2 us (58%)
  waiting for transfers between devices  20.4 us (12%)
  between operations  13.5 us (8%)
  local copies, waits for them, and re-layouts  9.58 us (6%)
  matrix products  7.55 us (5%)
  starting transfers between devices  7.14 us (4%)
  other arithmetic  6.34 us (4%)
  Pallas kernels  5.45 us (3%)
    all_to_all x1, blocking collectives, on_device(): recv = lax.all_to_all(send, ('oi', 'oj'), 0, 0, tiled=True)  55.4 us
    all_to_all x1, blocking collectives, on_device(): out_recv = lax.all_to_all(out_send, ('oi', 'oj'), 0, 0, tiled=True)  41.8 us
    ppermute x1, waiting for transfers between devices, on_device(): from_y = lax.ppermute(anti, 'oi', perms[1])  13.4 us
    ppermute x3, waiting for transfers between devices, on_device(): lax.ppermute(quarter(block), 'oi', p)  6.25 us
    ppermute x3, starting transfers between devices, on_device(): lax.ppermute(quarter(block), 'oi', p)  5.98 us
    pallas_call x2, Pallas kernels, vmem_call(): pl.pallas_call(kernel, out_shape=out_shape, in_specs=[pl.BlockSpec(memory...  5.45 us
    dot_general x4, matrix products, quarter(): lax.dot_general(w_blocks, block, contract, preferred_element_type=jnp.flo...  5.32 us
  transfers between devices with their start and end apart: 7, of which 4 were waited for; matrix products, arithmetic and copies ran while one was open for 9% of the time, Pallas kernels for 2%

profile of v4, /device:TPU:1, one launch (start us, length us, event | category | flops | bytes accessed | tf_op | source)
XLA Modules:
  0.0 167.1 jit_solution(13403851315658418150)
XLA Ops:
  6.5 0.0 copy-start
  6.5 0.0 all-gather.4.cloned.1.call-start
  6.5 1.0 copy-done
  7.6 0.7 dynamic-slice_bitcast_fusion
  8.2 0.0 all-gather.4.cloned.1.call-update
  8.3 2.1 %reshape.51 = bf16[4,4,256,128]{3,2,1,0:T(8,128)(2,1)S(1)} reshape(bf16[4,4,32768]{2,1,0:T(4,128)(2,1)} %param.5) | data formatting | bytes 2097152 | tf_op jit(solution)/shard_map/reshape | solution.py:81
  10.4 0.8 copy.24
  11.2 55.4 %all_to_all.10 = bf16[256,4,4,128]{3,2,1,0:T(4,128)(2,1)S(1)} all-to-all(bf16[256,4,4,128]{3,2,1,0:T(4,128)(2,1)S(1)} %copy.24), channel_id=1, replica_groups=mesh['oi'=16,'oj'=16] {'oi','oj'}, dimensions={0} | all-to-all | bytes 2097152 | tf_op jit(solution)/shard_map/all_to_all | solution.py:82
  66.6 0.3 copy.25
  66.9 0.8 copy.26
  67.7 0.2 convert_element_type.12
  67.9 2.6 %bitcast_subtract_fusion.2.d_ref = f32[64,64,128]{2,1,0:T(8,128)} fusion(f32[64,64,128]{2,0,1:T(8,128)S(1)} %convert_element_type.12), kind=kLoop, calls=%fused_computation.5 | loop fusion | flops 524288 | bytes 4194304 | tf_op jit(solution)/shard_map/sub | solution.py:93
  70.5 0.0 copy-start.7
  70.5 2.5 %shard_map.55 = bf16[16,126,128]{2,1,0:T(8,128)(2,1)} custom-call(f32[64,64,128]{2,1,0:T(8,128)} %bitcast_subtract_fusion.2.d_ref), custom_call_target="tpu_custom_call" | custom-call | tf_op jit(solution)/shard_map/pallas_call | solution.py:59
  73.1 0.0 collective-permute-start.2
  73.1 13.4 %collective-permute-done.2 = bf16[16,126,128]{2,1,0:T(8,128)(2,1)S(1)} collective-permute-done((bf16[16,126,128]{2,1,0:T(8,128)(2,1)}, bf16[16,126,128]{2,1,0:T(8,128)(2,1)S(1)}, u32[]{:S(2)}, u32[]{:S(2)}) %collective-permute-start.2) | collective-permute-done | bytes 516128 | tf_op jit(solution)/shard_map/ppermute | solution.py:102
  86.5 1.2 collective-permute-start.4
  87.6 0.8 dynamic_slice.7
  88.4 0.0 collective-permute-start
  88.4 0.0 copy-done.7
  88.4 0.1 broadcast_subtract_fusion
  88.4 0.7 collective-permute-done.4
  89.1 0.0 all-gather.4.cloned.1.call-done
  89.1 0.0 copy-start.1
  89.1 2.4 %convolution_bitcast_fusion = f32[504,128]{1,0:T(8,128)S(1)} fusion(bf16[16,126,504]{1,2,0:T(8,128)(2,1)} %all-gather.4.cloned.1.call-done, bf16[16,126,128]{2,1,0:T(8,128)(2,1)S(1)} %collective-permute-done.4), kind=kOutput, calls=%fused_computation.6 | convolution fusion | flops 260112384 | bytes 2806272 | tf_op jit(solution)/shard_map/dot_general | solution.py:109
  91.6 5.0 %collective-permute-start.5 = (f32[504,128]{1,0:T(8,128)S(1)}, f32[504,128]{1,0:T(8,128)S(1)}, u32[]{:S(2)}, u32[]{:S(2)}) collective-permute-start(f32[504,128]{1,0:T(8,128)S(1)} %convolution_bitcast_fusion), channel_id=1, source_target_pairs={{0,80},{16,64},{32,112},{48,96},{64,16},{80,0},{96,48},{112,32},{1... | collective-permute-start | bytes 774152 | tf_op jit(solution)/shard_map/ppermute | solution.py:113
  96.6 0.0 copy-done.1
  96.6 0.7 convolution_bitcast_fusion.1
  97.3 0.0 copy-start.6
  97.3 0.7 collective-permute-start.3
  98.0 0.0 collective-permute-done
  98.0 0.7 convolution_bitcast_fusion.2
  98.8 0.0 copy-start.3
  98.8 0.3 collective-permute-start.1
  99.1 0.0 copy-done.6
  99.1 2.2 %fusion.3 = f32[64,64,128]{2,0,1:T(8,128)} fusion(bf16[64,64,128]{2,0,1:T(8,128)(2,1)S(1)} %bitcast.50, bf16[64,64]{1,0:T(8,128)(2,1)S(1)} %copy-done.6), kind=kOutput, calls=%fused_computation.11 | convolution fusion | flops 67108864 | bytes 3153920 | tf_op jit(solution)/shard_map/ikp,kj->ijp/dot_general | solution.py:125
  101.3 0.0 copy-done.3
  101.3 1.4 convolution_bitcast_fusion.3.p0
  102.7 0.0 copy-start.2
  102.7 0.6 collective-permute-done.5.p3
  103.3 0.0 copy-start.4
  103.3 5.7 %collective-permute-done.3.p2 = f32[504,128]{1,0:T(8,128)} collective-permute-done((f32[504,128]{1,0:T(8,128)S(1)}, f32[504,128]{1,0:T(8,128)}, u32[]{:S(2)}, u32[]{:S(2)}) %collective-permute-start.3) | collective-permute-done | bytes 258080 | tf_op jit(solution)/shard_map/ppermute | solution.py:113
  109.0 0.0 collective-permute-done.1.p1
  109.0 0.0 copy-start.5
  109.0 0.0 copy-done.4
  109.0 0.7 copy-done.5
  109.7 2.9 %shard_map.56 = f32[64,64,128]{2,1,0:T(8,128)} custom-call(s32[1]{0:T(128)} %bitcast.q_ref, f32[504,128]{1,0:T(8,128)} %convolution_bitcast_fusion.3.p0, f32[504,128]{1,0:T(8,128)} %copy-done.5, f32[504,128]{1,0:T(8,128)} %collective-permute-done.3.p2, f32[504,128]{1,0:T(8,128)} %copy-done.4), custom_call_target="tpu_custom_call" | custom-call | tf_op jit(solution)/shard_map/pallas_call | solution.py:59
  112.6 0.0 copy-done.2
  112.6 2.1 %bitcast_subtract_fusion.1 = f32[64,64,128]{2,1,0:T(8,128)S(1)} fusion(f32[64,64,128]{2,1,0:T(8,128)} %shard_map.56, f32[64,64,128]{2,0,1:T(8,128)S(1)} %copy-done.2), kind=kLoop, calls=%fused_computation.4 | loop fusion | flops 524288 | bytes 6291456 | tf_op jit(solution)/shard_map/sub | solution.py:126
  114.7 1.4 fusion.2
  116.1 0.2 copy.31
  116.3 0.8 copy.32
  117.1 41.8 %all_to_all.11 = bf16[256,4,4,128]{3,2,1,0:T(4,128)(2,1)S(1)} all-to-all(bf16[256,4,4,128]{3,2,1,0:T(4,128)(2,1)S(1)} %copy.32), channel_id=1, replica_groups=mesh['oi'=16,'oj'=16] {'oi','oj'}, dimensions={0} | all-to-all | bytes 2097152 | tf_op jit(solution)/shard_map/all_to_all | solution.py:138
  159.0 1.3 copy_bitcast_fusion
Async XLA Ops:
  6.5 1.0 copy-start
  6.5 82.6 %all-gather.4.cloned.1.call-start = ((), (), s32[]{:S(2)}) async-start(), calls=%async_computation.2 | async-start | bytes 2193408 | tf_op jit(solution)/shard_map/all_gather | solution.py:105
  70.5 17.9 %copy-start.7 = (f32[64]{0:T(128)S(1)}, f32[64]{0:T(128)}, u32[]{:S(2)}) copy-start(f32[64]{0:T(128)} %param.8) | copy-start | bytes 772
  73.1 13.4 %collective-permute-start.2 = (bf16[16,126,128]{2,1,0:T(8,128)(2,1)}, bf16[16,126,128]{2,1,0:T(8,128)(2,1)S(1)}, u32[]{:S(2)}, u32[]{:S(2)}) collective-permute-start(bf16[16,126,128]{2,1,0:T(8,128)(2,1)} %shard_map.55), channel_id=1, source_target_pairs={{0,64},{16,80},{32,96},{48,112},{64,0},{80,16},{96,32},{112,48},{1... | collective-permute-start | bytes 1548296 | tf_op jit(solution)/shard_map/ppermute | solution.py:102
  86.5 2.7 %collective-permute-start.4 = (bf16[16,126,128]{2,1,0:T(8,128)(2,1)S(1)}, bf16[16,126,128]{2,1,0:T(8,128)(2,1)S(1)}, u32[]{:S(2)}, u32[]{:S(2)}) collective-permute-start(bf16[16,126,128]{2,1,0:T(8,128)(2,1)S(1)} %collective-permute-done.2), channel_id=1, source_target_pairs={{0,16},{16,0},{32,48},{48,32},{64,80},{80,64},{96,112},{112,96},{1... | collective-permute-start | bytes 1548296 | tf_op jit(solution)/shard_map/ppermute | solution.py:103
  88.4 9.7 %collective-permute-start = (bf16[16,126,128]{2,1,0:T(8,128)(2,1)}, bf16[16,126,128]{2,1,0:T(8,128)(2,1)S(1)}, u32[]{:S(2)}, u32[]{:S(2)}) collective-permute-start(bf16[16,126,128]{2,1,0:T(8,128)(2,1)} %shard_map.55), channel_id=1, source_target_pairs={{0,16},{16,0},{32,48},{48,32},{64,80},{80,64},{96,112},{112,96},{1... | collective-permute-start | bytes 1548296 | tf_op jit(solution)/shard_map/ppermute | solution.py:101
  89.1 7.4 %copy-start.1 = (bf16[16,126,504]{1,2,0:T(8,128)(2,1)S(1)}, bf16[16,126,504]{1,2,0:T(8,128)(2,1)}, u32[]{:S(2)}) copy-start(bf16[16,126,504]{1,2,0:T(8,128)(2,1)} %all-gather.4.cloned.1.call-done) | copy-start | bytes 6096388
  91.6 11.7 %collective-permute-start.5 = (f32[504,128]{1,0:T(8,128)S(1)}, f32[504,128]{1,0:T(8,128)S(1)}, u32[]{:S(2)}, u32[]{:S(2)}) collective-permute-start(f32[504,128]{1,0:T(8,128)S(1)} %convolution_bitcast_fusion), channel_id=1, source_target_pairs={{0,80},{16,64},{32,112},{48,96},{64,16},{80,0},{96,48},{112,32},{1... | collective-permute-start | bytes 774152 | tf_op jit(solution)/shard_map/ppermute | solution.py:113
  97.3 1.8 %copy-start.6 = (bf16[64,64]{1,0:T(8,128)(2,1)S(1)}, bf16[64,64]{1,0:T(8,128)(2,1)}, u32[]{:S(2)}) copy-start(bf16[64,64]{1,0:T(8,128)(2,1)} %param.7) | copy-start | bytes 24580
  97.3 11.7 %collective-permute-start.3 = (f32[504,128]{1,0:T(8,128)S(1)}, f32[504,128]{1,0:T(8,128)}, u32[]{:S(2)}, u32[]{:S(2)}) collective-permute-start(f32[504,128]{1,0:T(8,128)S(1)} %convolution_bitcast_fusion.1), channel_id=1, source_target_pairs={{0,64},{16,80},{32,96},{48,112},{64,0},{80,16},{96,32},{112,48},{1... | collective-permute-start | bytes 774152 | tf_op jit(solution)/shard_map/ppermute | solution.py:113
  98.8 2.5 %copy-start.3 = (bf16[16,126,128]{2,1,0:T(8,128)(2,1)S(1)}, bf16[16,126,128]{2,1,0:T(8,128)(2,1)}, u32[]{:S(2)}) copy-start(bf16[16,126,128]{2,1,0:T(8,128)(2,1)} %shard_map.55) | copy-start | bytes 1548292
  98.8 10.2 %collective-permute-start.1 = (f32[504,128]{1,0:T(8,128)S(1)}, f32[504,128]{1,0:T(8,128)S(1)}, u32[]{:S(2)}, u32[]{:S(2)}) collective-permute-start(f32[504,128]{1,0:T(8,128)S(1)} %convolution_bitcast_fusion.2), channel_id=1, source_target_pairs={{0,16},{16,0},{32,48},{48,32},{64,80},{80,64},{96,112},{112,96},{1... | collective-permute-start | bytes 774152 | tf_op jit(solution)/shard_map/ppermute | solution.py:113
  102.7 9.9 %copy-start.2 = (f32[64,64,128]{2,0,1:T(8,128)S(1)}, f32[64,64,128]{2,0,1:T(8,128)}, u32[]{:S(2)}) copy-start(f32[64,64,128]{2,0,1:T(8,128)} %fusion.3) | copy-start | bytes 6291460
  103.3 5.7 %copy-start.4 = (f32[504,128]{1,0:T(8,128)}, f32[504,128]{1,0:T(8,128)S(1)}, u32[]{:S(2)}) copy-start(f32[504,128]{1,0:T(8,128)S(1)} %collective-permute-done.5.p3) | copy-start | bytes 774148
  109.0 0.7 copy-start.5
Sparse Core Ops, SparseCore 0:
  9.1 77.5 all-gather.3

commit v5 on v4

--- a/solution.py
+++ b/solution.py
@@ -98,20 +98,33 @@
         diff,
     )
 
+    halfb = n_oj // 2
     from_core = lax.ppermute(anti, "oi", perms[0])
-    from_y = lax.ppermute(anti, "oi", perms[1])
-    from_diag = lax.ppermute(from_y, "oi", perms[0])
+    y_parts = [lax.ppermute(anti[s], "oi", perms[1]) for s in (slice(0, halfb), slice(halfb, None))]
+    diag_parts = [lax.ppermute(v, "oi", perms[0]) for v in y_parts]
     w_part = lax.dynamic_slice_in_dim(ladder_w, q * part, part, 1)
     w_blocks = lax.all_gather(w_part, "oj", axis=0, tiled=False)
     contract = (((0, 1), (0, 1)), ((), ()))
 
+    def quarter_of(w, block):
+        return lax.dot_general(w, block, contract, preferred_element_type=jnp.float32)
+
     def quarter(block):
-        return lax.dot_general(w_blocks, block, contract, preferred_element_type=jnp.float32)
+        return quarter_of(w_blocks, block)
+
+    def quarter_split(parts):
+        return quarter_of(w_blocks[:halfb], parts[0]) + quarter_of(w_blocks[halfb:], parts[1])
+
+    def send_split(piece, p):
+        rows = piece.shape[0] // 2
+        moved = [lax.ppermute(piece[s], "oi", p) for s in (slice(0, rows), slice(rows, None))]
+        return jnp.concatenate(moved, axis=0)
 
     own = quarter(anti)
     back = [
-        lax.ppermute(quarter(block), "oi", p)
-        for block, p in zip((from_core, from_y, from_diag), perms)
+        lax.ppermute(quarter(from_core), "oi", perms[0]),
+        send_split(quarter_split(y_parts), perms[1]),
+        send_split(quarter_split(diag_parts), perms[2]),
     ]
     upper_part = vmem_call(
         spread_kernel,

time: 167 us -> 169 us (1.012)
  waiting for transfers between devices: 20.4 us -> 13 us
  starting transfers between devices: 7.14 us -> 12.2 us
    ppermute x5 -> x9, waiting for transfers between devices: 20.3 us -> 13 us  [the longest x2 7.85 us: on_device(): lax.ppermute(anti[s], 'oi', perms[1])]
    ppermute x5 -> x9, starting transfers between devices: 7.13 us -> 11.2 us  [the longest x4 4.82 us: send_split(): lax.ppermute(piece[s], 'oi', p)]
    dot_general x4 -> x6, matrix products: 5.32 us -> 5.26 us  [quarter_of(): lax.dot_general(w, block, contract, preferred_element_type=jnp.float32)]
  transfers between devices with their start and end apart: 7 -> 11, of which waited for: 4 -> 4; matrix products, arithmetic and copies ran while one was open for 9% -> 11% of each run, Pallas kernels for 2% -> 2%
where the time goes in v5:
time: 169 us
  blocking collectives  98.2 us (58%)
  between operations  13.5 us (8%)
  waiting for transfers between devices  13 us (8%)
  starting transfers between devices  12.2 us (7%)
  local copies, waits for them, and re-layouts  10.8 us (6%)
  other arithmetic  7.83 us (5%)
  matrix products  7.48 us (4%)
  Pallas kernels  5.44 us (3%)
    all_to_all x1, blocking collectives, on_device(): recv = lax.all_to_all(send, ('oi', 'oj'), 0, 0, tiled=True)  55.4 us
    all_to_all x1, blocking collectives, on_device(): out_recv = lax.all_to_all(out_send, ('oi', 'oj'), 0, 0, tiled=True)  42.9 us
    ppermute x2, waiting for transfers between devices, on_device(): lax.ppermute(anti[s], 'oi', perms[1])  7.85 us
    pallas_call x2, Pallas kernels, vmem_call(): pl.pallas_call(kernel, out_shape=out_shape, in_specs=[pl.BlockSpec(memory...  5.44 us
    dot_general x6, matrix products, quarter_of(): lax.dot_general(w, block, contract, preferred_element_type=jnp.float32)  5.26 us
    ppermute x4, waiting for transfers between devices, send_split(): lax.ppermute(piece[s], 'oi', p)  5.13 us
    ppermute x4, starting transfers between devices, send_split(): lax.ppermute(piece[s], 'oi', p)  4.82 us
  transfers between devices with their start and end apart: 11, of which 4 were waited for; matrix products, arithmetic and copies ran while one was open for 11% of the time, Pallas kernels for 2%

profile of v5, /device:TPU:1, one launch (start us, length us, event | category | flops | bytes accessed | tf_op | source)
XLA Modules:
  0.0 168.5 jit_solution(220463381777882046)
XLA Ops:
  6.5 0.0 copy-start
  6.5 0.0 all-gather.4.cloned.1.call-start
  6.5 1.0 copy-done
  7.6 0.7 dynamic-slice_bitcast_fusion
  8.2 0.0 all-gather.4.cloned.1.call-update
  8.3 2.1 %reshape.51 = bf16[4,4,256,128]{3,2,1,0:T(8,128)(2,1)S(1)} reshape(bf16[4,4,32768]{2,1,0:T(4,128)(2,1)} %param.5) | data formatting | bytes 2097152 | tf_op jit(solution)/shard_map/reshape | solution.py:81
  10.4 0.8 copy.24
  11.2 55.4 %all_to_all.10 = bf16[256,4,4,128]{3,2,1,0:T(4,128)(2,1)S(1)} all-to-all(bf16[256,4,4,128]{3,2,1,0:T(4,128)(2,1)S(1)} %copy.24), channel_id=1, replica_groups=mesh['oi'=16,'oj'=16] {'oi','oj'}, dimensions={0} | all-to-all | bytes 2097152 | tf_op jit(solution)/shard_map/all_to_all | solution.py:82
  66.6 0.3 copy.25
  66.9 0.8 copy.26
  67.7 0.2 convert_element_type.12
  67.9 2.6 %bitcast_subtract_fusion.2.d_ref = f32[64,64,128]{2,1,0:T(8,128)} fusion(f32[64,64,128]{2,0,1:T(8,128)S(1)} %convert_element_type.12), kind=kLoop, calls=%fused_computation.5 | loop fusion | flops 524288 | bytes 4194304 | tf_op jit(solution)/shard_map/sub | solution.py:93
  70.5 0.0 copy-start.6
  70.5 0.0 copy-start.5
  70.5 2.5 %shard_map.55 = bf16[16,126,128]{2,1,0:T(8,128)(2,1)} custom-call(f32[64,64,128]{2,1,0:T(8,128)} %bitcast_subtract_fusion.2.d_ref), custom_call_target="tpu_custom_call" | custom-call | tf_op jit(solution)/shard_map/pallas_call | solution.py:59
  73.1 1.1 fusion.8
  74.1 0.1 collective-permute-start.3
  74.2 1.5 collective-permute-start.2
  75.7 0.8 dynamic_slice.7
  76.4 0.0 copy-done.6
  76.4 0.1 broadcast_subtract_fusion
  76.5 1.0 collective-permute-start
  77.5 4.3 %collective-permute-done.3 = bf16[8,126,128]{2,1,0:T(8,128)(2,1)S(1)} collective-permute-done((bf16[8,126,128]{2,1,0:T(8,128)(2,1)S(1)}, bf16[8,126,128]{2,1,0:T(8,128)(2,1)S(1)}, u32[]{:S(2)}, u32[]{:S(2)}) %collective-permute-start.3) | collective-permute-done | bytes 258080 | tf_op jit(solution)/shard_map/ppermute | solution.py:103
  81.8 2.0 %collective-permute-start.7 = (bf16[8,126,128]{2,1,0:T(8,128)(2,1)S(1)}, bf16[8,126,128]{2,1,0:T(8,128)(2,1)S(1)}, u32[]{:S(2)}, u32[]{:S(2)}) collective-permute-start(bf16[8,126,128]{2,1,0:T(8,128)(2,1)S(1)} %collective-permute-done.3), channel_id=1, source_target_pairs={{0,16},{16,0},{32,48},{48,32},{64,80},{80,64},{96,112},{112,96},{1... | collective-permute-start | bytes 774152 | tf_op jit(solution)/shard_map/ppermute | solution.py:104
  83.8 3.6 %collective-permute-done.2 = bf16[8,126,128]{2,1,0:T(8,128)(2,1)S(1)} collective-permute-done((bf16[8,126,128]{2,1,0:T(8,128)(2,1)S(1)}, bf16[8,126,128]{2,1,0:T(8,128)(2,1)S(1)}, u32[]{:S(2)}, u32[]{:S(2)}) %collective-permute-start.2) | collective-permute-done | bytes 258080 | tf_op jit(solution)/shard_map/ppermute | solution.py:103
  87.4 1.2 collective-permute-start.6
  88.6 0.0 copy-done.5
  88.6 2.2 %fusion.5 = f32[64,64,128]{2,0,1:T(8,128)} fusion(bf16[64,64,128]{2,0,1:T(8,128)(2,1)S(1)} %bitcast.62, bf16[64,64]{1,0:T(8,128)(2,1)S(1)} %copy-done.5), kind=kOutput, calls=%fused_computation.15 | convolution fusion | flops 67108864 | bytes 3153920 | tf_op jit(solution)/shard_map/ikp,kj->ijp/dot_general | solution.py:138
  90.8 0.0 collective-permute-done.7
  90.8 0.0 all-gather.4.cloned.1.call-done
  90.8 0.0 copy-start.1
  90.8 1.8 %convolution_bitcast_fusion = f32[504,128]{1,0:T(8,128)S(1)} fusion(bf16[16,126,504]{1,2,0:T(8,128)(2,1)} %all-gather.4.cloned.1.call-done, bf16[8,126,128]{2,1,0:T(8,128)(2,1)S(1)} %collective-permute-done.7), kind=kOutput, calls=%fused_computation.6 | convolution fusion | flops 130056192 | bytes 2548224 | tf_op jit(solution)/shard_map/dot_general | solution.py:110
  92.6 0.0 collective-permute-done.6
  92.6 0.1 copy-done.1
  92.7 0.4 fusion.4
  93.1 3.0 %collective-permute-start.8 = (f32[252,128]{1,0:T(8,128)S(1)}, f32[252,128]{1,0:T(8,128)S(1)}, u32[]{:S(2)}, u32[]{:S(2)}) collective-permute-start(f32[252,128]{1,0:T(8,128)S(1)} %get-tuple-element.7), channel_id=1, source_target_pairs={{0,80},{16,64},{32,112},{48,96},{64,16},{80,0},{96,48},{112,32},{1... | collective-permute-start | bytes 387080 | tf_op jit(solution)/shard_map/ppermute | solution.py:120
  96.1 0.3 collective-permute-start.9
  96.4 0.4 convolution_bitcast_fusion.2
  96.9 0.4 fusion.3
  97.3 0.0 copy-start.3
  97.3 1.0 collective-permute-start.4
  98.3 0.5 collective-permute-start.5
  98.9 0.0 collective-permute-done
  98.9 0.7 convolution_bitcast_fusion.4
  99.6 1.7 collective-permute-start.1
  101.3 0.0 copy-done.3
  101.3 1.4 convolution_bitcast_fusion.5.p0
  102.8 0.0 copy-start.2
  102.8 0.0 collective-permute-done.8
  102.8 0.0 collective-permute-done.9
  102.8 0.7 pad_maximum_fusion.1.p3
  103.5 3.2 %collective-permute-done.4 = f32[252,128]{1,0:T(8,128)S(1)} collective-permute-done((f32[252,128]{1,0:T(8,128)S(1)}, f32[252,128]{1,0:T(8,128)S(1)}, u32[]{:S(2)}, u32[]{:S(2)}) %collective-permute-start.4) | collective-permute-done | bytes 129056 | tf_op jit(solution)/shard_map/ppermute | solution.py:120
  106.7 1.9 %collective-permute-done.5 = f32[252,128]{1,0:T(8,128)S(1)} collective-permute-done((f32[252,128]{1,0:T(8,128)S(1)}, f32[252,128]{1,0:T(8,128)S(1)}, u32[]{:S(2)}, u32[]{:S(2)}) %collective-permute-start.5) | collective-permute-done | bytes 129056 | tf_op jit(solution)/shard_map/ppermute | solution.py:120
  108.6 0.7 pad_maximum_fusion.p2
  109.4 0.0 collective-permute-done.1.p1
  109.4 0.7 copy-done.4
  110.1 2.9 %shard_map.56 = f32[64,64,128]{2,1,0:T(8,128)} custom-call(s32[1]{0:T(128)} %bitcast.q_ref, f32[504,128]{1,0:T(8,128)} %convolution_bitcast_fusion.5.p0, f32[504,128]{1,0:T(8,128)} %copy-done.4, f32[504,128]{1,0:T(8,128)} %pad_maximum_fusion.p2, f32[504,128]{1,0:T(8,128)} %pad_maximum_fusion.1.p3), custom_call_target="tpu_custom_call" | custom-call | tf_op jit(solution)/shard_map/pallas_call | solution.py:59
  113.0 0.0 copy-done.2
  113.0 2.1 %bitcast_subtract_fusion.1 = f32[64,64,128]{2,1,0:T(8,128)S(1)} fusion(f32[64,64,128]{2,1,0:T(8,128)} %shard_map.56, f32[64,64,128]{2,0,1:T(8,128)S(1)} %copy-done.2), kind=kLoop, calls=%fused_computation.4 | loop fusion | flops 524288 | bytes 6291456 | tf_op jit(solution)/shard_map/sub | solution.py:139
  115.0 1.4 fusion.2
  116.4 0.2 copy.31
  116.7 0.8 copy.32
  117.5 42.9 %all_to_all.11 = bf16[256,4,4,128]{3,2,1,0:T(4,128)(2,1)S(1)} all-to-all(bf16[256,4,4,128]{3,2,1,0:T(4,128)(2,1)S(1)} %copy.32), channel_id=1, replica_groups=mesh['oi'=16,'oj'=16] {'oi','oj'}, dimensions={0} | all-to-all | bytes 2097152 | tf_op jit(solution)/shard_map/all_to_all | solution.py:151
  160.3 1.3 copy_bitcast_fusion
  (3 shorter events, 0.0 us)
Async XLA Ops:
  6.5 1.0 copy-start
  6.5 84.2 %all-gather.4.cloned.1.call-start = ((), (), s32[]{:S(2)}) async-start(), calls=%async_computation.2 | async-start | bytes 2193408 | tf_op jit(solution)/shard_map/all_gather | solution.py:106
  70.5 5.9 %copy-start.6 = (f32[64]{0:T(128)S(1)}, f32[64]{0:T(128)}, u32[]{:S(2)}) copy-start(f32[64]{0:T(128)} %param.8) | copy-start | bytes 772
  70.5 18.0 %copy-start.5 = (bf16[64,64]{1,0:T(8,128)(2,1)S(1)}, bf16[64,64]{1,0:T(8,128)(2,1)}, u32[]{:S(2)}) copy-start(bf16[64,64]{1,0:T(8,128)(2,1)} %param.7) | copy-start | bytes 24580
  74.1 7.6 %collective-permute-start.3 = (bf16[8,126,128]{2,1,0:T(8,128)(2,1)S(1)}, bf16[8,126,128]{2,1,0:T(8,128)(2,1)S(1)}, u32[]{:S(2)}, u32[]{:S(2)}) collective-permute-start(bf16[8,126,128]{2,1,0:T(8,128)(2,1)S(1)} %get-tuple-element.6), channel_id=1, source_target_pairs={{0,64},{16,80},{32,96},{48,112},{64,0},{80,16},{96,32},{112,48},{1... | collective-permute-start | bytes 774152 | tf_op jit(solution)/shard_map/ppermute | solution.py:103
  74.2 13.2 %collective-permute-start.2 = (bf16[8,126,128]{2,1,0:T(8,128)(2,1)S(1)}, bf16[8,126,128]{2,1,0:T(8,128)(2,1)S(1)}, u32[]{:S(2)}, u32[]{:S(2)}) collective-permute-start(bf16[8,126,128]{2,1,0:T(8,128)(2,1)S(1)} %get-tuple-element.5), channel_id=1, source_target_pairs={{0,64},{16,80},{32,96},{48,112},{64,0},{80,16},{96,32},{112,48},{1... | collective-permute-start | bytes 774152 | tf_op jit(solution)/shard_map/ppermute | solution.py:103
  76.5 22.4 %collective-permute-start = (bf16[16,126,128]{2,1,0:T(8,128)(2,1)}, bf16[16,126,128]{2,1,0:T(8,128)(2,1)S(1)}, u32[]{:S(2)}, u32[]{:S(2)}) collective-permute-start(bf16[16,126,128]{2,1,0:T(8,128)(2,1)} %shard_map.55), channel_id=1, source_target_pairs={{0,16},{16,0},{32,48},{48,32},{64,80},{80,64},{96,112},{112,96},{1... | collective-permute-start | bytes 1548296 | tf_op jit(solution)/shard_map/ppermute | solution.py:102
  81.8 9.0 %collective-permute-start.7 = (bf16[8,126,128]{2,1,0:T(8,128)(2,1)S(1)}, bf16[8,126,128]{2,1,0:T(8,128)(2,1)S(1)}, u32[]{:S(2)}, u32[]{:S(2)}) collective-permute-start(bf16[8,126,128]{2,1,0:T(8,128)(2,1)S(1)} %collective-permute-done.3), channel_id=1, source_target_pairs={{0,16},{16,0},{32,48},{48,32},{64,80},{80,64},{96,112},{112,96},{1... | collective-permute-start | bytes 774152 | tf_op jit(solution)/shard_map/ppermute | solution.py:104
  87.4 5.2 %collective-permute-start.6 = (bf16[8,126,128]{2,1,0:T(8,128)(2,1)S(1)}, bf16[8,126,128]{2,1,0:T(8,128)(2,1)S(1)}, u32[]{:S(2)}, u32[]{:S(2)}) collective-permute-start(bf16[8,126,128]{2,1,0:T(8,128)(2,1)S(1)} %collective-permute-done.2), channel_id=1, source_target_pairs={{0,16},{16,0},{32,48},{48,32},{64,80},{80,64},{96,112},{112,96},{1... | collective-permute-start | bytes 774152 | tf_op jit(solution)/shard_map/ppermute | solution.py:104
  90.8 1.9 %copy-start.1 = (bf16[16,126,504]{1,2,0:T(8,128)(2,1)S(1)}, bf16[16,126,504]{1,2,0:T(8,128)(2,1)}, u32[]{:S(2)}) copy-start(bf16[16,126,504]{1,2,0:T(8,128)(2,1)} %all-gather.4.cloned.1.call-done) | copy-start | bytes 6096388
  93.1 9.6 %collective-permute-start.8 = (f32[252,128]{1,0:T(8,128)S(1)}, f32[252,128]{1,0:T(8,128)S(1)}, u32[]{:S(2)}, u32[]{:S(2)}) collective-permute-start(f32[252,128]{1,0:T(8,128)S(1)} %get-tuple-element.7), channel_id=1, source_target_pairs={{0,80},{16,64},{32,112},{48,96},{64,16},{80,0},{96,48},{112,32},{1... | collective-permute-start | bytes 387080 | tf_op jit(solution)/shard_map/ppermute | solution.py:120
  96.1 6.6 %collective-permute-start.9 = (f32[252,128]{1,0:T(8,128)S(1)}, f32[252,128]{1,0:T(8,128)S(1)}, u32[]{:S(2)}, u32[]{:S(2)}) collective-permute-start(f32[252,128]{1,0:T(8,128)S(1)} %get-tuple-element.8), channel_id=1, source_target_pairs={{0,80},{16,64},{32,112},{48,96},{64,16},{80,0},{96,48},{112,32},{1... | collective-permute-start | bytes 387080 | tf_op jit(solution)/shard_map/ppermute | solution.py:120
  97.3 4.0 %copy-start.3 = (bf16[16,126,128]{2,1,0:T(8,128)(2,1)S(1)}, bf16[16,126,128]{2,1,0:T(8,128)(2,1)}, u32[]{:S(2)}) copy-start(bf16[16,126,128]{2,1,0:T(8,128)(2,1)} %shard_map.55) | copy-start | bytes 1548292
  97.3 9.4 %collective-permute-start.4 = (f32[252,128]{1,0:T(8,128)S(1)}, f32[252,128]{1,0:T(8,128)S(1)}, u32[]{:S(2)}, u32[]{:S(2)}) collective-permute-start(f32[252,128]{1,0:T(8,128)S(1)} %get-tuple-element.9), channel_id=1, source_target_pairs={{0,64},{16,80},{32,96},{48,112},{64,0},{80,16},{96,32},{112,48},{1... | collective-permute-start | bytes 387080 | tf_op jit(solution)/shard_map/ppermute | solution.py:120
  98.3 10.3 %collective-permute-start.5 = (f32[252,128]{1,0:T(8,128)S(1)}, f32[252,128]{1,0:T(8,128)S(1)}, u32[]{:S(2)}, u32[]{:S(2)}) collective-permute-start(f32[252,128]{1,0:T(8,128)S(1)} %get-tuple-element.10), channel_id=1, source_target_pairs={{0,64},{16,80},{32,96},{48,112},{64,0},{80,16},{96,32},{112,48},{1... | collective-permute-start | bytes 387080 | tf_op jit(solution)/shard_map/ppermute | solution.py:120
  99.6 9.7 %collective-permute-start.1 = (f32[504,128]{1,0:T(8,128)S(1)}, f32[504,128]{1,0:T(8,128)S(1)}, u32[]{:S(2)}, u32[]{:S(2)}) collective-permute-start(f32[504,128]{1,0:T(8,128)S(1)} %convolution_bitcast_fusion.4), channel_id=1, source_target_pairs={{0,16},{16,0},{32,48},{48,32},{64,80},{80,64},{96,112},{112,96},{1... | collective-permute-start | bytes 774152 | tf_op jit(solution)/shard_map/ppermute | solution.py:125
  102.8 10.2 %copy-start.2 = (f32[64,64,128]{2,0,1:T(8,128)S(1)}, f32[64,64,128]{2,0,1:T(8,128)}, u32[]{:S(2)}) copy-start(f32[64,64,128]{2,0,1:T(8,128)} %fusion.5) | copy-start | bytes 6291460
  109.4 0.7 copy-start.4
Sparse Core Ops, SparseCore 0:
  9.1 77.0 all-gather.3

commit v6 on v4

--- a/solution.py
+++ b/solution.py
@@ -102,7 +102,12 @@
     from_y = lax.ppermute(anti, "oi", perms[1])
     from_diag = lax.ppermute(from_y, "oi", perms[0])
     w_part = lax.dynamic_slice_in_dim(ladder_w, q * part, part, 1)
-    w_blocks = lax.all_gather(w_part, "oj", axis=0, tiled=False)
+    shifted = [w_part] + [
+        lax.ppermute(w_part, "oj", [(b, (b + s) % n_oj) for b in range(n_oj)])
+        for s in range(1, n_oj)
+    ]
+    source = (me_j - jnp.arange(n_oj, dtype=me_j.dtype)) % n_oj
+    w_blocks = jnp.zeros((n_oj,) + w_part.shape, w_part.dtype).at[source].set(jnp.stack(shifted))
     contract = (((0, 1), (0, 1)), ((), ()))
 
     def quarter(block):

time: 167 us -> 185 us (1.11)
  starting transfers between devices: 7.14 us -> 69.1 us
  blocking collectives: 97.2 us -> 44 us
  local copies, waits for them, and re-layouts: 9.58 us -> 23.3 us
  between operations: 13.5 us -> 0.18 us
  waiting for transfers between devices: 20.4 us -> 26.6 us
    all_to_all x1 -> x0, blocking collectives: 55.4 us -> none  [on_device(): recv = lax.all_to_all(send, ('oi', 'oj'), 0, 0, tiled=True)]
    ppermute x0 -> x15, starting transfers between devices: none -> 44.1 us  [on_device(): lax.ppermute(w_part, 'oj', [(b, (b + s) % n_oj) for b in range(n_oj)])]
    ppermute x0 -> x15, waiting for transfers between devices: none -> 18.5 us  [on_device(): lax.ppermute(w_part, 'oj', [(b, (b + s) % n_oj) for b in range(n_oj)])]
    all_to_all x0 -> x1, starting transfers between devices: none -> 12.1 us  [on_device(): recv = lax.all_to_all(send, ('oi', 'oj'), 0, 0, tiled=True)]
    ppermute x1, waiting for transfers between devices: 13.4 us -> 2.2 us  [on_device(): from_y = lax.ppermute(anti, 'oi', perms[1])]
    unnamed x17 -> x25, local copies, waits for them, and re-layouts: 2.43 us -> 10.9 us
    ppermute x1, starting transfers between devices: 0.01 us -> 4.33 us  [on_device(): from_core = lax.ppermute(anti, 'oi', perms[0])]
    ppermute x1, starting transfers between devices: 1.15 us -> 4.92 us  [on_device(): from_diag = lax.ppermute(from_y, 'oi', perms[0])]
  transfers between devices with their start and end apart: 7 -> 22, of which waited for: 4 -> 5; matrix products, arithmetic and copies ran while one was open for 9% -> 17% of each run, Pallas kernels for 2% -> 1%
where the time goes in v6:
time: 185 us; the launch traced here: 184 us
  starting transfers between devices  69.1 us (37%)
  blocking collectives  44 us (24%)
  waiting for transfers between devices  26.6 us (14%)
  local copies, waits for them, and re-layouts  23.3 us (13%)
  matrix products  8.86 us (5%)
  other arithmetic  6.27 us (3%)
  Pallas kernels  5.62 us (3%)
    ppermute x15, starting transfers between devices, on_device(): lax.ppermute(w_part, 'oj', [(b, (b + s) % n_oj) for b in range(n_oj)])  44.1 us
    all_to_all x1, blocking collectives, on_device(): out_recv = lax.all_to_all(out_send, ('oi', 'oj'), 0, 0, tiled=True)  44 us
    ppermute x15, waiting for transfers between devices, on_device(): lax.ppermute(w_part, 'oj', [(b, (b + s) % n_oj) for b in range(n_oj)])  18.5 us
    all_to_all x1, starting transfers between devices, on_device(): recv = lax.all_to_all(send, ('oi', 'oj'), 0, 0, tiled=True)  12.1 us
    unnamed x25, local copies, waits for them, and re-layouts  10.9 us
    dot_general x4, matrix products, quarter(): lax.dot_general(w_blocks, block, contract, preferred_element_type=jnp.flo...  6.63 us
    ppermute x3, waiting for transfers between devices, on_device(): lax.ppermute(quarter(block), 'oi', p)  5.96 us
    pallas_call x2, Pallas kernels, vmem_call(): pl.pallas_call(kernel, out_shape=out_shape, in_specs=[pl.BlockSpec(memory...  5.62 us
  transfers between devices with their start and end apart: 22, of which 5 were waited for; matrix products, arithmetic and copies ran while one was open for 17% of the time, Pallas kernels for 1%

profile of v6, /device:TPU:1, one launch (start us, length us, event | category | flops | bytes accessed | tf_op | source)
XLA Modules:
  0.0 184.0 jit_solution(6069541408085407663)
XLA Ops:
  0.0 1.6 bitcast_dynamic-update-slice_fusion.15
  1.6 2.0 %collective-permute-start = (bf16[126,504]{0,1:T(8,128)(2,1)S(1)}, bf16[126,504]{0,1:T(8,128)(2,1)S(1)}, u32[]{:S(2)}, u32[]{:S(2)}) collective-permute-start(bf16[126,504]{0,1:T(8,128)(2,1)S(1)} %get-tuple-element.6), channel_id=1, source_target_pairs={{0,1},{1,2},{2,3},{3,4},{4,5},{5,6},{6,7},{7,8},{8,9},{9,10},{10,1... | collective-permute-start | bytes 381032 | tf_op jit(solution)/shard_map/ppermute | solution.py:106
  3.6 1.6 collective-permute-start.1
  5.3 3.0 %collective-permute-start.2 = (bf16[126,504]{0,1:T(8,128)(2,1)S(1)}, bf16[126,504]{0,1:T(8,128)(2,1)S(1)}, u32[]{:S(2)}, u32[]{:S(2)}) collective-permute-start(bf16[126,504]{0,1:T(8,128)(2,1)S(1)} %get-tuple-element.6), channel_id=1, source_target_pairs={{0,3},{1,4},{2,5},{3,6},{4,7},{5,8},{6,9},{7,10},{8,11},{9,12},{10... | collective-permute-start | bytes 381032 | tf_op jit(solution)/shard_map/ppermute | solution.py:106
  8.2 3.3 %collective-permute-start.3 = (bf16[126,504]{0,1:T(8,128)(2,1)S(1)}, bf16[126,504]{0,1:T(8,128)(2,1)S(1)}, u32[]{:S(2)}, u32[]{:S(2)}) collective-permute-start(bf16[126,504]{0,1:T(8,128)(2,1)S(1)} %get-tuple-element.6), channel_id=1, source_target_pairs={{0,4},{1,5},{2,6},{3,7},{4,8},{5,9},{6,10},{7,11},{8,12},{9,13},{1... | collective-permute-start | bytes 381032 | tf_op jit(solution)/shard_map/ppermute | solution.py:106
  11.5 2.1 %collective-permute-start.4 = (bf16[126,504]{0,1:T(8,128)(2,1)S(1)}, bf16[126,504]{0,1:T(8,128)(2,1)S(1)}, u32[]{:S(2)}, u32[]{:S(2)}) collective-permute-start(bf16[126,504]{0,1:T(8,128)(2,1)S(1)} %get-tuple-element.6), channel_id=1, source_target_pairs={{0,5},{1,6},{2,7},{3,8},{4,9},{5,10},{6,11},{7,12},{8,13},{9,14},{... | collective-permute-start | bytes 381032 | tf_op jit(solution)/shard_map/ppermute | solution.py:106
  13.6 2.1 %reshape.100 = bf16[4,4,256,128]{3,2,1,0:T(8,128)(2,1)S(1)} reshape(bf16[4,4,32768]{2,1,0:T(4,128)(2,1)} %param.5) | data formatting | bytes 2097152 | tf_op jit(solution)/shard_map/reshape | solution.py:81
  15.8 1.8 copy.24
  17.6 12.1 %all-to-all-start = ((bf16[256,4,4,128]{3,2,1,0:T(4,128)(2,1)}), bf16[256,4,4,128]{3,2,1,0:T(4,128)(2,1)S(1)}, u32[]{:S(2)}, u32[]{:S(2)}) async-start(bf16[256,4,4,128]{3,2,1,0:T(4,128)(2,1)} %copy.24), calls=%async_computation | async-start | bytes 2097152 | tf_op jit(solution)/shard_map/all_to_all | solution.py:82
  29.7 0.8 dynamic_slice.7
  30.6 3.9 %collective-permute-start.5 = (bf16[126,504]{0,1:T(8,128)(2,1)S(1)}, bf16[126,504]{0,1:T(8,128)(2,1)S(1)}, u32[]{:S(2)}, u32[]{:S(2)}) collective-permute-start(bf16[126,504]{0,1:T(8,128)(2,1)S(1)} %get-tuple-element.6), channel_id=1, source_target_pairs={{0,6},{1,7},{2,8},{3,9},{4,10},{5,11},{6,12},{7,13},{8,14},{9,15},... | collective-permute-start | bytes 381032 | tf_op jit(solution)/shard_map/ppermute | solution.py:106
  34.5 0.7 bitcast_dynamic-update-slice_fusion.14
  35.1 4.1 %collective-permute-start.6 = (bf16[126,504]{0,1:T(8,128)(2,1)S(1)}, bf16[126,504]{0,1:T(8,128)(2,1)S(1)}, u32[]{:S(2)}, u32[]{:S(2)}) collective-permute-start(bf16[126,504]{0,1:T(8,128)(2,1)S(1)} %get-tuple-element.6), channel_id=1, source_target_pairs={{0,7},{1,8},{2,9},{3,10},{4,11},{5,12},{6,13},{7,14},{8,15},{9,0},... | collective-permute-start | bytes 381032 | tf_op jit(solution)/shard_map/ppermute | solution.py:106
  39.3 0.7 bitcast_dynamic-update-slice_fusion.13
  39.9 1.0 collective-permute-start.7
  40.9 0.7 bitcast_dynamic-update-slice_fusion.12
  41.6 4.6 %collective-permute-start.8 = (bf16[126,504]{0,1:T(8,128)(2,1)S(1)}, bf16[126,504]{0,1:T(8,128)(2,1)S(1)}, u32[]{:S(2)}, u32[]{:S(2)}) collective-permute-start(bf16[126,504]{0,1:T(8,128)(2,1)S(1)} %get-tuple-element.6), channel_id=1, source_target_pairs={{0,9},{1,10},{2,11},{3,12},{4,13},{5,14},{6,15},{7,0},{8,1},{9,2},... | collective-permute-start | bytes 381032 | tf_op jit(solution)/shard_map/ppermute | solution.py:106
  46.2 0.7 bitcast_dynamic-update-slice_fusion.11
  46.9 3.4 %collective-permute-start.9 = (bf16[126,504]{0,1:T(8,128)(2,1)S(1)}, bf16[126,504]{0,1:T(8,128)(2,1)S(1)}, u32[]{:S(2)}, u32[]{:S(2)}) collective-permute-start(bf16[126,504]{0,1:T(8,128)(2,1)S(1)} %get-tuple-element.6), channel_id=1, source_target_pairs={{0,10},{1,11},{2,12},{3,13},{4,14},{5,15},{6,0},{7,1},{8,2},{9,3},... | collective-permute-start | bytes 381032 | tf_op jit(solution)/shard_map/ppermute | solution.py:106
  50.3 0.7 bitcast_dynamic-update-slice_fusion.10
  50.9 16.8 %collective-permute-done.5 = bf16[126,504]{0,1:T(8,128)(2,1)S(1)} collective-permute-done((bf16[126,504]{0,1:T(8,128)(2,1)S(1)}, bf16[126,504]{0,1:T(8,128)(2,1)S(1)}, u32[]{:S(2)}, u32[]{:S(2)}) %collective-permute-start.5) | collective-permute-done | bytes 127040 | tf_op jit(solution)/shard_map/ppermute | solution.py:106
  67.7 1.0 collective-permute-start.10
  68.7 0.7 bitcast_dynamic-update-slice_fusion.9
  69.4 1.1 collective-permute-done.6
  70.5 9.0 %collective-permute-start.11 = (bf16[126,504]{0,1:T(8,128)(2,1)S(1)}, bf16[126,504]{0,1:T(8,128)(2,1)S(1)}, u32[]{:S(2)}, u32[]{:S(2)}) collective-permute-start(bf16[126,504]{0,1:T(8,128)(2,1)S(1)} %get-tuple-element.6), channel_id=1, source_target_pairs={{0,12},{1,13},{2,14},{3,15},{4,0},{5,1},{6,2},{7,3},{8,4},{9,5},{1... | collective-permute-start | bytes 381032 | tf_op jit(solution)/shard_map/ppermute | solution.py:106
  79.5 0.7 bitcast_dynamic-update-slice_fusion.8
  80.2 0.9 collective-permute-start.12
  81.1 0.7 bitcast_dynamic-update-slice_fusion.7
  81.7 0.7 bitcast_dynamic-update-slice_fusion.6
  82.4 4.1 %collective-permute-start.14 = (bf16[126,504]{0,1:T(8,128)(2,1)S(1)}, bf16[126,504]{0,1:T(8,128)(2,1)S(1)}, u32[]{:S(2)}, u32[]{:S(2)}) collective-permute-start(bf16[126,504]{0,1:T(8,128)(2,1)S(1)} %get-tuple-element.6), channel_id=1, source_target_pairs={{0,15},{1,0},{2,1},{3,2},{4,3},{5,4},{6,5},{7,6},{8,7},{9,8},{10,9... | collective-permute-start | bytes 381032 | tf_op jit(solution)/shard_map/ppermute | solution.py:106
  86.5 0.7 bitcast_dynamic-update-slice_fusion.5
  87.2 0.5 collective-permute-done.10
  87.7 0.7 bitcast_dynamic-update-slice_fusion.4
  88.4 0.3 copy.25
  88.7 0.8 copy.26
  89.5 0.2 convert_element_type.12
  89.8 2.6 %bitcast_subtract_fusion.2.d_ref = f32[64,64,128]{2,1,0:T(8,128)} fusion(f32[64,64,128]{2,0,1:T(8,128)S(1)} %convert_element_type.12), kind=kLoop, calls=%fused_computation.6 | loop fusion | flops 524288 | bytes 4194304 | tf_op jit(solution)/shard_map/sub | solution.py:93
  92.3 2.5 %shard_map.55 = bf16[16,126,128]{2,1,0:T(8,128)(2,1)} custom-call(f32[64,64,128]{2,1,0:T(8,128)} %bitcast_subtract_fusion.2.d_ref), custom_call_target="tpu_custom_call" | custom-call | tf_op jit(solution)/shard_map/pallas_call | solution.py:59
  94.9 1.2 collective-permute-start.17
  96.1 0.7 bitcast_dynamic-update-slice_fusion.3
  96.7 4.3 %collective-permute-start.15 = (bf16[16,126,128]{2,1,0:T(8,128)(2,1)}, bf16[16,126,128]{2,1,0:T(8,128)(2,1)}, u32[]{:S(2)}, u32[]{:S(2)}) collective-permute-start(bf16[16,126,128]{2,1,0:T(8,128)(2,1)} %shard_map.55), channel_id=1, source_target_pairs={{0,16},{16,0},{32,48},{48,32},{64,80},{80,64},{96,112},{112,96},{1... | collective-permute-start | bytes 1548296 | tf_op jit(solution)/shard_map/ppermute | solution.py:101
  101.1 0.6 bitcast_dynamic-update-slice_fusion.2
  101.7 0.7 bitcast_dynamic-update-slice_fusion.1
  102.4 2.2 %collective-permute-done.17 = bf16[16,126,128]{2,1,0:T(8,128)(2,1)} collective-permute-done((bf16[16,126,128]{2,1,0:T(8,128)(2,1)}, bf16[16,126,128]{2,1,0:T(8,128)(2,1)}, u32[]{:S(2)}, u32[]{:S(2)}) %collective-permute-start.17) | collective-permute-done | bytes 516128 | tf_op jit(solution)/shard_map/ppermute | solution.py:102
  104.6 4.9 %collective-permute-start.19 = (bf16[16,126,128]{2,1,0:T(8,128)(2,1)}, bf16[16,126,128]{2,1,0:T(8,128)(2,1)}, u32[]{:S(2)}, u32[]{:S(2)}) collective-permute-start(bf16[16,126,128]{2,1,0:T(8,128)(2,1)} %collective-permute-done.17), channel_id=1, source_target_pairs={{0,16},{16,0},{32,48},{48,32},{64,80},{80,64},{96,112},{112,96},{1... | collective-permute-start | bytes 1548296 | tf_op jit(solution)/shard_map/ppermute | solution.py:103
  109.5 0.7 bitcast_dynamic-update-slice_fusion
  110.2 0.3 broadcast_in_dim.2
  110.4 3.4 %scatter_fusion = bf16[16,126,504]{1,2,0:T(8,128)(2,1)S(1)} fusion(bf16[16,126,504]{1,2,0:T(8,128)(2,1)S(1)} %broadcast_in_dim.2, s32[16]{0:T(128)S(1)} %fusion.7, bf16[16,126,504]{1,2,0:T(8,128)(2,1)} %bitcast_dynamic-update-slice_fusion), kind=kCustom, calls=%fused_computation | custom fusion | bytes 6096448 | tf_op jit(solution)/shard_map/scatter | solution.py:110
  113.9 1.7 convolution_bitcast_fusion.2
  115.7 0.1 collective-permute-start.16
  115.8 1.7 convolution_bitcast_fusion.1
  117.5 1.3 collective-permute-start.18
  118.8 1.7 convolution_bitcast_fusion
  120.6 1.0 collective-permute-start.20
  121.6 2.2 %fusion.3 = f32[64,64,128]{2,0,1:T(8,128)} fusion(bf16[64,64,128]{2,0,1:T(8,128)(2,1)S(1)} %bitcast.82, bf16[64,64]{1,0:T(8,128)(2,1)S(1)} %copy-done), kind=kOutput, calls=%fused_computation.12 | convolution fusion | flops 67108864 | bytes 3153920 | tf_op jit(solution)/shard_map/ikp,kj->ijp/dot_general | solution.py:130
  123.8 1.4 convolution_bitcast_fusion.3.p0
  125.2 6.0 %collective-permute-done.20.p3 = f32[504,128]{1,0:T(8,128)} collective-permute-done((f32[504,128]{1,0:T(8,128)S(1)}, f32[504,128]{1,0:T(8,128)}, u32[]{:S(2)}, u32[]{:S(2)}) %collective-permute-start.20) | collective-permute-done | bytes 258080 | tf_op jit(solution)/shard_map/ppermute | solution.py:118
  131.2 3.1 %shard_map.56 = f32[64,64,128]{2,1,0:T(8,128)} custom-call(s32[1]{0:T(128)} %bitcast.q_ref, f32[504,128]{1,0:T(8,128)} %convolution_bitcast_fusion.3.p0, f32[504,128]{1,0:T(8,128)} %copy-done.3, f32[504,128]{1,0:T(8,128)} %collective-permute-done.18.p2, f32[504,128]{1,0:T(8,128)} %collective-permute-done.20.p3), custom_call_target="tpu_custom_call" | custom-call | tf_op jit(solution)/shard_map/pallas_call | solution.py:59
  134.3 2.0 %bitcast_subtract_fusion.1 = f32[64,64,128]{2,1,0:T(8,128)S(1)} fusion(f32[64,64,128]{2,1,0:T(8,128)} %shard_map.56, f32[64,64,128]{2,0,1:T(8,128)S(1)} %copy-done.1), kind=kLoop, calls=%fused_computation.5 | loop fusion | flops 524288 | bytes 6291456 | tf_op jit(solution)/shard_map/sub | solution.py:131
  136.3 1.4 fusion.2
  137.7 0.2 copy.31
  137.9 0.8 copy.32
  138.7 44.0 %all_to_all.10 = bf16[256,4,4,128]{3,2,1,0:T(4,128)(2,1)S(1)} all-to-all(bf16[256,4,4,128]{3,2,1,0:T(4,128)(2,1)S(1)} %copy.32), channel_id=1, replica_groups=mesh['oi'=16,'oj'=16] {'oi','oj'}, dimensions={0} | all-to-all | bytes 2097152 | tf_op jit(solution)/shard_map/all_to_all | solution.py:143
  182.7 1.3 copy_bitcast_fusion
  (30 shorter events, 0.2 us)
Async XLA Ops:
  0.0 121.6 %copy-start = (bf16[64,64]{1,0:T(8,128)(2,1)S(1)}, bf16[64,64]{1,0:T(8,128)(2,1)}, u32[]{:S(2)}) copy-start(bf16[64,64]{1,0:T(8,128)(2,1)} %param.7) | copy-start | bytes 24580
  1.6 29.0 %collective-permute-start = (bf16[126,504]{0,1:T(8,128)(2,1)S(1)}, bf16[126,504]{0,1:T(8,128)(2,1)S(1)}, u32[]{:S(2)}, u32[]{:S(2)}) collective-permute-start(bf16[126,504]{0,1:T(8,128)(2,1)S(1)} %get-tuple-element.6), channel_id=1, source_target_pairs={{0,1},{1,2},{2,3},{3,4},{4,5},{5,6},{6,7},{7,8},{8,9},{9,10},{10,1... | collective-permute-start | bytes 381032 | tf_op jit(solution)/shard_map/ppermute | solution.py:106
  3.6 31.5 %collective-permute-start.1 = (bf16[126,504]{0,1:T(8,128)(2,1)S(1)}, bf16[126,504]{0,1:T(8,128)(2,1)S(1)}, u32[]{:S(2)}, u32[]{:S(2)}) collective-permute-start(bf16[126,504]{0,1:T(8,128)(2,1)S(1)} %get-tuple-element.6), channel_id=1, source_target_pairs={{0,2},{1,3},{2,4},{3,5},{4,6},{5,7},{6,8},{7,9},{8,10},{9,11},{10,... | collective-permute-start | bytes 381032 | tf_op jit(solution)/shard_map/ppermute | solution.py:106
  5.3 34.7 %collective-permute-start.2 = (bf16[126,504]{0,1:T(8,128)(2,1)S(1)}, bf16[126,504]{0,1:T(8,128)(2,1)S(1)}, u32[]{:S(2)}, u32[]{:S(2)}) collective-permute-start(bf16[126,504]{0,1:T(8,128)(2,1)S(1)} %get-tuple-element.6), channel_id=1, source_target_pairs={{0,3},{1,4},{2,5},{3,6},{4,7},{5,8},{6,9},{7,10},{8,11},{9,12},{10... | collective-permute-start | bytes 381032 | tf_op jit(solution)/shard_map/ppermute | solution.py:106
  8.2 33.4 %collective-permute-start.3 = (bf16[126,504]{0,1:T(8,128)(2,1)S(1)}, bf16[126,504]{0,1:T(8,128)(2,1)S(1)}, u32[]{:S(2)}, u32[]{:S(2)}) collective-permute-start(bf16[126,504]{0,1:T(8,128)(2,1)S(1)} %get-tuple-element.6), channel_id=1, source_target_pairs={{0,4},{1,5},{2,6},{3,7},{4,8},{5,9},{6,10},{7,11},{8,12},{9,13},{1... | collective-permute-start | bytes 381032 | tf_op jit(solution)/shard_map/ppermute | solution.py:106
  11.5 35.4 %collective-permute-start.4 = (bf16[126,504]{0,1:T(8,128)(2,1)S(1)}, bf16[126,504]{0,1:T(8,128)(2,1)S(1)}, u32[]{:S(2)}, u32[]{:S(2)}) collective-permute-start(bf16[126,504]{0,1:T(8,128)(2,1)S(1)} %get-tuple-element.6), channel_id=1, source_target_pairs={{0,5},{1,6},{2,7},{3,8},{4,9},{5,10},{6,11},{7,12},{8,13},{9,14},{... | collective-permute-start | bytes 381032 | tf_op jit(solution)/shard_map/ppermute | solution.py:106
  15.8 14.7 %copy-start.4 = (f32[64]{0:T(128)S(1)}, f32[64]{0:T(128)}, u32[]{:S(2)}) copy-start(f32[64]{0:T(128)} %param.8) | copy-start | bytes 772
  17.6 70.8 %all-to-all-start = ((bf16[256,4,4,128]{3,2,1,0:T(4,128)(2,1)}), bf16[256,4,4,128]{3,2,1,0:T(4,128)(2,1)S(1)}, u32[]{:S(2)}, u32[]{:S(2)}) async-start(bf16[256,4,4,128]{3,2,1,0:T(4,128)(2,1)} %copy.24), calls=%async_computation | async-start | bytes 2097152 | tf_op jit(solution)/shard_map/all_to_all | solution.py:82
  30.6 37.1 %collective-permute-start.5 = (bf16[126,504]{0,1:T(8,128)(2,1)S(1)}, bf16[126,504]{0,1:T(8,128)(2,1)S(1)}, u32[]{:S(2)}, u32[]{:S(2)}) collective-permute-start(bf16[126,504]{0,1:T(8,128)(2,1)S(1)} %get-tuple-element.6), channel_id=1, source_target_pairs={{0,6},{1,7},{2,8},{3,9},{4,10},{5,11},{6,12},{7,13},{8,14},{9,15},... | collective-permute-start | bytes 381032 | tf_op jit(solution)/shard_map/ppermute | solution.py:106
  35.1 35.4 %collective-permute-start.6 = (bf16[126,504]{0,1:T(8,128)(2,1)S(1)}, bf16[126,504]{0,1:T(8,128)(2,1)S(1)}, u32[]{:S(2)}, u32[]{:S(2)}) collective-permute-start(bf16[126,504]{0,1:T(8,128)(2,1)S(1)} %get-tuple-element.6), channel_id=1, source_target_pairs={{0,7},{1,8},{2,9},{3,10},{4,11},{5,12},{6,13},{7,14},{8,15},{9,0},... | collective-permute-start | bytes 381032 | tf_op jit(solution)/shard_map/ppermute | solution.py:106
  39.9 40.2 %collective-permute-start.7 = (bf16[126,504]{0,1:T(8,128)(2,1)S(1)}, bf16[126,504]{0,1:T(8,128)(2,1)S(1)}, u32[]{:S(2)}, u32[]{:S(2)}) collective-permute-start(bf16[126,504]{0,1:T(8,128)(2,1)S(1)} %get-tuple-element.6), channel_id=1, source_target_pairs={{0,8},{1,9},{2,10},{3,11},{4,12},{5,13},{6,14},{7,15},{8,0},{9,1},... | collective-permute-start | bytes 381032 | tf_op jit(solution)/shard_map/ppermute | solution.py:106
  41.6 40.1 %collective-permute-start.8 = (bf16[126,504]{0,1:T(8,128)(2,1)S(1)}, bf16[126,504]{0,1:T(8,128)(2,1)S(1)}, u32[]{:S(2)}, u32[]{:S(2)}) collective-permute-start(bf16[126,504]{0,1:T(8,128)(2,1)S(1)} %get-tuple-element.6), channel_id=1, source_target_pairs={{0,9},{1,10},{2,11},{3,12},{4,13},{5,14},{6,15},{7,0},{8,1},{9,2},... | collective-permute-start | bytes 381032 | tf_op jit(solution)/shard_map/ppermute | solution.py:106
  46.9 35.5 %collective-permute-start.9 = (bf16[126,504]{0,1:T(8,128)(2,1)S(1)}, bf16[126,504]{0,1:T(8,128)(2,1)S(1)}, u32[]{:S(2)}, u32[]{:S(2)}) collective-permute-start(bf16[126,504]{0,1:T(8,128)(2,1)S(1)} %get-tuple-element.6), channel_id=1, source_target_pairs={{0,10},{1,11},{2,12},{3,13},{4,14},{5,15},{6,0},{7,1},{8,2},{9,3},... | collective-permute-start | bytes 381032 | tf_op jit(solution)/shard_map/ppermute | solution.py:106
  67.7 20.0 %collective-permute-start.10 = (bf16[126,504]{0,1:T(8,128)(2,1)S(1)}, bf16[126,504]{0,1:T(8,128)(2,1)S(1)}, u32[]{:S(2)}, u32[]{:S(2)}) collective-permute-start(bf16[126,504]{0,1:T(8,128)(2,1)S(1)} %get-tuple-element.6), channel_id=1, source_target_pairs={{0,11},{1,12},{2,13},{3,14},{4,15},{5,0},{6,1},{7,2},{8,3},{9,4},{... | collective-permute-start | bytes 381032 | tf_op jit(solution)/shard_map/ppermute | solution.py:106
  70.5 25.6 %collective-permute-start.11 = (bf16[126,504]{0,1:T(8,128)(2,1)S(1)}, bf16[126,504]{0,1:T(8,128)(2,1)S(1)}, u32[]{:S(2)}, u32[]{:S(2)}) collective-permute-start(bf16[126,504]{0,1:T(8,128)(2,1)S(1)} %get-tuple-element.6), channel_id=1, source_target_pairs={{0,12},{1,13},{2,14},{3,15},{4,0},{5,1},{6,2},{7,3},{8,4},{9,5},{1... | collective-permute-start | bytes 381032 | tf_op jit(solution)/shard_map/ppermute | solution.py:106
  80.2 20.9 %collective-permute-start.12 = (bf16[126,504]{0,1:T(8,128)(2,1)S(1)}, bf16[126,504]{0,1:T(8,128)(2,1)S(1)}, u32[]{:S(2)}, u32[]{:S(2)}) collective-permute-start(bf16[126,504]{0,1:T(8,128)(2,1)S(1)} %get-tuple-element.6), channel_id=1, source_target_pairs={{0,13},{1,14},{2,15},{3,0},{4,1},{5,2},{6,3},{7,4},{8,5},{9,6},{10... | collective-permute-start | bytes 381032 | tf_op jit(solution)/shard_map/ppermute | solution.py:106
  81.7 20.0 %collective-permute-start.13 = (bf16[126,504]{0,1:T(8,128)(2,1)S(1)}, bf16[126,504]{0,1:T(8,128)(2,1)S(1)}, u32[]{:S(2)}, u32[]{:S(2)}) collective-permute-start(bf16[126,504]{0,1:T(8,128)(2,1)S(1)} %get-tuple-element.6), channel_id=1, source_target_pairs={{0,14},{1,15},{2,0},{3,1},{4,2},{5,3},{6,4},{7,5},{8,6},{9,7},{10,... | collective-permute-start | bytes 381032 | tf_op jit(solution)/shard_map/ppermute | solution.py:106
  82.4 27.1 %collective-permute-start.14 = (bf16[126,504]{0,1:T(8,128)(2,1)S(1)}, bf16[126,504]{0,1:T(8,128)(2,1)S(1)}, u32[]{:S(2)}, u32[]{:S(2)}) collective-permute-start(bf16[126,504]{0,1:T(8,128)(2,1)S(1)} %get-tuple-element.6), channel_id=1, source_target_pairs={{0,15},{1,0},{2,1},{3,2},{4,3},{5,4},{6,5},{7,6},{8,7},{9,8},{10,9... | collective-permute-start | bytes 381032 | tf_op jit(solution)/shard_map/ppermute | solution.py:106
  94.9 9.7 %collective-permute-start.17 = (bf16[16,126,128]{2,1,0:T(8,128)(2,1)}, bf16[16,126,128]{2,1,0:T(8,128)(2,1)}, u32[]{:S(2)}, u32[]{:S(2)}) collective-permute-start(bf16[16,126,128]{2,1,0:T(8,128)(2,1)} %shard_map.55), channel_id=1, source_target_pairs={{0,64},{16,80},{32,96},{48,112},{64,0},{80,16},{96,32},{112,48},{1... | collective-permute-start | bytes 1548296 | tf_op jit(solution)/shard_map/ppermute | solution.py:102
  96.7 17.2 %collective-permute-start.15 = (bf16[16,126,128]{2,1,0:T(8,128)(2,1)}, bf16[16,126,128]{2,1,0:T(8,128)(2,1)}, u32[]{:S(2)}, u32[]{:S(2)}) collective-permute-start(bf16[16,126,128]{2,1,0:T(8,128)(2,1)} %shard_map.55), channel_id=1, source_target_pairs={{0,16},{16,0},{32,48},{48,32},{64,80},{80,64},{96,112},{112,96},{1... | collective-permute-start | bytes 1548296 | tf_op jit(solution)/shard_map/ppermute | solution.py:101
  104.6 14.2 %collective-permute-start.19 = (bf16[16,126,128]{2,1,0:T(8,128)(2,1)}, bf16[16,126,128]{2,1,0:T(8,128)(2,1)}, u32[]{:S(2)}, u32[]{:S(2)}) collective-permute-start(bf16[16,126,128]{2,1,0:T(8,128)(2,1)} %collective-permute-done.17), channel_id=1, source_target_pairs={{0,16},{16,0},{32,48},{48,32},{64,80},{80,64},{96,112},{112,96},{1... | collective-permute-start | bytes 1548296 | tf_op jit(solution)/shard_map/ppermute | solution.py:103
  115.7 9.6 %collective-permute-start.16 = (f32[504,128]{1,0:T(8,128)S(1)}, f32[504,128]{1,0:T(8,128)S(1)}, u32[]{:S(2)}, u32[]{:S(2)}) collective-permute-start(f32[504,128]{1,0:T(8,128)S(1)} %convolution_bitcast_fusion.2), channel_id=1, source_target_pairs={{0,16},{16,0},{32,48},{48,32},{64,80},{80,64},{96,112},{112,96},{1... | collective-permute-start | bytes 774152 | tf_op jit(solution)/shard_map/ppermute | solution.py:118
  117.5 7.7 %collective-permute-start.18 = (f32[504,128]{1,0:T(8,128)S(1)}, f32[504,128]{1,0:T(8,128)}, u32[]{:S(2)}, u32[]{:S(2)}) collective-permute-start(f32[504,128]{1,0:T(8,128)S(1)} %convolution_bitcast_fusion.1), channel_id=1, source_target_pairs={{0,64},{16,80},{32,96},{48,112},{64,0},{80,16},{96,32},{112,48},{1... | collective-permute-start | bytes 774152 | tf_op jit(solution)/shard_map/ppermute | solution.py:118
  120.6 3.2 %copy-start.2 = (bf16[16,126,128]{2,1,0:T(8,128)(2,1)S(1)}, bf16[16,126,128]{2,1,0:T(8,128)(2,1)}, u32[]{:S(2)}) copy-start(bf16[16,126,128]{2,1,0:T(8,128)(2,1)} %shard_map.55) | copy-start | bytes 1548292
  120.6 10.6 %collective-permute-start.20 = (f32[504,128]{1,0:T(8,128)S(1)}, f32[504,128]{1,0:T(8,128)}, u32[]{:S(2)}, u32[]{:S(2)}) collective-permute-start(f32[504,128]{1,0:T(8,128)S(1)} %convolution_bitcast_fusion), channel_id=1, source_target_pairs={{0,80},{16,64},{32,112},{48,96},{64,16},{80,0},{96,48},{112,32},{1... | collective-permute-start | bytes 774152 | tf_op jit(solution)/shard_map/ppermute | solution.py:118
  125.2 9.1 %copy-start.1 = (f32[64,64,128]{2,0,1:T(8,128)S(1)}, f32[64,64,128]{2,0,1:T(8,128)}, u32[]{:S(2)}) copy-start(f32[64,64,128]{2,0,1:T(8,128)} %fusion.3) | copy-start | bytes 6291460
  125.2 6.0 %copy-start.3 = (f32[504,128]{1,0:T(8,128)}, f32[504,128]{1,0:T(8,128)S(1)}, u32[]{:S(2)}) copy-start(f32[504,128]{1,0:T(8,128)S(1)} %collective-permute-done.16.p1) | copy-start | bytes 774148

commit v7 on v4

--- a/solution.py
+++ b/solution.py
@@ -36,7 +36,7 @@
         o_ref[b] = tmp_ref[b * rows : (b + 1) * rows, :].astype(o_ref.dtype)
 
 
-def spread_kernel(q_ref, p0, p1, p2, p3, o_ref, lad_ref):
+def spread_kernel(q_ref, a_ref, p0, p1, p2, p3, o_ref, lad_ref):
     pieces = (p0, p1, p2, p3)
     part = p0.shape[0]
     q = q_ref[0]
@@ -51,7 +51,7 @@
     occ, width = o_ref.shape[0], o_ref.shape[2]
     col = lax.broadcasted_iota(jnp.int32, (occ, width), 0)
     for i, s in enumerate(row_starts(occ)):
-        o_ref[i] = jnp.where(col > i, lad_ref[7 + s : 7 + s + occ, :], 0.0)
+        o_ref[i] = jnp.where(col > i, lad_ref[7 + s : 7 + s + occ, :] - a_ref[i], 0.0)
 
 
 def vmem_call(kernel, out_shape, scratch, *args, smem=0):
@@ -108,6 +108,8 @@
     def quarter(block):
         return lax.dot_general(w_blocks, block, contract, preferred_element_type=jnp.float32)
 
+    mixed = jnp.einsum("ikp,kj->ijp", pair_amps, fock, preferred_element_type=jnp.float32)
+    mixed_anti = mixed - jnp.transpose(mixed, (1, 0, 2))
     own = quarter(anti)
     back = [
         lax.ppermute(quarter(block), "oi", p)
@@ -118,13 +120,12 @@
         jax.ShapeDtypeStruct((occ, occ, width), jnp.float32),
         [pltpu.VMEM((8 + npairs, width), jnp.float32)],
         q.astype(jnp.int32).reshape(1),
+        mixed_anti,
         own,
         *back,
         smem=1,
     )
-    mixed = jnp.einsum("ikp,kj->ijp", pair_amps, fock, preferred_element_type=jnp.float32)
-    x = upper_part - mixed
-    resid = x - jnp.transpose(x, (1, 0, 2))
+    resid = upper_part - jnp.transpose(upper_part, (1, 0, 2))
     resid = lax.reduce_precision(resid, exponent_bits=8, mantissa_bits=7)
     energies = lax.dynamic_slice_in_dim(eps_pair, me * width, width, 0)
     denom = energies[None, None, :] - eps_occ[:, None, None] - eps_occ[None, :, None]

time: 167 us -> 169 us (1.012)
  other arithmetic: 6.34 us -> 9.26 us
  waiting for transfers between devices: 20.4 us -> 18.5 us
    convert_element_type x1, other arithmetic: 1.38 us -> 3.77 us  [on_device(): upd = (resid / denom).astype(jnp.bfloat16)]
  transfers between devices with their start and end apart: 7 -> 7, of which waited for: 4 -> 3; matrix products, arithmetic and copies ran while one was open for 9% -> 11% of each run, Pallas kernels for 2% -> 2%
where the time goes in v7:
time: 169 us
  blocking collectives  97.7 us (58%)
  waiting for transfers between devices  18.5 us (11%)
  between operations  13.5 us (8%)
  local copies, waits for them, and re-layouts  9.66 us (6%)
  other arithmetic  9.26 us (5%)
  matrix products  7.53 us (4%)
  starting transfers between devices  6.37 us (4%)
  Pallas kernels  6.08 us (4%)
    all_to_all x1, blocking collectives, on_device(): recv = lax.all_to_all(send, ('oi', 'oj'), 0, 0, tiled=True)  55.4 us
    all_to_all x1, blocking collectives, on_device(): out_recv = lax.all_to_all(out_send, ('oi', 'oj'), 0, 0, tiled=True)  42.4 us
    ppermute x1, waiting for transfers between devices, on_device(): from_y = lax.ppermute(anti, 'oi', perms[1])  12.6 us
    pallas_call x2, Pallas kernels, vmem_call(): pl.pallas_call(kernel, out_shape=out_shape, in_specs=[pl.BlockSpec(memory...  6.08 us
    ppermute x3, waiting for transfers between devices, on_device(): lax.ppermute(quarter(block), 'oi', p)  5.8 us
    dot_general x4, matrix products, quarter(): lax.dot_general(w_blocks, block, contract, preferred_element_type=jnp.flo...  5.29 us
    ppermute x3, starting transfers between devices, on_device(): lax.ppermute(quarter(block), 'oi', p)  5.18 us
    convert_element_type x1, other arithmetic, on_device(): upd = (resid / denom).astype(jnp.bfloat16)  3.77 us
  transfers between devices with their start and end apart: 7, of which 3 were waited for; matrix products, arithmetic and copies ran while one was open for 11% of the time, Pallas kernels for 2%

profile of v7, /device:TPU:1, one launch (start us, length us, event | category | flops | bytes accessed | tf_op | source)
XLA Modules:
  0.0 168.6 jit_solution(14288743145928617310)
XLA Ops:
  6.5 0.0 copy-start
  6.5 0.0 all-gather.4.cloned.1.call-start
  6.5 1.0 copy-done
  7.6 0.7 dynamic-slice_bitcast_fusion
  8.2 0.0 all-gather.4.cloned.1.call-update
  8.3 2.1 %reshape.51 = bf16[4,4,256,128]{3,2,1,0:T(8,128)(2,1)S(1)} reshape(bf16[4,4,32768]{2,1,0:T(4,128)(2,1)} %param.5) | data formatting | bytes 2097152 | tf_op jit(solution)/shard_map/reshape | solution.py:81
  10.4 0.8 copy.27
  11.2 55.4 %all_to_all.10 = bf16[256,4,4,128]{3,2,1,0:T(4,128)(2,1)S(1)} all-to-all(bf16[256,4,4,128]{3,2,1,0:T(4,128)(2,1)S(1)} %copy.27), channel_id=1, replica_groups=mesh['oi'=16,'oj'=16] {'oi','oj'}, dimensions={0} | all-to-all | bytes 2097152 | tf_op jit(solution)/shard_map/all_to_all | solution.py:82
  66.6 0.3 copy.28
  66.9 0.8 copy.29
  67.7 0.2 convert_element_type.12
  67.9 2.6 %bitcast_subtract_fusion.1.d_ref = f32[64,64,128]{2,1,0:T(8,128)} fusion(f32[64,64,128]{2,0,1:T(8,128)S(1)} %convert_element_type.12), kind=kLoop, calls=%fused_computation.4 | loop fusion | flops 524288 | bytes 4194304 | tf_op jit(solution)/shard_map/sub | solution.py:93
  70.5 0.0 copy-start.8
  70.5 0.0 copy-start.7
  70.5 2.5 %shard_map.55 = bf16[16,126,128]{2,1,0:T(8,128)(2,1)} custom-call(f32[64,64,128]{2,1,0:T(8,128)} %bitcast_subtract_fusion.1.d_ref), custom_call_target="tpu_custom_call" | custom-call | tf_op jit(solution)/shard_map/pallas_call | solution.py:59
  73.1 0.0 collective-permute-start.2
  73.1 0.8 dynamic_slice.7
  73.8 12.6 %collective-permute-done.2 = bf16[16,126,128]{2,1,0:T(8,128)(2,1)S(1)} collective-permute-done((bf16[16,126,128]{2,1,0:T(8,128)(2,1)}, bf16[16,126,128]{2,1,0:T(8,128)(2,1)S(1)}, u32[]{:S(2)}, u32[]{:S(2)}) %collective-permute-start.2) | collective-permute-done | bytes 516128 | tf_op jit(solution)/shard_map/ppermute | solution.py:102
  86.5 1.2 collective-permute-start.4
  87.6 0.0 copy-done.8
  87.6 0.1 broadcast_subtract_fusion
  87.7 0.0 collective-permute-start
  87.7 0.0 copy-done.7
  87.8 2.2 %fusion.3 = f32[64,64,128]{2,0,1:T(8,128)} fusion(bf16[64,64,128]{2,0,1:T(8,128)(2,1)S(1)} %bitcast.50, bf16[64,64]{1,0:T(8,128)(2,1)S(1)} %copy-done.7), kind=kOutput, calls=%fused_computation.11 | convolution fusion | flops 67108864 | bytes 3153920 | tf_op jit(solution)/shard_map/ikp,kj->ijp/dot_general | solution.py:111
  90.0 0.0 collective-permute-done.4
  90.0 0.0 all-gather.4.cloned.1.call-done
  90.0 0.0 copy-start.1
  90.0 2.4 %convolution_bitcast_fusion = f32[504,128]{1,0:T(8,128)S(1)} fusion(bf16[16,126,504]{1,2,0:T(8,128)(2,1)} %all-gather.4.cloned.1.call-done, bf16[16,126,128]{2,1,0:T(8,128)(2,1)S(1)} %collective-permute-done.4), kind=kOutput, calls=%fused_computation.6 | convolution fusion | flops 260112384 | bytes 2806272 | tf_op jit(solution)/shard_map/dot_general | solution.py:109
  92.4 4.2 %collective-permute-start.5 = (f32[504,128]{1,0:T(8,128)S(1)}, f32[504,128]{1,0:T(8,128)S(1)}, u32[]{:S(2)}, u32[]{:S(2)}) collective-permute-start(f32[504,128]{1,0:T(8,128)S(1)} %convolution_bitcast_fusion), channel_id=1, source_target_pairs={{0,80},{16,64},{32,112},{48,96},{64,16},{80,0},{96,48},{112,32},{1... | collective-permute-start | bytes 774152 | tf_op jit(solution)/shard_map/ppermute | solution.py:115
  96.6 0.0 copy-done.1
  96.6 0.7 convolution_bitcast_fusion.1
  97.4 0.0 copy-start.2
  97.4 0.7 collective-permute-start.3
  98.1 0.0 collective-permute-done
  98.1 0.7 convolution_bitcast_fusion.2
  98.8 0.0 copy-start.3
  98.8 0.3 collective-permute-start.1
  99.1 0.0 copy-done.2
  99.1 2.6 %bitcast_subtract_fusion.2.a_ref = f32[64,64,128]{2,1,0:T(8,128)} fusion(f32[64,64,128]{2,0,1:T(8,128)S(1)} %copy-done.2), kind=kLoop, calls=%fused_computation.5 | loop fusion | flops 524288 | bytes 4194304 | tf_op jit(solution)/shard_map/sub | solution.py:112
  101.7 0.0 copy-done.3
  101.7 1.4 convolution_bitcast_fusion.3.p0
  103.1 0.2 collective-permute-done.5.p3
  103.3 0.0 copy-start.4
  103.4 5.6 %collective-permute-done.3.p2 = f32[504,128]{1,0:T(8,128)S(1)} collective-permute-done((f32[504,128]{1,0:T(8,128)S(1)}, f32[504,128]{1,0:T(8,128)S(1)}, u32[]{:S(2)}, u32[]{:S(2)}) %collective-permute-start.3) | collective-permute-done | bytes 258080 | tf_op jit(solution)/shard_map/ppermute | solution.py:115
  108.9 0.0 copy-start.5
  108.9 0.0 collective-permute-done.1.p1
  108.9 0.0 copy-start.6
  108.9 0.0 copy-done.4
  108.9 0.7 copy-done.5
  109.6 0.1 copy-done.6
  109.7 3.5 %shard_map.56 = f32[64,64,128]{2,1,0:T(8,128)} custom-call(s32[1]{0:T(128)} %bitcast.q_ref, f32[64,64,128]{2,1,0:T(8,128)} %bitcast_subtract_fusion.2.a_ref, f32[504,128]{1,0:T(8,128)} %convolution_bitcast_fusion.3.p0, f32[504,128]{1,0:T(8,128)} %copy-done.6, f32[504,128]{1,0:T(8,128)} %copy-done.5, f32[504,128]{1,0:T(8,128)} %copy-done.4), custom_call_target="tpu_custom_call" | custom-call | tf_op jit(solution)/shard_map/pallas_call | solution.py:59
  113.3 3.8 %fusion.2 = bf16[64,64,128]{2,1,0:T(8,128)(2,1)S(1)} fusion(f32[64,64,128]{2,1,0:T(8,128)} %shard_map.56, f32[64]{0:T(128)S(1)} %copy-done.8, f32[64,128]{1,0:T(8,128)S(1)} %broadcast_subtract_fusion), kind=kLoop, calls=%fused_computation.3 | loop fusion | flops 2621440 | bytes 3178752 | tf_op jit(solution)/shard_map/convert_element_type | solution.py:132
  117.0 0.2 copy.35
  117.3 0.8 copy.36
  118.1 42.4 %all_to_all.11 = bf16[256,4,4,128]{3,2,1,0:T(4,128)(2,1)S(1)} all-to-all(bf16[256,4,4,128]{3,2,1,0:T(4,128)(2,1)S(1)} %copy.36), channel_id=1, replica_groups=mesh['oi'=16,'oj'=16] {'oi','oj'}, dimensions={0} | all-to-all | bytes 2097152 | tf_op jit(solution)/shard_map/all_to_all | solution.py:139
  160.4 1.3 copy_bitcast_fusion
Async XLA Ops:
  6.5 1.0 copy-start
  6.5 83.5 %all-gather.4.cloned.1.call-start = ((), (), s32[]{:S(2)}) async-start(), calls=%async_computation.2 | async-start | bytes 2193408 | tf_op jit(solution)/shard_map/all_gather | solution.py:105
  70.5 17.1 %copy-start.8 = (f32[64]{0:T(128)S(1)}, f32[64]{0:T(128)}, u32[]{:S(2)}) copy-start(f32[64]{0:T(128)} %param.8) | copy-start | bytes 772
  70.5 17.2 %copy-start.7 = (bf16[64,64]{1,0:T(8,128)(2,1)S(1)}, bf16[64,64]{1,0:T(8,128)(2,1)}, u32[]{:S(2)}) copy-start(bf16[64,64]{1,0:T(8,128)(2,1)} %param.7) | copy-start | bytes 24580
  73.1 13.4 %collective-permute-start.2 = (bf16[16,126,128]{2,1,0:T(8,128)(2,1)}, bf16[16,126,128]{2,1,0:T(8,128)(2,1)S(1)}, u32[]{:S(2)}, u32[]{:S(2)}) collective-permute-start(bf16[16,126,128]{2,1,0:T(8,128)(2,1)} %shard_map.55), channel_id=1, source_target_pairs={{0,64},{16,80},{32,96},{48,112},{64,0},{80,16},{96,32},{112,48},{1... | collective-permute-start | bytes 1548296 | tf_op jit(solution)/shard_map/ppermute | solution.py:102
  86.5 3.5 %collective-permute-start.4 = (bf16[16,126,128]{2,1,0:T(8,128)(2,1)S(1)}, bf16[16,126,128]{2,1,0:T(8,128)(2,1)S(1)}, u32[]{:S(2)}, u32[]{:S(2)}) collective-permute-start(bf16[16,126,128]{2,1,0:T(8,128)(2,1)S(1)} %collective-permute-done.2), channel_id=1, source_target_pairs={{0,16},{16,0},{32,48},{48,32},{64,80},{80,64},{96,112},{112,96},{1... | collective-permute-start | bytes 1548296 | tf_op jit(solution)/shard_map/ppermute | solution.py:103
  87.7 10.4 %collective-permute-start = (bf16[16,126,128]{2,1,0:T(8,128)(2,1)}, bf16[16,126,128]{2,1,0:T(8,128)(2,1)S(1)}, u32[]{:S(2)}, u32[]{:S(2)}) collective-permute-start(bf16[16,126,128]{2,1,0:T(8,128)(2,1)} %shard_map.55), channel_id=1, source_target_pairs={{0,16},{16,0},{32,48},{48,32},{64,80},{80,64},{96,112},{112,96},{1... | collective-permute-start | bytes 1548296 | tf_op jit(solution)/shard_map/ppermute | solution.py:101
  90.0 6.6 %copy-start.1 = (bf16[16,126,504]{1,2,0:T(8,128)(2,1)S(1)}, bf16[16,126,504]{1,2,0:T(8,128)(2,1)}, u32[]{:S(2)}) copy-start(bf16[16,126,504]{1,2,0:T(8,128)(2,1)} %all-gather.4.cloned.1.call-done) | copy-start | bytes 6096388
  92.4 10.9 %collective-permute-start.5 = (f32[504,128]{1,0:T(8,128)S(1)}, f32[504,128]{1,0:T(8,128)S(1)}, u32[]{:S(2)}, u32[]{:S(2)}) collective-permute-start(f32[504,128]{1,0:T(8,128)S(1)} %convolution_bitcast_fusion), channel_id=1, source_target_pairs={{0,80},{16,64},{32,112},{48,96},{64,16},{80,0},{96,48},{112,32},{1... | collective-permute-start | bytes 774152 | tf_op jit(solution)/shard_map/ppermute | solution.py:115
  97.4 1.8 %copy-start.2 = (f32[64,64,128]{2,0,1:T(8,128)S(1)}, f32[64,64,128]{2,0,1:T(8,128)}, u32[]{:S(2)}) copy-start(f32[64,64,128]{2,0,1:T(8,128)} %fusion.3) | copy-start | bytes 6291460
  97.4 11.6 %collective-permute-start.3 = (f32[504,128]{1,0:T(8,128)S(1)}, f32[504,128]{1,0:T(8,128)S(1)}, u32[]{:S(2)}, u32[]{:S(2)}) collective-permute-start(f32[504,128]{1,0:T(8,128)S(1)} %convolution_bitcast_fusion.1), channel_id=1, source_target_pairs={{0,64},{16,80},{32,96},{48,112},{64,0},{80,16},{96,32},{112,48},{1... | collective-permute-start | bytes 774152 | tf_op jit(solution)/shard_map/ppermute | solution.py:115
  98.8 2.9 %copy-start.3 = (bf16[16,126,128]{2,1,0:T(8,128)(2,1)S(1)}, bf16[16,126,128]{2,1,0:T(8,128)(2,1)}, u32[]{:S(2)}) copy-start(bf16[16,126,128]{2,1,0:T(8,128)(2,1)} %shard_map.55) | copy-start | bytes 1548292
  98.8 10.1 %collective-permute-start.1 = (f32[504,128]{1,0:T(8,128)S(1)}, f32[504,128]{1,0:T(8,128)S(1)}, u32[]{:S(2)}, u32[]{:S(2)}) collective-permute-start(f32[504,128]{1,0:T(8,128)S(1)} %convolution_bitcast_fusion.2), channel_id=1, source_target_pairs={{0,16},{16,0},{32,48},{48,32},{64,80},{80,64},{96,112},{112,96},{1... | collective-permute-start | bytes 774152 | tf_op jit(solution)/shard_map/ppermute | solution.py:115
  103.3 5.6 %copy-start.4 = (f32[504,128]{1,0:T(8,128)}, f32[504,128]{1,0:T(8,128)S(1)}, u32[]{:S(2)}) copy-start(f32[504,128]{1,0:T(8,128)S(1)} %collective-permute-done.5.p3) | copy-start | bytes 774148
  108.9 0.7 copy-start.5
  108.9 0.8 copy-start.6
Sparse Core Ops, SparseCore 0:
  9.1 76.5 all-gather.3

commit v8 on v4

--- a/solution.py
+++ b/solution.py
@@ -109,9 +109,9 @@
         return lax.dot_general(w_blocks, block, contract, preferred_element_type=jnp.float32)
 
     own = quarter(anti)
-    back = [
-        lax.ppermute(quarter(block), "oi", p)
-        for block, p in zip((from_core, from_y, from_diag), perms)
+    back = [lax.ppermute(quarter(from_core), "oi", perms[0])] + [
+        lax.ppermute(quarter(block).astype(jnp.bfloat16), "oi", p).astype(jnp.float32)
+        for block, p in zip((from_y, from_diag), perms[1:])
     ]
     upper_part = vmem_call(
         spread_kernel,

time: 167 us -> 163 us (0.976)
  waiting for transfers between devices: 20.4 us -> 14.4 us
    ppermute x3, waiting for transfers between devices: 6.25 us -> 1.52 us  [the longest x2 1.52 us: on_device(): lax.ppermute(quarter(block).astype(jnp.bfloat16), 'oi', p)]
  transfers between devices with their start and end apart: 7 -> 7, of which waited for: 4 -> 2; matrix products, arithmetic and copies ran while one was open for 9% -> 10% of each run, Pallas kernels for 2% -> 2%
where the time goes in v8:
time: 163 us
  blocking collectives  98.5 us (60%)
  waiting for transfers between devices  14.4 us (9%)
  between operations  13.5 us (8%)
  local copies, waits for them, and re-layouts  9.55 us (6%)
  other arithmetic  7.83 us (5%)
  matrix products  7.54 us (5%)
  starting transfers between devices  6.11 us (4%)
  Pallas kernels  5.45 us (3%)
    all_to_all x1, blocking collectives, on_device(): recv = lax.all_to_all(send, ('oi', 'oj'), 0, 0, tiled=True)  55.4 us
    all_to_all x1, blocking collectives, on_device(): out_recv = lax.all_to_all(out_send, ('oi', 'oj'), 0, 0, tiled=True)  43.1 us
    ppermute x1, waiting for transfers between devices, on_device(): from_y = lax.ppermute(anti, 'oi', perms[1])  12.8 us
    pallas_call x2, Pallas kernels, vmem_call(): pl.pallas_call(kernel, out_shape=out_shape, in_specs=[pl.BlockSpec(memory...  5.45 us
    dot_general x4, matrix products, quarter(): lax.dot_general(w_blocks, block, contract, preferred_element_type=jnp.flo...  5.31 us
    ppermute x2, starting transfers between devices, on_device(): lax.ppermute(quarter(block).astype(jnp.bfloat16), 'oi', p)  5 us
  transfers between devices with their start and end apart: 7, of which 2 were waited for; matrix products, arithmetic and copies ran while one was open for 10% of the time, Pallas kernels for 2%

profile of v8, /device:TPU:1, one launch (start us, length us, event | category | flops | bytes accessed | tf_op | source)
XLA Modules:
  0.0 162.8 jit_solution(6106031354190944881)
XLA Ops:
  6.5 0.0 copy-start
  6.5 0.0 all-gather.4.cloned.1.call-start
  6.5 1.0 copy-done
  7.6 0.7 dynamic-slice_bitcast_fusion
  8.2 0.0 all-gather.4.cloned.1.call-update
  8.2 2.1 %reshape.51 = bf16[4,4,256,128]{3,2,1,0:T(8,128)(2,1)S(1)} reshape(bf16[4,4,32768]{2,1,0:T(4,128)(2,1)} %param.5) | data formatting | bytes 2097152 | tf_op jit(solution)/shard_map/reshape | solution.py:81
  10.4 0.8 copy.24
  11.2 55.4 %all_to_all.10 = bf16[256,4,4,128]{3,2,1,0:T(4,128)(2,1)S(1)} all-to-all(bf16[256,4,4,128]{3,2,1,0:T(4,128)(2,1)S(1)} %copy.24), channel_id=1, replica_groups=mesh['oi'=16,'oj'=16] {'oi','oj'}, dimensions={0} | all-to-all | bytes 2097152 | tf_op jit(solution)/shard_map/all_to_all | solution.py:82
  66.6 0.3 copy.25
  66.9 0.8 copy.26
  67.7 0.2 convert_element_type.24
  67.9 2.6 %bitcast_subtract_fusion.2.d_ref = f32[64,64,128]{2,1,0:T(8,128)} fusion(f32[64,64,128]{2,0,1:T(8,128)S(1)} %convert_element_type.24), kind=kLoop, calls=%fused_computation.5 | loop fusion | flops 524288 | bytes 4194304 | tf_op jit(solution)/shard_map/sub | solution.py:93
  70.5 0.0 copy-start.6
  70.5 0.0 copy-start.5
  70.5 2.5 %shard_map.55 = bf16[16,126,128]{2,1,0:T(8,128)(2,1)} custom-call(f32[64,64,128]{2,1,0:T(8,128)} %bitcast_subtract_fusion.2.d_ref), custom_call_target="tpu_custom_call" | custom-call | tf_op jit(solution)/shard_map/pallas_call | solution.py:59
  73.1 0.0 collective-permute-start.2
  73.1 0.8 dynamic_slice.7
  73.8 12.8 %collective-permute-done.2 = bf16[16,126,128]{2,1,0:T(8,128)(2,1)S(1)} collective-permute-done((bf16[16,126,128]{2,1,0:T(8,128)(2,1)}, bf16[16,126,128]{2,1,0:T(8,128)(2,1)S(1)}, u32[]{:S(2)}, u32[]{:S(2)}) %collective-permute-start.2) | collective-permute-done | bytes 516128 | tf_op jit(solution)/shard_map/ppermute | solution.py:102
  86.6 1.0 collective-permute-start.4
  87.6 0.0 copy-done.6
  87.6 0.1 broadcast_subtract_fusion
  87.7 0.0 collective-permute-start
  87.7 0.0 copy-done.5
  87.8 2.2 %fusion.5 = f32[64,64,128]{2,0,1:T(8,128)} fusion(bf16[64,64,128]{2,0,1:T(8,128)(2,1)S(1)} %bitcast.54, bf16[64,64]{1,0:T(8,128)(2,1)S(1)} %copy-done.5), kind=kOutput, calls=%fused_computation.13 | convolution fusion | flops 67108864 | bytes 3153920 | tf_op jit(solution)/shard_map/ikp,kj->ijp/dot_general | solution.py:125
  90.0 0.0 collective-permute-done.4
  90.0 0.0 all-gather.4.cloned.1.call-done
  90.0 0.0 copy-start.1
  90.0 2.4 %fusion.4 = bf16[504,128]{1,0:T(8,128)(2,1)S(1)} fusion(bf16[16,126,504]{1,2,0:T(8,128)(2,1)} %all-gather.4.cloned.1.call-done, bf16[16,126,128]{2,1,0:T(8,128)(2,1)S(1)} %collective-permute-done.4), kind=kOutput, calls=%fused_computation.11 | convolution fusion | flops 260176896 | bytes 2677248 | tf_op jit(solution)/shard_map/dot_general | solution.py:109
  92.4 0.0 copy-start.3
  92.4 3.9 %collective-permute-start.5 = (bf16[504,128]{1,0:T(8,128)(2,1)S(1)}, bf16[504,128]{1,0:T(8,128)(2,1)S(1)}, u32[]{:S(2)}, u32[]{:S(2)}) collective-permute-start(bf16[504,128]{1,0:T(8,128)(2,1)S(1)} %fusion.4), channel_id=1, source_target_pairs={{0,80},{16,64},{32,112},{48,96},{64,16},{80,0},{96,48},{112,32},{1... | collective-permute-start | bytes 387080 | tf_op jit(solution)/shard_map/ppermute | solution.py:113
  96.4 0.0 collective-permute-done
  96.4 0.0 copy-done.1
  96.4 0.7 convolution_bitcast_fusion.2
  97.1 0.1 collective-permute-start.1
  97.2 0.7 fusion.3
  97.9 1.1 collective-permute-start.3
  99.0 0.0 copy-done.3
  99.0 1.4 convolution_bitcast_fusion.3.p0
  100.4 0.0 copy-start.2
  100.4 0.0 collective-permute-done.5
  100.5 0.7 convert_element_type.30.p3
  101.2 1.5 collective-permute-done.3
  102.7 0.7 convert_element_type.28.p2
  103.4 0.0 collective-permute-done.1.p1
  103.4 0.0 copy-start.4
  103.4 0.7 copy-done.4
  104.1 2.9 %shard_map.56 = f32[64,64,128]{2,1,0:T(8,128)} custom-call(s32[1]{0:T(128)} %bitcast.q_ref, f32[504,128]{1,0:T(8,128)} %convolution_bitcast_fusion.3.p0, f32[504,128]{1,0:T(8,128)} %copy-done.4, f32[504,128]{1,0:T(8,128)} %convert_element_type.28.p2, f32[504,128]{1,0:T(8,128)} %convert_element_type.30.p3), custom_call_target="tpu_custom_call" | custom-call | tf_op jit(solution)/shard_map/pallas_call | solution.py:59
  107.0 0.0 copy-done.2
  107.0 2.1 %bitcast_subtract_fusion.1 = f32[64,64,128]{2,1,0:T(8,128)S(1)} fusion(f32[64,64,128]{2,1,0:T(8,128)} %shard_map.56, f32[64,64,128]{2,0,1:T(8,128)S(1)} %copy-done.2), kind=kLoop, calls=%fused_computation.4 | loop fusion | flops 524288 | bytes 6291456 | tf_op jit(solution)/shard_map/sub | solution.py:126
  109.1 1.4 fusion.2
  110.5 0.2 copy.31
  110.7 0.8 copy.32
  111.5 43.1 %all_to_all.11 = bf16[256,4,4,128]{3,2,1,0:T(4,128)(2,1)S(1)} all-to-all(bf16[256,4,4,128]{3,2,1,0:T(4,128)(2,1)S(1)} %copy.32), channel_id=1, replica_groups=mesh['oi'=16,'oj'=16] {'oi','oj'}, dimensions={0} | all-to-all | bytes 2097152 | tf_op jit(solution)/shard_map/all_to_all | solution.py:138
  154.7 1.3 copy_bitcast_fusion
Async XLA Ops:
  6.5 1.0 copy-start
  6.5 83.4 %all-gather.4.cloned.1.call-start = ((), (), s32[]{:S(2)}) async-start(), calls=%async_computation.2 | async-start | bytes 2193408 | tf_op jit(solution)/shard_map/all_gather | solution.py:105
  70.5 17.1 %copy-start.6 = (f32[64]{0:T(128)S(1)}, f32[64]{0:T(128)}, u32[]{:S(2)}) copy-start(f32[64]{0:T(128)} %param.8) | copy-start | bytes 772
  70.5 17.2 %copy-start.5 = (bf16[64,64]{1,0:T(8,128)(2,1)S(1)}, bf16[64,64]{1,0:T(8,128)(2,1)}, u32[]{:S(2)}) copy-start(bf16[64,64]{1,0:T(8,128)(2,1)} %param.7) | copy-start | bytes 24580
  73.1 13.6 %collective-permute-start.2 = (bf16[16,126,128]{2,1,0:T(8,128)(2,1)}, bf16[16,126,128]{2,1,0:T(8,128)(2,1)S(1)}, u32[]{:S(2)}, u32[]{:S(2)}) collective-permute-start(bf16[16,126,128]{2,1,0:T(8,128)(2,1)} %shard_map.55), channel_id=1, source_target_pairs={{0,64},{16,80},{32,96},{48,112},{64,0},{80,16},{96,32},{112,48},{1... | collective-permute-start | bytes 1548296 | tf_op jit(solution)/shard_map/ppermute | solution.py:102
  86.6 3.3 %collective-permute-start.4 = (bf16[16,126,128]{2,1,0:T(8,128)(2,1)S(1)}, bf16[16,126,128]{2,1,0:T(8,128)(2,1)S(1)}, u32[]{:S(2)}, u32[]{:S(2)}) collective-permute-start(bf16[16,126,128]{2,1,0:T(8,128)(2,1)S(1)} %collective-permute-done.2), channel_id=1, source_target_pairs={{0,16},{16,0},{32,48},{48,32},{64,80},{80,64},{96,112},{112,96},{1... | collective-permute-start | bytes 1548296 | tf_op jit(solution)/shard_map/ppermute | solution.py:103
  87.7 8.7 %collective-permute-start = (bf16[16,126,128]{2,1,0:T(8,128)(2,1)}, bf16[16,126,128]{2,1,0:T(8,128)(2,1)S(1)}, u32[]{:S(2)}, u32[]{:S(2)}) collective-permute-start(bf16[16,126,128]{2,1,0:T(8,128)(2,1)} %shard_map.55), channel_id=1, source_target_pairs={{0,16},{16,0},{32,48},{48,32},{64,80},{80,64},{96,112},{112,96},{1... | collective-permute-start | bytes 1548296 | tf_op jit(solution)/shard_map/ppermute | solution.py:101
  90.0 6.4 %copy-start.1 = (bf16[16,126,504]{1,2,0:T(8,128)(2,1)S(1)}, bf16[16,126,504]{1,2,0:T(8,128)(2,1)}, u32[]{:S(2)}) copy-start(bf16[16,126,504]{1,2,0:T(8,128)(2,1)} %all-gather.4.cloned.1.call-done) | copy-start | bytes 6096388
  92.4 6.6 %copy-start.3 = (bf16[16,126,128]{2,1,0:T(8,128)(2,1)S(1)}, bf16[16,126,128]{2,1,0:T(8,128)(2,1)}, u32[]{:S(2)}) copy-start(bf16[16,126,128]{2,1,0:T(8,128)(2,1)} %shard_map.55) | copy-start | bytes 1548292
  92.4 8.0 %collective-permute-start.5 = (bf16[504,128]{1,0:T(8,128)(2,1)S(1)}, bf16[504,128]{1,0:T(8,128)(2,1)S(1)}, u32[]{:S(2)}, u32[]{:S(2)}) collective-permute-start(bf16[504,128]{1,0:T(8,128)(2,1)S(1)} %fusion.4), channel_id=1, source_target_pairs={{0,80},{16,64},{32,112},{48,96},{64,16},{80,0},{96,48},{112,32},{1... | collective-permute-start | bytes 387080 | tf_op jit(solution)/shard_map/ppermute | solution.py:113
  97.1 6.3 %collective-permute-start.1 = (f32[504,128]{1,0:T(8,128)S(1)}, f32[504,128]{1,0:T(8,128)S(1)}, u32[]{:S(2)}, u32[]{:S(2)}) collective-permute-start(f32[504,128]{1,0:T(8,128)S(1)} %convolution_bitcast_fusion.2), channel_id=1, source_target_pairs={{0,16},{16,0},{32,48},{48,32},{64,80},{80,64},{96,112},{112,96},{1... | collective-permute-start | bytes 774152 | tf_op jit(solution)/shard_map/ppermute | solution.py:112
  97.9 4.8 %collective-permute-start.3 = (bf16[504,128]{1,0:T(8,128)(2,1)S(1)}, bf16[504,128]{1,0:T(8,128)(2,1)S(1)}, u32[]{:S(2)}, u32[]{:S(2)}) collective-permute-start(bf16[504,128]{1,0:T(8,128)(2,1)S(1)} %fusion.3), channel_id=1, source_target_pairs={{0,64},{16,80},{32,96},{48,112},{64,0},{80,16},{96,32},{112,48},{1... | collective-permute-start | bytes 387080 | tf_op jit(solution)/shard_map/ppermute | solution.py:113
  100.4 6.6 %copy-start.2 = (f32[64,64,128]{2,0,1:T(8,128)S(1)}, f32[64,64,128]{2,0,1:T(8,128)}, u32[]{:S(2)}) copy-start(f32[64,64,128]{2,0,1:T(8,128)} %fusion.5) | copy-start | bytes 6291460
  103.4 0.7 copy-start.4
Sparse Core Ops, SparseCore 0:
  9.1 77.2 all-gather.3

commit v9 on v8

--- a/solution.py
+++ b/solution.py
@@ -46,7 +46,7 @@
 
             @pl.when(jnp.bitwise_xor(q, r) == n)
             def _():
-                lad_ref[8 + r * part : 8 + (r + 1) * part, :] = pieces[n][...]
+                lad_ref[8 + r * part : 8 + (r + 1) * part, :] = pieces[n][...].astype(lad_ref.dtype)
 
     occ, width = o_ref.shape[0], o_ref.shape[2]
     col = lax.broadcasted_iota(jnp.int32, (occ, width), 0)
@@ -110,7 +110,7 @@
 
     own = quarter(anti)
     back = [lax.ppermute(quarter(from_core), "oi", perms[0])] + [
-        lax.ppermute(quarter(block).astype(jnp.bfloat16), "oi", p).astype(jnp.float32)
+        lax.ppermute(quarter(block).astype(jnp.bfloat16), "oi", p)
         for block, p in zip((from_y, from_diag), perms[1:])
     ]
     upper_part = vmem_call(

time: 163 us -> 163 us (level)
  transfers between devices with their start and end apart: 7 -> 7, of which waited for: 2 -> 2; matrix products, arithmetic and copies ran while one was open for 10% -> 9% of each run, Pallas kernels for 2% -> 2%
where the time goes in v9:
time: 163 us; the launch traced here: 162 us
  blocking collectives  98.4 us (60%)
  waiting for transfers between devices  15.1 us (9%)
  between operations  13.5 us (8%)
  local copies, waits for them, and re-layouts  9.62 us (6%)
  matrix products  7.56 us (5%)
  starting transfers between devices  6.37 us (4%)
  other arithmetic  6.37 us (4%)
  Pallas kernels  5.36 us (3%)
    all_to_all x1, blocking collectives, on_device(): recv = lax.all_to_all(send, ('oi', 'oj'), 0, 0, tiled=True)  55.4 us
    all_to_all x1, blocking collectives, on_device(): out_recv = lax.all_to_all(out_send, ('oi', 'oj'), 0, 0, tiled=True)  43.1 us
    ppermute x1, waiting for transfers between devices, on_device(): from_y = lax.ppermute(anti, 'oi', perms[1])  12.6 us
    pallas_call x2, Pallas kernels, vmem_call(): pl.pallas_call(kernel, out_shape=out_shape, in_specs=[pl.BlockSpec(memory...  5.36 us
    dot_general x4, matrix products, quarter(): lax.dot_general(w_blocks, block, contract, preferred_element_type=jnp.flo...  5.33 us
    ppermute x2, starting transfers between devices, on_device(): lax.ppermute(quarter(block).astype(jnp.bfloat16), 'oi', p)  5.09 us
  transfers between devices with their start and end apart: 7, of which 2 were waited for; matrix products, arithmetic and copies ran while one was open for 9% of the time, Pallas kernels for 2%

profile of v9, /device:TPU:1, one launch (start us, length us, event | category | flops | bytes accessed | tf_op | source)
XLA Modules:
  0.0 162.3 jit_solution(17324268491212467677)
XLA Ops:
  6.5 0.0 copy-start
  6.5 0.0 all-gather.4.cloned.1.call-start
  6.5 1.0 copy-done
  7.6 0.7 dynamic-slice_bitcast_fusion
  8.2 0.0 all-gather.4.cloned.1.call-update
  8.3 2.1 %reshape.51 = bf16[4,4,256,128]{3,2,1,0:T(8,128)(2,1)S(1)} reshape(bf16[4,4,32768]{2,1,0:T(4,128)(2,1)} %param.5) | data formatting | bytes 2097152 | tf_op jit(solution)/shard_map/reshape | solution.py:81
  10.4 0.8 copy.24
  11.2 55.4 %all_to_all.10 = bf16[256,4,4,128]{3,2,1,0:T(4,128)(2,1)S(1)} all-to-all(bf16[256,4,4,128]{3,2,1,0:T(4,128)(2,1)S(1)} %copy.24), channel_id=1, replica_groups=mesh['oi'=16,'oj'=16] {'oi','oj'}, dimensions={0} | all-to-all | bytes 2097152 | tf_op jit(solution)/shard_map/all_to_all | solution.py:82
  66.6 0.3 copy.25
  66.9 0.8 copy.26
  67.7 0.2 convert_element_type.18
  67.9 2.6 %bitcast_subtract_fusion.2.d_ref = f32[64,64,128]{2,1,0:T(8,128)} fusion(f32[64,64,128]{2,0,1:T(8,128)S(1)} %convert_element_type.18), kind=kLoop, calls=%fused_computation.5 | loop fusion | flops 524288 | bytes 4194304 | tf_op jit(solution)/shard_map/sub | solution.py:93
  70.5 0.0 copy-start.8
  70.5 0.0 copy-start.7
  70.5 2.5 %shard_map.55 = bf16[16,126,128]{2,1,0:T(8,128)(2,1)} custom-call(f32[64,64,128]{2,1,0:T(8,128)} %bitcast_subtract_fusion.2.d_ref), custom_call_target="tpu_custom_call" | custom-call | tf_op jit(solution)/shard_map/pallas_call | solution.py:59
  73.1 0.0 collective-permute-start.2
  73.1 0.8 dynamic_slice.7
  73.8 12.6 %collective-permute-done.2 = bf16[16,126,128]{2,1,0:T(8,128)(2,1)S(1)} collective-permute-done((bf16[16,126,128]{2,1,0:T(8,128)(2,1)}, bf16[16,126,128]{2,1,0:T(8,128)(2,1)S(1)}, u32[]{:S(2)}, u32[]{:S(2)}) %collective-permute-start.2) | collective-permute-done | bytes 516128 | tf_op jit(solution)/shard_map/ppermute | solution.py:102
  86.5 1.2 collective-permute-start.4
  87.6 0.0 copy-done.8
  87.6 0.1 broadcast_subtract_fusion
  87.7 0.0 collective-permute-start
  87.7 0.0 copy-done.7
  87.8 2.2 %fusion.5 = f32[64,64,128]{2,0,1:T(8,128)} fusion(bf16[64,64,128]{2,0,1:T(8,128)(2,1)S(1)} %bitcast.54, bf16[64,64]{1,0:T(8,128)(2,1)S(1)} %copy-done.7), kind=kOutput, calls=%fused_computation.13 | convolution fusion | flops 67108864 | bytes 3153920 | tf_op jit(solution)/shard_map/ikp,kj->ijp/dot_general | solution.py:125
  90.0 0.0 collective-permute-done.4
  90.0 0.0 all-gather.4.cloned.1.call-done
  90.0 0.0 copy-start.1
  90.0 2.4 %fusion.4 = bf16[504,128]{1,0:T(8,128)(2,1)S(1)} fusion(bf16[16,126,504]{1,2,0:T(8,128)(2,1)} %all-gather.4.cloned.1.call-done, bf16[16,126,128]{2,1,0:T(8,128)(2,1)S(1)} %collective-permute-done.4), kind=kOutput, calls=%fused_computation.11 | convolution fusion | flops 260176896 | bytes 2677248 | tf_op jit(solution)/shard_map/dot_general | solution.py:109
  92.4 0.0 copy-start.3
  92.5 4.2 %collective-permute-start.5 = (bf16[504,128]{1,0:T(8,128)(2,1)S(1)}, bf16[504,128]{1,0:T(8,128)(2,1)S(1)}, u32[]{:S(2)}, u32[]{:S(2)}) collective-permute-start(bf16[504,128]{1,0:T(8,128)(2,1)S(1)} %fusion.4), channel_id=1, source_target_pairs={{0,80},{16,64},{32,112},{48,96},{64,16},{80,0},{96,48},{112,32},{1... | collective-permute-start | bytes 387080 | tf_op jit(solution)/shard_map/ppermute | solution.py:113
  96.6 0.0 collective-permute-done
  96.6 0.0 copy-done.1
  96.6 0.7 convolution_bitcast_fusion.2
  97.4 0.1 collective-permute-start.1
  97.5 0.7 fusion.3
  98.2 0.9 collective-permute-start.3
  99.1 0.0 copy-done.3
  99.1 1.4 convolution_bitcast_fusion.3.p0
  100.6 0.0 copy-start.2
  100.6 0.0 collective-permute-done.5.p3
  100.6 0.0 copy-start.5
  100.6 2.4 %collective-permute-done.3.p2 = bf16[504,128]{1,0:T(8,128)(2,1)S(1)} collective-permute-done((bf16[504,128]{1,0:T(8,128)(2,1)S(1)}, bf16[504,128]{1,0:T(8,128)(2,1)S(1)}, u32[]{:S(2)}, u32[]{:S(2)}) %collective-permute-start.3) | collective-permute-done | bytes 129056 | tf_op jit(solution)/shard_map/ppermute | solution.py:113
  103.0 0.0 copy-start.6
  103.0 0.0 collective-permute-done.1.p1
  103.0 0.0 copy-start.4
  103.0 0.0 copy-done.5
  103.0 0.6 copy-done.6
  103.6 0.1 copy-done.4
  103.8 2.8 %shard_map.56 = f32[64,64,128]{2,1,0:T(8,128)} custom-call(s32[1]{0:T(128)} %bitcast.q_ref, f32[504,128]{1,0:T(8,128)} %convolution_bitcast_fusion.3.p0, f32[504,128]{1,0:T(8,128)} %copy-done.4, bf16[504,128]{1,0:T(8,128)(2,1)} %copy-done.6, bf16[504,128]{1,0:T(8,128)(2,1)} %copy-done.5), custom_call_target="tpu_custom_call" | custom-call | tf_op jit(solution)/shard_map/pallas_call | solution.py:59
  106.6 0.0 copy-done.2
  106.6 2.1 %bitcast_subtract_fusion.1 = f32[64,64,128]{2,1,0:T(8,128)S(1)} fusion(f32[64,64,128]{2,1,0:T(8,128)} %shard_map.56, f32[64,64,128]{2,0,1:T(8,128)S(1)} %copy-done.2), kind=kLoop, calls=%fused_computation.4 | loop fusion | flops 524288 | bytes 6291456 | tf_op jit(solution)/shard_map/sub | solution.py:126
  108.6 1.4 fusion.2
  110.0 0.2 copy.31
  110.2 0.8 copy.32
  111.1 43.1 %all_to_all.11 = bf16[256,4,4,128]{3,2,1,0:T(4,128)(2,1)S(1)} all-to-all(bf16[256,4,4,128]{3,2,1,0:T(4,128)(2,1)S(1)} %copy.32), channel_id=1, replica_groups=mesh['oi'=16,'oj'=16] {'oi','oj'}, dimensions={0} | all-to-all | bytes 2097152 | tf_op jit(solution)/shard_map/all_to_all | solution.py:138
  154.1 1.3 copy_bitcast_fusion
Async XLA Ops:
  6.5 1.0 copy-start
  6.5 83.5 %all-gather.4.cloned.1.call-start = ((), (), s32[]{:S(2)}) async-start(), calls=%async_computation.2 | async-start | bytes 2193408 | tf_op jit(solution)/shard_map/all_gather | solution.py:105
  70.5 17.1 %copy-start.8 = (f32[64]{0:T(128)S(1)}, f32[64]{0:T(128)}, u32[]{:S(2)}) copy-start(f32[64]{0:T(128)} %param.8) | copy-start | bytes 772
  70.5 17.2 %copy-start.7 = (bf16[64,64]{1,0:T(8,128)(2,1)S(1)}, bf16[64,64]{1,0:T(8,128)(2,1)}, u32[]{:S(2)}) copy-start(bf16[64,64]{1,0:T(8,128)(2,1)} %param.7) | copy-start | bytes 24580
  73.1 13.4 %collective-permute-start.2 = (bf16[16,126,128]{2,1,0:T(8,128)(2,1)}, bf16[16,126,128]{2,1,0:T(8,128)(2,1)S(1)}, u32[]{:S(2)}, u32[]{:S(2)}) collective-permute-start(bf16[16,126,128]{2,1,0:T(8,128)(2,1)} %shard_map.55), channel_id=1, source_target_pairs={{0,64},{16,80},{32,96},{48,112},{64,0},{80,16},{96,32},{112,48},{1... | collective-permute-start | bytes 1548296 | tf_op jit(solution)/shard_map/ppermute | solution.py:102
  86.5 3.5 %collective-permute-start.4 = (bf16[16,126,128]{2,1,0:T(8,128)(2,1)S(1)}, bf16[16,126,128]{2,1,0:T(8,128)(2,1)S(1)}, u32[]{:S(2)}, u32[]{:S(2)}) collective-permute-start(bf16[16,126,128]{2,1,0:T(8,128)(2,1)S(1)} %collective-permute-done.2), channel_id=1, source_target_pairs={{0,16},{16,0},{32,48},{48,32},{64,80},{80,64},{96,112},{112,96},{1... | collective-permute-start | bytes 1548296 | tf_op jit(solution)/shard_map/ppermute | solution.py:103
  87.7 8.9 %collective-permute-start = (bf16[16,126,128]{2,1,0:T(8,128)(2,1)}, bf16[16,126,128]{2,1,0:T(8,128)(2,1)S(1)}, u32[]{:S(2)}, u32[]{:S(2)}) collective-permute-start(bf16[16,126,128]{2,1,0:T(8,128)(2,1)} %shard_map.55), channel_id=1, source_target_pairs={{0,16},{16,0},{32,48},{48,32},{64,80},{80,64},{96,112},{112,96},{1... | collective-permute-start | bytes 1548296 | tf_op jit(solution)/shard_map/ppermute | solution.py:101
  90.0 6.6 %copy-start.1 = (bf16[16,126,504]{1,2,0:T(8,128)(2,1)S(1)}, bf16[16,126,504]{1,2,0:T(8,128)(2,1)}, u32[]{:S(2)}) copy-start(bf16[16,126,504]{1,2,0:T(8,128)(2,1)} %all-gather.4.cloned.1.call-done) | copy-start | bytes 6096388
  92.4 6.7 %copy-start.3 = (bf16[16,126,128]{2,1,0:T(8,128)(2,1)S(1)}, bf16[16,126,128]{2,1,0:T(8,128)(2,1)}, u32[]{:S(2)}) copy-start(bf16[16,126,128]{2,1,0:T(8,128)(2,1)} %shard_map.55) | copy-start | bytes 1548292
  92.5 8.1 %collective-permute-start.5 = (bf16[504,128]{1,0:T(8,128)(2,1)S(1)}, bf16[504,128]{1,0:T(8,128)(2,1)S(1)}, u32[]{:S(2)}, u32[]{:S(2)}) collective-permute-start(bf16[504,128]{1,0:T(8,128)(2,1)S(1)} %fusion.4), channel_id=1, source_target_pairs={{0,80},{16,64},{32,112},{48,96},{64,16},{80,0},{96,48},{112,32},{1... | collective-permute-start | bytes 387080 | tf_op jit(solution)/shard_map/ppermute | solution.py:113
  97.4 5.6 %collective-permute-start.1 = (f32[504,128]{1,0:T(8,128)S(1)}, f32[504,128]{1,0:T(8,128)S(1)}, u32[]{:S(2)}, u32[]{:S(2)}) collective-permute-start(f32[504,128]{1,0:T(8,128)S(1)} %convolution_bitcast_fusion.2), channel_id=1, source_target_pairs={{0,16},{16,0},{32,48},{48,32},{64,80},{80,64},{96,112},{112,96},{1... | collective-permute-start | bytes 774152 | tf_op jit(solution)/shard_map/ppermute | solution.py:112
  98.2 4.8 %collective-permute-start.3 = (bf16[504,128]{1,0:T(8,128)(2,1)S(1)}, bf16[504,128]{1,0:T(8,128)(2,1)S(1)}, u32[]{:S(2)}, u32[]{:S(2)}) collective-permute-start(bf16[504,128]{1,0:T(8,128)(2,1)S(1)} %fusion.3), channel_id=1, source_target_pairs={{0,64},{16,80},{32,96},{48,112},{64,0},{80,16},{96,32},{112,48},{1... | collective-permute-start | bytes 387080 | tf_op jit(solution)/shard_map/ppermute | solution.py:113
  100.6 6.0 %copy-start.2 = (f32[64,64,128]{2,0,1:T(8,128)S(1)}, f32[64,64,128]{2,0,1:T(8,128)}, u32[]{:S(2)}) copy-start(f32[64,64,128]{2,0,1:T(8,128)} %fusion.5) | copy-start | bytes 6291460
  100.6 2.4 %copy-start.5 = (bf16[504,128]{1,0:T(8,128)(2,1)}, bf16[504,128]{1,0:T(8,128)(2,1)S(1)}, u32[]{:S(2)}) copy-start(bf16[504,128]{1,0:T(8,128)(2,1)S(1)} %collective-permute-done.5.p3) | copy-start | bytes 387076
  103.0 0.7 copy-start.6
  103.0 0.8 copy-start.4
Sparse Core Ops, SparseCore 0:
  9.1 76.5 all-gather.3

commit v10 on v9

--- a/solution.py
+++ b/solution.py
@@ -78,11 +78,11 @@
     q = ((me_i >> 2) & 1) * 2 + (me_i & 1)
     perms = [[(a, a ^ f) for a in range(n_oi)] for f in FLIPS]
 
-    send = amps.reshape(rows_i, rows_j, ndev, width).transpose(2, 0, 1, 3)
-    recv = lax.all_to_all(send, ("oi", "oj"), 0, 0, tiled=True)
+    send = amps.reshape(rows_i, rows_j, ndev, width)
+    recv = lax.all_to_all(send, ("oi", "oj"), 2, 2, tiled=True)
     pair_amps = (
-        recv.reshape(n_oi, n_oj, rows_i, rows_j, width)
-        .transpose(0, 2, 1, 3, 4)
+        recv.reshape(rows_i, rows_j, n_oi, n_oj, width)
+        .transpose(2, 0, 3, 1, 4)
         .reshape(occ, occ, width)
     )
 

time: 163 us -> 163 us (level)
  local copies, waits for them, and re-layouts: 9.62 us -> 7.57 us
  starting transfers between devices: 6.37 us -> 8.1 us
    ppermute x2, starting transfers between devices: 5.09 us -> 6.95 us  [on_device(): lax.ppermute(quarter(block).astype(jnp.bfloat16), 'oi', p)]
    reshape x1, local copies, waits for them, and re-layouts: 2.15 us -> 0.36 us  [on_device(): send = amps.reshape(rows_i, rows_j, ndev, width)]
  transfers between devices with their start and end apart: 7 -> 7, of which waited for: 2 -> 2; matrix products, arithmetic and copies ran while one was open for 9% -> 8% of each run, Pallas kernels for 2% -> 2%
where the time goes in v10:
time: 163 us
  blocking collectives  98.8 us (61%)
  waiting for transfers between devices  15.8 us (10%)
  between operations  13.5 us (8%)
  starting transfers between devices  8.1 us (5%)
  local copies, waits for them, and re-layouts  7.57 us (5%)
  matrix products  7.57 us (5%)
  other arithmetic  6.27 us (4%)
  Pallas kernels  5.55 us (3%)
    all_to_all x1, blocking collectives, on_device(): recv = lax.all_to_all(send, ('oi', 'oj'), 2, 2, tiled=True)  56.3 us
    all_to_all x1, blocking collectives, on_device(): out_recv = lax.all_to_all(out_send, ('oi', 'oj'), 0, 0, tiled=True)  42.5 us
    ppermute x1, waiting for transfers between devices, on_device(): from_y = lax.ppermute(anti, 'oi', perms[1])  12.8 us
    ppermute x2, starting transfers between devices, on_device(): lax.ppermute(quarter(block).astype(jnp.bfloat16), 'oi', p)  6.95 us
    pallas_call x2, Pallas kernels, vmem_call(): pl.pallas_call(kernel, out_shape=out_shape, in_specs=[pl.BlockSpec(memory...  5.55 us
    dot_general x4, matrix products, quarter(): lax.dot_general(w_blocks, block, contract, preferred_element_type=jnp.flo...  5.33 us
  transfers between devices with their start and end apart: 7, of which 2 were waited for; matrix products, arithmetic and copies ran while one was open for 8% of the time, Pallas kernels for 2%

profile of v10, /device:TPU:1, one launch (start us, length us, event | category | flops | bytes accessed | tf_op | source)
XLA Modules:
  0.0 163.1 jit_solution(12824652896330577193)
XLA Ops:
  6.5 0.0 copy-start
  6.5 0.0 all-gather.4.cloned.1.call-start
  6.5 1.7 %dynamic-slice_bitcast_fusion = bf16[1,126,504]{1,2,0:T(8,128)(2,1)} fusion(bf16[126,2016]{0,1:T(8,128)(2,1)} %param.6, s32[]{:T(128)S(6)} %select_n.6), kind=kLoop, calls=%fused_computation.16 | loop fusion | bytes 254020
  8.2 0.0 all-gather.4.cloned.1.call-update
  8.2 0.0 copy-done
  8.2 0.4 copy_bitcast_fusion.1
  8.6 56.3 %all_to_all.10 = bf16[4,4,256,128]{3,1,0,2:T(4,128)(2,1)S(1)} all-to-all(bf16[4,4,256,128]{3,1,0,2:T(4,128)(2,1)S(1)} %copy_bitcast_fusion.1), channel_id=1, replica_groups=mesh['oi'=16,'oj'=16] {'oi','oj'}, dimensions={2} | all-to-all | bytes 2097152 | tf_op jit(solution)/shard_map/all_to_all | solution.py:82
  64.9 0.3 copy.25
  65.1 0.8 copy.26
  66.0 0.2 convert_element_type.18
  66.2 2.6 %bitcast_subtract_fusion.2.d_ref = f32[64,64,128]{2,1,0:T(8,128)} fusion(f32[64,64,128]{2,0,1:T(8,128)S(1)} %convert_element_type.18), kind=kLoop, calls=%fused_computation.5 | loop fusion | flops 524288 | bytes 4194304 | tf_op jit(solution)/shard_map/sub | solution.py:93
  68.8 0.0 copy-start.8
  68.8 0.0 copy-start.7
  68.8 2.6 %shard_map.55 = bf16[16,126,128]{2,1,0:T(8,128)(2,1)} custom-call(f32[64,64,128]{2,1,0:T(8,128)} %bitcast_subtract_fusion.2.d_ref), custom_call_target="tpu_custom_call" | custom-call | tf_op jit(solution)/shard_map/pallas_call | solution.py:59
  71.4 0.0 collective-permute-start.2
  71.4 0.8 dynamic_slice.7
  72.1 12.8 %collective-permute-done.2 = bf16[16,126,128]{2,1,0:T(8,128)(2,1)S(1)} collective-permute-done((bf16[16,126,128]{2,1,0:T(8,128)(2,1)}, bf16[16,126,128]{2,1,0:T(8,128)(2,1)S(1)}, u32[]{:S(2)}, u32[]{:S(2)}) %collective-permute-start.2) | collective-permute-done | bytes 516128 | tf_op jit(solution)/shard_map/ppermute | solution.py:102
  84.9 1.0 collective-permute-start.4
  85.9 0.0 copy-done.8
  85.9 0.1 broadcast_subtract_fusion
  86.0 0.0 collective-permute-start
  86.0 0.0 copy-done.7
  86.0 2.2 %fusion.5 = f32[64,64,128]{2,0,1:T(8,128)} fusion(bf16[64,64,128]{2,0,1:T(8,128)(2,1)S(1)} %bitcast.58, bf16[64,64]{1,0:T(8,128)(2,1)S(1)} %copy-done.7), kind=kOutput, calls=%fused_computation.14 | convolution fusion | flops 67108864 | bytes 3153920 | tf_op jit(solution)/shard_map/ikp,kj->ijp/dot_general | solution.py:125
  88.3 0.0 collective-permute-done.4
  88.3 0.0 all-gather.4.cloned.1.call-done
  88.3 0.0 copy-start.1
  88.3 2.5 %fusion.4 = bf16[504,128]{1,0:T(8,128)(2,1)S(1)} fusion(bf16[16,126,504]{1,2,0:T(8,128)(2,1)} %all-gather.4.cloned.1.call-done, bf16[16,126,128]{2,1,0:T(8,128)(2,1)} %collective-permute-done.4), kind=kOutput, calls=%fused_computation.11 | convolution fusion | flops 260176896 | bytes 2677248 | tf_op jit(solution)/shard_map/dot_general | solution.py:109
  90.8 0.0 copy-start.3
  90.8 6.7 %collective-permute-start.5 = (bf16[504,128]{1,0:T(8,128)(2,1)S(1)}, bf16[504,128]{1,0:T(8,128)(2,1)S(1)}, u32[]{:S(2)}, u32[]{:S(2)}) collective-permute-start(bf16[504,128]{1,0:T(8,128)(2,1)S(1)} %fusion.4), channel_id=1, source_target_pairs={{0,80},{16,64},{32,112},{48,96},{64,16},{80,0},{96,48},{112,32},{1... | collective-permute-start | bytes 387080 | tf_op jit(solution)/shard_map/ppermute | solution.py:113
  97.6 0.0 collective-permute-done
  97.6 0.0 copy-done.1
  97.6 0.7 convolution_bitcast_fusion.2
  98.3 0.1 collective-permute-start.1
  98.4 0.7 fusion.3
  99.1 0.2 collective-permute-start.3
  99.3 0.0 copy-done.3
  99.3 1.4 convolution_bitcast_fusion.3.p0
  100.7 0.0 copy-start.2
  100.7 0.0 collective-permute-done.5.p3
  100.7 0.0 copy-start.5
  100.7 3.0 %collective-permute-done.3.p2 = bf16[504,128]{1,0:T(8,128)(2,1)S(1)} collective-permute-done((bf16[504,128]{1,0:T(8,128)(2,1)S(1)}, bf16[504,128]{1,0:T(8,128)(2,1)S(1)}, u32[]{:S(2)}, u32[]{:S(2)}) %collective-permute-start.3) | collective-permute-done | bytes 129056 | tf_op jit(solution)/shard_map/ppermute | solution.py:113
  103.7 0.0 copy-start.6
  103.7 0.0 collective-permute-done.1.p1
  103.7 0.0 copy-done.5
  103.7 0.6 copy-done.6
  104.3 0.0 copy-start.4
  104.3 0.7 copy-done.4
  105.0 3.0 %shard_map.56 = f32[64,64,128]{2,1,0:T(8,128)} custom-call(s32[1]{0:T(128)} %bitcast.q_ref, f32[504,128]{1,0:T(8,128)} %convolution_bitcast_fusion.3.p0, f32[504,128]{1,0:T(8,128)} %copy-done.4, bf16[504,128]{1,0:T(8,128)(2,1)} %copy-done.6, bf16[504,128]{1,0:T(8,128)(2,1)} %copy-done.5), custom_call_target="tpu_custom_call" | custom-call | tf_op jit(solution)/shard_map/pallas_call | solution.py:59
  108.0 0.0 copy-done.2
  108.0 2.0 %bitcast_subtract_fusion.1 = f32[64,64,128]{2,1,0:T(8,128)S(1)} fusion(f32[64,64,128]{2,1,0:T(8,128)} %shard_map.56, f32[64,64,128]{2,0,1:T(8,128)S(1)} %copy-done.2), kind=kLoop, calls=%fused_computation.4 | loop fusion | flops 524288 | bytes 6291456 | tf_op jit(solution)/shard_map/sub | solution.py:126
  110.0 1.4 fusion.2
  111.4 0.2 copy.31
  111.6 0.8 copy.32
  112.4 42.5 %all_to_all.11 = bf16[256,4,4,128]{3,2,1,0:T(4,128)(2,1)S(1)} all-to-all(bf16[256,4,4,128]{3,2,1,0:T(4,128)(2,1)S(1)} %copy.32), channel_id=1, replica_groups=mesh['oi'=16,'oj'=16] {'oi','oj'}, dimensions={0} | all-to-all | bytes 2097152 | tf_op jit(solution)/shard_map/all_to_all | solution.py:138
  154.9 1.3 copy_bitcast_fusion
Async XLA Ops:
  6.5 1.7 %copy-start = (bf16[4,4,32768]{2,1,0:T(4,128)(2,1)S(1)}, bf16[4,4,32768]{2,1,0:T(4,128)(2,1)}, u32[]{:S(2)}) copy-start(bf16[4,4,32768]{2,1,0:T(4,128)(2,1)} %param.5) | copy-start | bytes 3145732
  6.5 81.8 %all-gather.4.cloned.1.call-start = ((), (), s32[]{:S(2)}) async-start(), calls=%async_computation.2 | async-start | bytes 2193408 | tf_op jit(solution)/shard_map/all_gather | solution.py:105
  68.8 17.1 %copy-start.8 = (f32[64]{0:T(128)S(1)}, f32[64]{0:T(128)}, u32[]{:S(2)}) copy-start(f32[64]{0:T(128)} %param.8) | copy-start | bytes 772
  68.8 17.2 %copy-start.7 = (bf16[64,64]{1,0:T(8,128)(2,1)S(1)}, bf16[64,64]{1,0:T(8,128)(2,1)}, u32[]{:S(2)}) copy-start(bf16[64,64]{1,0:T(8,128)(2,1)} %param.7) | copy-start | bytes 24580
  71.4 13.5 %collective-permute-start.2 = (bf16[16,126,128]{2,1,0:T(8,128)(2,1)}, bf16[16,126,128]{2,1,0:T(8,128)(2,1)S(1)}, u32[]{:S(2)}, u32[]{:S(2)}) collective-permute-start(bf16[16,126,128]{2,1,0:T(8,128)(2,1)} %shard_map.55), channel_id=1, source_target_pairs={{0,64},{16,80},{32,96},{48,112},{64,0},{80,16},{96,32},{112,48},{1... | collective-permute-start | bytes 1548296 | tf_op jit(solution)/shard_map/ppermute | solution.py:102
  84.9 3.4 %collective-permute-start.4 = (bf16[16,126,128]{2,1,0:T(8,128)(2,1)S(1)}, bf16[16,126,128]{2,1,0:T(8,128)(2,1)}, u32[]{:S(2)}, u32[]{:S(2)}) collective-permute-start(bf16[16,126,128]{2,1,0:T(8,128)(2,1)S(1)} %collective-permute-done.2), channel_id=1, source_target_pairs={{0,16},{16,0},{32,48},{48,32},{64,80},{80,64},{96,112},{112,96},{1... | collective-permute-start | bytes 1548296 | tf_op jit(solution)/shard_map/ppermute | solution.py:103
  86.0 11.6 %collective-permute-start = (bf16[16,126,128]{2,1,0:T(8,128)(2,1)}, bf16[16,126,128]{2,1,0:T(8,128)(2,1)S(1)}, u32[]{:S(2)}, u32[]{:S(2)}) collective-permute-start(bf16[16,126,128]{2,1,0:T(8,128)(2,1)} %shard_map.55), channel_id=1, source_target_pairs={{0,16},{16,0},{32,48},{48,32},{64,80},{80,64},{96,112},{112,96},{1... | collective-permute-start | bytes 1548296 | tf_op jit(solution)/shard_map/ppermute | solution.py:101
  88.3 9.3 %copy-start.1 = (bf16[16,126,504]{1,2,0:T(8,128)(2,1)S(1)}, bf16[16,126,504]{1,2,0:T(8,128)(2,1)}, u32[]{:S(2)}) copy-start(bf16[16,126,504]{1,2,0:T(8,128)(2,1)} %all-gather.4.cloned.1.call-done) | copy-start | bytes 6096388
  90.8 8.5 %copy-start.3 = (bf16[16,126,128]{2,1,0:T(8,128)(2,1)S(1)}, bf16[16,126,128]{2,1,0:T(8,128)(2,1)}, u32[]{:S(2)}) copy-start(bf16[16,126,128]{2,1,0:T(8,128)(2,1)} %shard_map.55) | copy-start | bytes 1548292
  90.8 9.9 %collective-permute-start.5 = (bf16[504,128]{1,0:T(8,128)(2,1)S(1)}, bf16[504,128]{1,0:T(8,128)(2,1)S(1)}, u32[]{:S(2)}, u32[]{:S(2)}) collective-permute-start(bf16[504,128]{1,0:T(8,128)(2,1)S(1)} %fusion.4), channel_id=1, source_target_pairs={{0,80},{16,64},{32,112},{48,96},{64,16},{80,0},{96,48},{112,32},{1... | collective-permute-start | bytes 387080 | tf_op jit(solution)/shard_map/ppermute | solution.py:113
  98.3 5.4 %collective-permute-start.1 = (f32[504,128]{1,0:T(8,128)S(1)}, f32[504,128]{1,0:T(8,128)S(1)}, u32[]{:S(2)}, u32[]{:S(2)}) collective-permute-start(f32[504,128]{1,0:T(8,128)S(1)} %convolution_bitcast_fusion.2), channel_id=1, source_target_pairs={{0,16},{16,0},{32,48},{48,32},{64,80},{80,64},{96,112},{112,96},{1... | collective-permute-start | bytes 774152 | tf_op jit(solution)/shard_map/ppermute | solution.py:112
  99.1 4.6 %collective-permute-start.3 = (bf16[504,128]{1,0:T(8,128)(2,1)S(1)}, bf16[504,128]{1,0:T(8,128)(2,1)S(1)}, u32[]{:S(2)}, u32[]{:S(2)}) collective-permute-start(bf16[504,128]{1,0:T(8,128)(2,1)S(1)} %fusion.3), channel_id=1, source_target_pairs={{0,64},{16,80},{32,96},{48,112},{64,0},{80,16},{96,32},{112,48},{1... | collective-permute-start | bytes 387080 | tf_op jit(solution)/shard_map/ppermute | solution.py:113
  100.7 7.3 %copy-start.2 = (f32[64,64,128]{2,0,1:T(8,128)S(1)}, f32[64,64,128]{2,0,1:T(8,128)}, u32[]{:S(2)}) copy-start(f32[64,64,128]{2,0,1:T(8,128)} %fusion.5) | copy-start | bytes 6291460
  100.7 3.0 %copy-start.5 = (bf16[504,128]{1,0:T(8,128)(2,1)}, bf16[504,128]{1,0:T(8,128)(2,1)S(1)}, u32[]{:S(2)}) copy-start(bf16[504,128]{1,0:T(8,128)(2,1)S(1)} %collective-permute-done.5.p3) | copy-start | bytes 387076
  103.7 0.7 copy-start.6
  104.3 0.7 copy-start.4
Sparse Core Ops, SparseCore 0:
  9.1 77.0 all-gather.3

commit v11 on v9

--- a/solution.py
+++ b/solution.py
@@ -36,9 +36,10 @@
         o_ref[b] = tmp_ref[b * rows : (b + 1) * rows, :].astype(o_ref.dtype)
 
 
-def spread_kernel(q_ref, p0, p1, p2, p3, o_ref, lad_ref):
-    pieces = (p0, p1, p2, p3)
-    part = p0.shape[0]
+def spread_kernel(q_ref, *refs):
+    o_ref, lad_ref = refs[-2], refs[-1]
+    halves = refs[:-2]
+    rows = halves[0].shape[0]
     q = q_ref[0]
     lad_ref[0:8, :] = jnp.zeros((8, lad_ref.shape[1]), lad_ref.dtype)
     for r in range(4):
@@ -46,7 +47,9 @@
 
             @pl.when(jnp.bitwise_xor(q, r) == n)
             def _():
-                lad_ref[8 + r * part : 8 + (r + 1) * part, :] = pieces[n][...].astype(lad_ref.dtype)
+                for h in range(2):
+                    start = 8 + (2 * r + h) * rows
+                    lad_ref[start : start + rows, :] = halves[2 * n + h][...].astype(lad_ref.dtype)
 
     occ, width = o_ref.shape[0], o_ref.shape[2]
     col = lax.broadcasted_iota(jnp.int32, (occ, width), 0)
@@ -101,25 +104,33 @@
     from_core = lax.ppermute(anti, "oi", perms[0])
     from_y = lax.ppermute(anti, "oi", perms[1])
     from_diag = lax.ppermute(from_y, "oi", perms[0])
-    w_part = lax.dynamic_slice_in_dim(ladder_w, q * part, part, 1)
-    w_blocks = lax.all_gather(w_part, "oj", axis=0, tiled=False)
+    half = part // 2
+    w_halves = [
+        lax.all_gather(
+            lax.dynamic_slice_in_dim(ladder_w, q * part + h * half, half, 1), "oj", axis=0, tiled=False
+        )
+        for h in range(2)
+    ]
     contract = (((0, 1), (0, 1)), ((), ()))
 
-    def quarter(block):
-        return lax.dot_general(w_blocks, block, contract, preferred_element_type=jnp.float32)
+    def quarter(w, block):
+        return lax.dot_general(w, block, contract, preferred_element_type=jnp.float32)
 
-    own = quarter(anti)
-    back = [lax.ppermute(quarter(from_core), "oi", perms[0])] + [
-        lax.ppermute(quarter(block).astype(jnp.bfloat16), "oi", p)
-        for block, p in zip((from_y, from_diag), perms[1:])
-    ]
+    pieces = []
+    for n, block in enumerate((anti, from_core, from_y, from_diag)):
+        for w in w_halves:
+            v = quarter(w, block)
+            if n >= 2:
+                v = v.astype(jnp.bfloat16)
+            if n >= 1:
+                v = lax.ppermute(v, "oi", perms[n - 1])
+            pieces.append(v)
     upper_part = vmem_call(
         spread_kernel,
         jax.ShapeDtypeStruct((occ, occ, width), jnp.float32),
         [pltpu.VMEM((8 + npairs, width), jnp.float32)],
         q.astype(jnp.int32).reshape(1),
-        own,
-        *back,
+        *pieces,
         smem=1,
     )
     mixed = jnp.einsum("ikp,kj->ijp", pair_amps, fock, preferred_element_type=jnp.float32)

time: 163 us -> 200 us (1.23)
  starting transfers between devices: 6.37 us -> 39 us
  blocking collectives: 98.4 us -> 129 us
  waiting for transfers between devices: 15.1 us -> 0.67 us
  between operations: 13.5 us -> 0.18 us
    all_gather x0 -> x2, blocking collectives: none -> 86 us  [on_device(): lax.all_gather(lax.dynamic_slice_in_dim(ladder_w, q * part + h * half, ha...]
    all_to_all x1 -> x0, blocking collectives: 55.4 us -> none  [on_device(): recv = lax.all_to_all(send, ('oi', 'oj'), 0, 0, tiled=True)]
    all_to_all x0 -> x1, starting transfers between devices: none -> 15.6 us  [on_device(): recv = lax.all_to_all(send, ('oi', 'oj'), 0, 0, tiled=True)]
    ppermute x1, waiting for transfers between devices: 12.6 us -> 0.01 us  [on_device(): from_y = lax.ppermute(anti, 'oi', perms[1])]
    ppermute x1, starting transfers between devices: 0.03 us -> 12.5 us  [on_device(): from_core = lax.ppermute(anti, 'oi', perms[0])]
    ppermute x1, starting transfers between devices: 1.15 us -> 3.95 us  [on_device(): from_diag = lax.ppermute(from_y, 'oi', perms[0])]
    ppermute x3 -> x6, starting transfers between devices: 5.18 us -> 6.34 us  [on_device(): v = lax.ppermute(v, 'oi', perms[n - 1])]
    dot_general x4 -> x8, matrix products: 5.33 us -> 6.18 us  [quarter(): lax.dot_general(w, block, contract, preferred_element_type=jnp.float32)]
  transfers between devices with their start and end apart: 7 -> 10, of which waited for: 2 -> 2; matrix products, arithmetic and copies ran while one was open for 9% -> 5% of each run, Pallas kernels for 2% -> 0%
where the time goes in v11:
time: 200 us
  blocking collectives  129 us (64%)
  starting transfers between devices  39 us (20%)
  local copies, waits for them, and re-layouts  11.2 us (6%)
  matrix products  8.41 us (4%)
  other arithmetic  6.27 us (3%)
  Pallas kernels  5.26 us (3%)
    all_gather x2, blocking collectives, on_device(): lax.all_gather(lax.dynamic_slice_in_dim(ladder_w, q * part + h * half, ha...  86 us
    all_to_all x1, blocking collectives, on_device(): out_recv = lax.all_to_all(out_send, ('oi', 'oj'), 0, 0, tiled=True)  43.1 us
    all_to_all x1, starting transfers between devices, on_device(): recv = lax.all_to_all(send, ('oi', 'oj'), 0, 0, tiled=True)  15.6 us
    ppermute x1, starting transfers between devices, on_device(): from_core = lax.ppermute(anti, 'oi', perms[0])  12.5 us
    ppermute x6, starting transfers between devices, on_device(): v = lax.ppermute(v, 'oi', perms[n - 1])  6.34 us
    dot_general x8, matrix products, quarter(): lax.dot_general(w, block, contract, preferred_element_type=jnp.float32)  6.18 us
    pallas_call x2, Pallas kernels, vmem_call(): pl.pallas_call(kernel, out_shape=out_shape, in_specs=[pl.BlockSpec(memory...  5.26 us
  transfers between devices with their start and end apart: 10, of which 2 were waited for; matrix products, arithmetic and copies ran while one was open for 5% of the time, Pallas kernels for 0%

profile of v11, /device:TPU:1, one launch (start us, length us, event | category | flops | bytes accessed | tf_op | source)
XLA Modules:
  0.0 200.1 jit_solution(10402398917664508894)
XLA Ops:
  0.0 0.0 copy-start
  0.0 2.2 %reshape.51 = bf16[4,4,256,128]{3,2,1,0:T(8,128)(2,1)S(1)} reshape(bf16[4,4,32768]{2,1,0:T(4,128)(2,1)} %param.5) | data formatting | bytes 2097152 | tf_op jit(solution)/shard_map/reshape | solution.py:84
  2.2 1.8 copy.35
  4.0 15.6 %all-to-all-start = ((bf16[256,4,4,128]{3,2,1,0:T(4,128)(2,1)}), bf16[256,4,4,128]{3,2,1,0:T(4,128)(2,1)S(1)}, u32[]{:S(2)}, u32[]{:S(2)}) async-start(bf16[256,4,4,128]{3,2,1,0:T(4,128)(2,1)} %copy.35), calls=%async_computation | async-start | bytes 2097152 | tf_op jit(solution)/shard_map/all_to_all | solution.py:85
  19.6 1.0 constant_dynamic-slice_fusion
  20.6 0.1 copy.34
  20.7 0.1 copy.40
  20.9 0.8 dynamic_slice.11
  21.6 52.8 %all-gather.2 = bf16[16,126,252]{2,1,0:T(8,128)(2,1)S(1)} all-gather(bf16[1,126,252]{2,1,0:T(8,128)(2,1)S(1)} %bitcast.79), channel_id=2, replica_groups=mesh['oi'=16,'oj'=16] {'oj'}, dimensions={0}, use_global_device_ids=true | all-gather | bytes 1079568 | tf_op jit(solution)/shard_map/all_gather | solution.py:109
  74.4 33.2 %all-gather.3 = bf16[16,126,252]{2,1,0:T(8,128)(2,1)S(1)} all-gather(bf16[1,126,252]{2,1,0:T(8,128)(2,1)S(1)} %bitcast.80), channel_id=3, replica_groups=mesh['oi'=16,'oj'=16] {'oj'}, dimensions={0}, use_global_device_ids=true | all-gather | bytes 1079568 | tf_op jit(solution)/shard_map/all_gather | solution.py:109
  107.7 0.0 all-to-all-done
  107.7 0.3 copy.36
  107.9 0.8 copy.37
  108.8 0.2 convert_element_type.24
  109.0 2.6 %bitcast_subtract_fusion.2.d_ref = f32[64,64,128]{2,1,0:T(8,128)} fusion(f32[64,64,128]{2,0,1:T(8,128)S(1)} %convert_element_type.24), kind=kLoop, calls=%fused_computation.5 | loop fusion | flops 524288 | bytes 4194304 | tf_op jit(solution)/shard_map/sub | solution.py:96
  111.6 2.5 %shard_map.55 = bf16[16,126,128]{2,1,0:T(8,128)(2,1)} custom-call(f32[64,64,128]{2,1,0:T(8,128)} %bitcast_subtract_fusion.2.d_ref), custom_call_target="tpu_custom_call" | custom-call | tf_op jit(solution)/shard_map/pallas_call | solution.py:62
  114.1 0.5 collective-permute-start.3
  114.6 0.0 copy-done.9
  114.6 0.1 broadcast_subtract_fusion
  114.7 12.5 %collective-permute-start = (bf16[16,126,128]{2,1,0:T(8,128)(2,1)}, bf16[16,126,128]{2,1,0:T(8,128)(2,1)S(1)}, u32[]{:S(2)}, u32[]{:S(2)}) collective-permute-start(bf16[16,126,128]{2,1,0:T(8,128)(2,1)} %shard_map.55), channel_id=1, source_target_pairs={{0,16},{16,0},{32,48},{48,32},{64,80},{80,64},{96,112},{112,96},{1... | collective-permute-start | bytes 1548296 | tf_op jit(solution)/shard_map/ppermute | solution.py:104
  127.2 2.2 %convolution_bitcast_fusion.6.refs_1_ = f32[252,128]{1,0:T(8,128)} fusion(bf16[16,126,252]{2,1,0:T(8,128)(2,1)S(1)} %all-gather.3, bf16[16,126,128]{2,1,0:T(8,128)(2,1)} %shard_map.55), kind=kOutput, calls=%fused_computation.12 | convolution fusion | flops 130056192 | bytes 1661184 | tf_op jit(solution)/shard_map/dot_general | solution.py:117
  129.4 0.0 copy-done
  129.4 2.2 %fusion.7 = f32[64,64,128]{2,0,1:T(8,128)} fusion(bf16[64,64,128]{2,0,1:T(8,128)(2,1)S(1)} %bitcast.74, bf16[64,64]{1,0:T(8,128)(2,1)S(1)} %copy-done), kind=kOutput, calls=%fused_computation.19 | convolution fusion | flops 67108864 | bytes 3153920 | tf_op jit(solution)/shard_map/ikp,kj->ijp/dot_general | solution.py:136
  131.6 0.0 collective-permute-done.3
  131.6 0.5 fusion.3
  132.1 1.8 collective-permute-start.4
  133.9 3.9 %collective-permute-start.6 = (bf16[16,126,128]{2,1,0:T(8,128)(2,1)S(1)}, bf16[16,126,128]{2,1,0:T(8,128)(2,1)S(1)}, u32[]{:S(2)}, u32[]{:S(2)}) collective-permute-start(bf16[16,126,128]{2,1,0:T(8,128)(2,1)S(1)} %collective-permute-done.3), channel_id=1, source_target_pairs={{0,16},{16,0},{32,48},{48,32},{64,80},{80,64},{96,112},{112,96},{1... | collective-permute-start | bytes 1548296 | tf_op jit(solution)/shard_map/ppermute | solution.py:106
  137.9 0.5 fusion.4
  138.4 1.7 collective-permute-start.5
  140.1 0.0 collective-permute-done
  140.1 0.5 convolution_bitcast_fusion.5
  140.6 0.0 copy-start.2
  140.6 0.6 collective-permute-start.1
  141.1 0.5 convolution_bitcast_fusion.4
  141.6 0.3 collective-permute-start.2
  141.9 0.0 collective-permute-done.6
  141.9 0.5 fusion.5
  142.4 0.1 collective-permute-start.7
  142.5 0.5 fusion.6
  143.0 0.0 copy-start.1
  143.0 0.0 collective-permute-done.4.refs_4_
  143.0 0.0 copy-start.5
  143.1 1.8 collective-permute-start.8
  144.9 0.0 copy-done.2
  144.9 1.1 convolution_bitcast_fusion.7.refs_0_
  146.0 0.0 collective-permute-done.5.refs_5_
  146.0 0.0 collective-permute-done.1.refs_2_
  146.0 0.0 copy-start.3
  146.0 0.0 collective-permute-done.2.refs_3_
  146.1 0.6 copy-done.6
  146.6 0.6 collective-permute-done.7.refs_6_
  147.2 0.6 copy-done.7
  147.8 0.1 collective-permute-done.8.refs_7_
  147.9 0.6 copy-done.8
  148.5 0.0 copy-done.5
  148.5 0.0 copy-done.4
  148.5 2.7 %shard_map.56 = f32[64,64,128]{2,1,0:T(8,128)} custom-call(s32[1]{0:T(128)} %bitcast.q_ref, f32[252,128]{1,0:T(8,128)} %convolution_bitcast_fusion.7.refs_0_, f32[252,128]{1,0:T(8,128)} %convolution_bitcast_fusion.6.refs_1_, f32[252,128]{1,0:T(8,128)} %copy-done.3, f32[252,128]{1,0:T(8,128)} %copy-done.4, bf16[252,128]{1,0:T(8,128)(2,1)} %copy-done.5, ...), custom_call_target="tpu_custom_call" | custom-call | tf_op jit(solution)/shard_map/pallas_call | solution.py:62
  151.3 0.0 copy-done.1
  151.3 2.0 bitcast_subtract_fusion.1
  153.3 1.4 fusion.2
  154.7 0.2 copy.51
  154.9 0.8 copy.52
  155.7 43.1 %all_to_all.10 = bf16[256,4,4,128]{3,2,1,0:T(4,128)(2,1)S(1)} all-to-all(bf16[256,4,4,128]{3,2,1,0:T(4,128)(2,1)S(1)} %copy.52), channel_id=1, replica_groups=mesh['oi'=16,'oj'=16] {'oi','oj'}, dimensions={0} | all-to-all | bytes 2097152 | tf_op jit(solution)/shard_map/all_to_all | solution.py:149
  198.8 1.3 copy_bitcast_fusion
  (6 shorter events, 0.0 us)
Async XLA Ops:
  0.0 129.4 %copy-start = (bf16[64,64]{1,0:T(8,128)(2,1)S(1)}, bf16[64,64]{1,0:T(8,128)(2,1)}, u32[]{:S(2)}) copy-start(bf16[64,64]{1,0:T(8,128)(2,1)} %param.7) | copy-start | bytes 24580
  4.0 103.7 %all-to-all-start = ((bf16[256,4,4,128]{3,2,1,0:T(4,128)(2,1)}), bf16[256,4,4,128]{3,2,1,0:T(4,128)(2,1)S(1)}, u32[]{:S(2)}, u32[]{:S(2)}) async-start(bf16[256,4,4,128]{3,2,1,0:T(4,128)(2,1)} %copy.35), calls=%async_computation | async-start | bytes 2097152 | tf_op jit(solution)/shard_map/all_to_all | solution.py:85
  111.6 3.0 %copy-start.9 = (f32[64]{0:T(128)S(1)}, f32[64]{0:T(128)}, u32[]{:S(2)}) copy-start(f32[64]{0:T(128)} %param.8) | copy-start | bytes 772
  114.1 17.5 %collective-permute-start.3 = (bf16[16,126,128]{2,1,0:T(8,128)(2,1)}, bf16[16,126,128]{2,1,0:T(8,128)(2,1)S(1)}, u32[]{:S(2)}, u32[]{:S(2)}) collective-permute-start(bf16[16,126,128]{2,1,0:T(8,128)(2,1)} %shard_map.55), channel_id=1, source_target_pairs={{0,64},{16,80},{32,96},{48,112},{64,0},{80,16},{96,32},{112,48},{1... | collective-permute-start | bytes 1548296 | tf_op jit(solution)/shard_map/ppermute | solution.py:105
  114.7 25.4 %collective-permute-start = (bf16[16,126,128]{2,1,0:T(8,128)(2,1)}, bf16[16,126,128]{2,1,0:T(8,128)(2,1)S(1)}, u32[]{:S(2)}, u32[]{:S(2)}) collective-permute-start(bf16[16,126,128]{2,1,0:T(8,128)(2,1)} %shard_map.55), channel_id=1, source_target_pairs={{0,16},{16,0},{32,48},{48,32},{64,80},{80,64},{96,112},{112,96},{1... | collective-permute-start | bytes 1548296 | tf_op jit(solution)/shard_map/ppermute | solution.py:104
  132.1 10.9 %collective-permute-start.4 = (bf16[252,128]{1,0:T(8,128)(2,1)S(1)}, bf16[252,128]{1,0:T(8,128)(2,1)S(1)}, u32[]{:S(2)}, u32[]{:S(2)}) collective-permute-start(bf16[252,128]{1,0:T(8,128)(2,1)S(1)} %fusion.3), channel_id=1, source_target_pairs={{0,64},{16,80},{32,96},{48,112},{64,0},{80,16},{96,32},{112,48},{1... | collective-permute-start | bytes 193544 | tf_op jit(solution)/shard_map/ppermute | solution.py:126
  133.9 8.0 %collective-permute-start.6 = (bf16[16,126,128]{2,1,0:T(8,128)(2,1)S(1)}, bf16[16,126,128]{2,1,0:T(8,128)(2,1)S(1)}, u32[]{:S(2)}, u32[]{:S(2)}) collective-permute-start(bf16[16,126,128]{2,1,0:T(8,128)(2,1)S(1)} %collective-permute-done.3), channel_id=1, source_target_pairs={{0,16},{16,0},{32,48},{48,32},{64,80},{80,64},{96,112},{112,96},{1... | collective-permute-start | bytes 1548296 | tf_op jit(solution)/shard_map/ppermute | solution.py:106
  138.4 7.7 %collective-permute-start.5 = (bf16[252,128]{1,0:T(8,128)(2,1)S(1)}, bf16[252,128]{1,0:T(8,128)(2,1)S(1)}, u32[]{:S(2)}, u32[]{:S(2)}) collective-permute-start(bf16[252,128]{1,0:T(8,128)(2,1)S(1)} %fusion.4), channel_id=1, source_target_pairs={{0,64},{16,80},{32,96},{48,112},{64,0},{80,16},{96,32},{112,48},{1... | collective-permute-start | bytes 193544 | tf_op jit(solution)/shard_map/ppermute | solution.py:126
  140.6 4.3 %copy-start.2 = (bf16[16,126,128]{2,1,0:T(8,128)(2,1)S(1)}, bf16[16,126,128]{2,1,0:T(8,128)(2,1)}, u32[]{:S(2)}) copy-start(bf16[16,126,128]{2,1,0:T(8,128)(2,1)} %shard_map.55) | copy-start | bytes 1548292
  140.6 5.4 %collective-permute-start.1 = (f32[252,128]{1,0:T(8,128)S(1)}, f32[252,128]{1,0:T(8,128)S(1)}, u32[]{:S(2)}, u32[]{:S(2)}) collective-permute-start(f32[252,128]{1,0:T(8,128)S(1)} %convolution_bitcast_fusion.5), channel_id=1, source_target_pairs={{0,16},{16,0},{32,48},{48,32},{64,80},{80,64},{96,112},{112,96},{1... | collective-permute-start | bytes 387080 | tf_op jit(solution)/shard_map/ppermute | solution.py:126
  141.6 4.4 %collective-permute-start.2 = (f32[252,128]{1,0:T(8,128)S(1)}, f32[252,128]{1,0:T(8,128)S(1)}, u32[]{:S(2)}, u32[]{:S(2)}) collective-permute-start(f32[252,128]{1,0:T(8,128)S(1)} %convolution_bitcast_fusion.4), channel_id=1, source_target_pairs={{0,16},{16,0},{32,48},{48,32},{64,80},{80,64},{96,112},{112,96},{1... | collective-permute-start | bytes 387080 | tf_op jit(solution)/shard_map/ppermute | solution.py:126
  142.4 4.8 %collective-permute-start.7 = (bf16[252,128]{1,0:T(8,128)(2,1)S(1)}, bf16[252,128]{1,0:T(8,128)(2,1)S(1)}, u32[]{:S(2)}, u32[]{:S(2)}) collective-permute-start(bf16[252,128]{1,0:T(8,128)(2,1)S(1)} %fusion.5), channel_id=1, source_target_pairs={{0,80},{16,64},{32,112},{48,96},{64,16},{80,0},{96,48},{112,32},{1... | collective-permute-start | bytes 193544 | tf_op jit(solution)/shard_map/ppermute | solution.py:126
  143.0 8.2 %copy-start.1 = (f32[64,64,128]{2,0,1:T(8,128)S(1)}, f32[64,64,128]{2,0,1:T(8,128)}, u32[]{:S(2)}) copy-start(f32[64,64,128]{2,0,1:T(8,128)} %fusion.7) | copy-start | bytes 6291460
  143.0 5.5 %copy-start.5 = (bf16[252,128]{1,0:T(8,128)(2,1)}, bf16[252,128]{1,0:T(8,128)(2,1)S(1)}, u32[]{:S(2)}) copy-start(bf16[252,128]{1,0:T(8,128)(2,1)S(1)} %collective-permute-done.4.refs_4_) | copy-start | bytes 193540
  143.1 4.9 %collective-permute-start.8 = (bf16[252,128]{1,0:T(8,128)(2,1)S(1)}, bf16[252,128]{1,0:T(8,128)(2,1)S(1)}, u32[]{:S(2)}, u32[]{:S(2)}) collective-permute-start(bf16[252,128]{1,0:T(8,128)(2,1)S(1)} %fusion.6), channel_id=1, source_target_pairs={{0,80},{16,64},{32,112},{48,96},{64,16},{80,0},{96,48},{112,32},{1... | collective-permute-start | bytes 193544 | tf_op jit(solution)/shard_map/ppermute | solution.py:126
  146.0 0.6 copy-start.6
  146.0 2.5 %copy-start.3 = (f32[252,128]{1,0:T(8,128)}, f32[252,128]{1,0:T(8,128)S(1)}, u32[]{:S(2)}) copy-start(f32[252,128]{1,0:T(8,128)S(1)} %collective-permute-done.1.refs_2_) | copy-start | bytes 387076
  146.6 1.9 copy-start.4
  147.2 0.6 copy-start.7
  147.9 0.6 copy-start.8

commit v12 on v9

--- a/solution.py
+++ b/solution.py
@@ -108,11 +108,13 @@
     def quarter(block):
         return lax.dot_general(w_blocks, block, contract, preferred_element_type=jnp.float32)
 
+    far = quarter(jnp.concatenate([from_y, from_diag], axis=2)).astype(jnp.bfloat16)
+    far_back = [
+        lax.ppermute(far[:, n * width : (n + 1) * width], "oi", p)
+        for n, p in enumerate(perms[1:])
+    ]
     own = quarter(anti)
-    back = [lax.ppermute(quarter(from_core), "oi", perms[0])] + [
-        lax.ppermute(quarter(block).astype(jnp.bfloat16), "oi", p)
-        for block, p in zip((from_y, from_diag), perms[1:])
-    ]
+    back = [lax.ppermute(quarter(from_core), "oi", perms[0])] + far_back
     upper_part = vmem_call(
         spread_kernel,
         jax.ShapeDtypeStruct((occ, occ, width), jnp.float32),

time: 163 us -> 164 us (level)
    ppermute x3, waiting for transfers between devices: 2.43 us -> 4.81 us  [the longest x2 4.8 us: on_device(): lax.ppermute(far[:, n * width:(n + 1) * width], 'oi', p)]
    dot_general x4 -> x3, matrix products: 5.33 us -> 5.81 us  [quarter(): lax.dot_general(w_blocks, block, contract, preferred_element_type=jnp.flo...]
  transfers between devices with their start and end apart: 7 -> 7, of which waited for: 2 -> 3; matrix products, arithmetic and copies ran while one was open for 9% -> 10% of each run, Pallas kernels for 2% -> 2%
where the time goes in v12:
time: 164 us
  blocking collectives  97.4 us (59%)
  waiting for transfers between devices  16.5 us (10%)
  between operations  13.5 us (8%)
  local copies, waits for them, and re-layouts  9.67 us (6%)
  matrix products  8.04 us (5%)
  starting transfers between devices  7.14 us (4%)
  other arithmetic  6.35 us (4%)
  Pallas kernels  5.53 us (3%)
    all_to_all x1, blocking collectives, on_device(): recv = lax.all_to_all(send, ('oi', 'oj'), 0, 0, tiled=True)  55.4 us
    all_to_all x1, blocking collectives, on_device(): out_recv = lax.all_to_all(out_send, ('oi', 'oj'), 0, 0, tiled=True)  42.1 us
    ppermute x1, waiting for transfers between devices, on_device(): from_y = lax.ppermute(anti, 'oi', perms[1])  11.6 us
    dot_general x3, matrix products, quarter(): lax.dot_general(w_blocks, block, contract, preferred_element_type=jnp.flo...  5.81 us
    pallas_call x2, Pallas kernels, vmem_call(): pl.pallas_call(kernel, out_shape=out_shape, in_specs=[pl.BlockSpec(memory...  5.53 us
    ppermute x2, waiting for transfers between devices, on_device(): lax.ppermute(far[:, n * width:(n + 1) * width], 'oi', p)  4.8 us
  transfers between devices with their start and end apart: 7, of which 3 were waited for; matrix products, arithmetic and copies ran while one was open for 10% of the time, Pallas kernels for 2%

profile of v12, /device:TPU:1, one launch (start us, length us, event | category | flops | bytes accessed | tf_op | source)
XLA Modules:
  0.0 164.1 jit_solution(15394921590597874657)
XLA Ops:
  6.5 0.0 copy-start
  6.5 0.0 all-gather.4.cloned.1.call-start
  6.5 1.0 copy-done
  7.6 0.7 dynamic-slice_bitcast_fusion
  8.3 0.0 all-gather.4.cloned.1.call-update
  8.3 2.1 %reshape.51 = bf16[4,4,256,128]{3,2,1,0:T(8,128)(2,1)S(1)} reshape(bf16[4,4,32768]{2,1,0:T(4,128)(2,1)} %param.5) | data formatting | bytes 2097152 | tf_op jit(solution)/shard_map/reshape | solution.py:81
  10.4 0.8 copy.24
  11.3 55.4 %all_to_all.10 = bf16[256,4,4,128]{3,2,1,0:T(4,128)(2,1)S(1)} all-to-all(bf16[256,4,4,128]{3,2,1,0:T(4,128)(2,1)S(1)} %copy.24), channel_id=1, replica_groups=mesh['oi'=16,'oj'=16] {'oi','oj'}, dimensions={0} | all-to-all | bytes 2097152 | tf_op jit(solution)/shard_map/all_to_all | solution.py:82
  66.7 0.3 copy.25
  66.9 0.8 copy.26
  67.7 0.2 convert_element_type.15
  68.0 2.6 %bitcast_subtract_fusion.2.d_ref = f32[64,64,128]{2,1,0:T(8,128)} fusion(f32[64,64,128]{2,0,1:T(8,128)S(1)} %convert_element_type.15), kind=kLoop, calls=%fused_computation.5 | loop fusion | flops 524288 | bytes 4194304 | tf_op jit(solution)/shard_map/sub | solution.py:93
  70.6 0.0 copy-start.8
  70.6 0.0 copy-start.7
  70.6 2.5 %shard_map.55 = bf16[16,126,128]{2,1,0:T(8,128)(2,1)} custom-call(f32[64,64,128]{2,1,0:T(8,128)} %bitcast_subtract_fusion.2.d_ref), custom_call_target="tpu_custom_call" | custom-call | tf_op jit(solution)/shard_map/pallas_call | solution.py:59
  73.1 0.0 collective-permute-start.2
  73.1 0.8 dynamic_slice.7
  73.9 1.0 collective-permute-start
  74.9 0.0 copy-done.8
  74.9 0.1 broadcast_subtract_fusion
  74.9 11.6 %collective-permute-done.2 = bf16[16,126,128]{2,1,0:T(8,128)(2,1)} collective-permute-done((bf16[16,126,128]{2,1,0:T(8,128)(2,1)}, bf16[16,126,128]{2,1,0:T(8,128)(2,1)}, u32[]{:S(2)}, u32[]{:S(2)}) %collective-permute-start.2) | collective-permute-done | bytes 516128 | tf_op jit(solution)/shard_map/ppermute | solution.py:102
  86.6 1.2 collective-permute-start.3
  87.8 0.0 copy-done.7
  87.8 2.2 %fusion.7 = f32[64,64,128]{2,0,1:T(8,128)} fusion(bf16[64,64,128]{2,0,1:T(8,128)(2,1)S(1)} %bitcast.47, bf16[64,64]{1,0:T(8,128)(2,1)S(1)} %copy-done.7), kind=kOutput, calls=%fused_computation.14 | convolution fusion | flops 67108864 | bytes 3153920 | tf_op jit(solution)/shard_map/ikp,kj->ijp/dot_general | solution.py:127
  90.0 0.0 collective-permute-done
  90.0 0.0 all-gather.4.cloned.1.call-done
  90.0 0.0 copy-start.2
  90.0 2.4 %convolution_bitcast_fusion.1 = f32[504,128]{1,0:T(8,128)S(1)} fusion(bf16[16,126,504]{1,2,0:T(8,128)(2,1)} %all-gather.4.cloned.1.call-done, bf16[16,126,128]{2,1,0:T(8,128)(2,1)S(1)} %collective-permute-done), kind=kOutput, calls=%fused_computation.8 | convolution fusion | flops 260112384 | bytes 2806272 | tf_op jit(solution)/shard_map/dot_general | solution.py:109
  92.5 0.0 copy-start.3
  92.5 3.2 %collective-permute-start.1 = (f32[504,128]{1,0:T(8,128)S(1)}, f32[504,128]{1,0:T(8,128)S(1)}, u32[]{:S(2)}, u32[]{:S(2)}) collective-permute-start(f32[504,128]{1,0:T(8,128)S(1)} %convolution_bitcast_fusion.1), channel_id=1, source_target_pairs={{0,16},{16,0},{32,48},{48,32},{64,80},{80,64},{96,112},{112,96},{1... | collective-permute-start | bytes 774152 | tf_op jit(solution)/shard_map/ppermute | solution.py:117
  95.7 0.0 collective-permute-done.3
  95.7 0.0 copy-done.2
  95.7 1.9 %fusion.3 = bf16[504,256]{1,0:T(8,128)(2,1)S(1)} fusion(bf16[16,126,504]{1,2,0:T(8,128)(2,1)S(1)} %copy-done.2, bf16[16,126,128]{2,1,0:T(8,128)(2,1)} %collective-permute-done.3, bf16[16,126,128]{2,1,0:T(8,128)(2,1)} %collective-permute-done.2), kind=kOutput, calls=%fused_computation.7 | convolution fusion | flops 522418176 | bytes 3322368 | tf_op jit(solution)/shard_map/dot_general | solution.py:109
  97.6 0.8 collective-permute-start.4
  98.5 0.9 collective-permute-start.5
  99.4 0.0 copy-done.3
  99.4 1.4 convolution_bitcast_fusion.2.p0
  100.8 0.0 copy-start.1
  100.9 1.8 %collective-permute-done.4.p2 = bf16[504,128]{1,0:T(8,128)(2,1)S(1)} collective-permute-done((bf16[504,128]{1,0:T(8,128)(2,1)S(1)}, bf16[504,128]{1,0:T(8,128)(2,1)S(1)}, u32[]{:S(2)}, u32[]{:S(2)}) %collective-permute-start.4) | collective-permute-done | bytes 129056 | tf_op jit(solution)/shard_map/ppermute | solution.py:113
  102.7 0.0 copy-start.5
  102.7 3.0 %collective-permute-done.5.p3 = bf16[504,128]{1,0:T(8,128)(2,1)S(1)} collective-permute-done((bf16[504,128]{1,0:T(8,128)(2,1)S(1)}, bf16[504,128]{1,0:T(8,128)(2,1)S(1)}, u32[]{:S(2)}, u32[]{:S(2)}) %collective-permute-start.5) | collective-permute-done | bytes 129056 | tf_op jit(solution)/shard_map/ppermute | solution.py:113
  105.7 0.0 copy-start.6
  105.7 0.0 collective-permute-done.1.p1
  105.7 0.0 copy-start.4
  105.7 0.0 copy-done.5
  105.7 0.6 copy-done.6
  106.3 0.1 copy-done.4
  106.4 3.0 %shard_map.56 = f32[64,64,128]{2,1,0:T(8,128)} custom-call(s32[1]{0:T(128)} %bitcast.q_ref, f32[504,128]{1,0:T(8,128)} %convolution_bitcast_fusion.2.p0, f32[504,128]{1,0:T(8,128)} %copy-done.4, bf16[504,128]{1,0:T(8,128)(2,1)} %copy-done.5, bf16[504,128]{1,0:T(8,128)(2,1)} %copy-done.6), custom_call_target="tpu_custom_call" | custom-call | tf_op jit(solution)/shard_map/pallas_call | solution.py:59
  109.4 0.0 copy-done.1
  109.4 2.1 %bitcast_subtract_fusion.1 = f32[64,64,128]{2,1,0:T(8,128)S(1)} fusion(f32[64,64,128]{2,1,0:T(8,128)} %shard_map.56, f32[64,64,128]{2,0,1:T(8,128)S(1)} %copy-done.1), kind=kLoop, calls=%fused_computation.4 | loop fusion | flops 524288 | bytes 6291456 | tf_op jit(solution)/shard_map/sub | solution.py:128
  111.5 1.4 fusion.2
  112.9 0.2 copy.31
  113.1 0.8 copy.32
  113.9 42.1 %all_to_all.11 = bf16[256,4,4,128]{3,2,1,0:T(4,128)(2,1)S(1)} all-to-all(bf16[256,4,4,128]{3,2,1,0:T(4,128)(2,1)S(1)} %copy.32), channel_id=1, replica_groups=mesh['oi'=16,'oj'=16] {'oi','oj'}, dimensions={0} | all-to-all | bytes 2097152 | tf_op jit(solution)/shard_map/all_to_all | solution.py:140
  155.9 1.3 copy_bitcast_fusion
  (1 shorter events, 0.0 us)
Async XLA Ops:
  6.5 1.0 copy-start
  6.5 83.5 %all-gather.4.cloned.1.call-start = ((), (), s32[]{:S(2)}) async-start(), calls=%async_computation.2 | async-start | bytes 2193408 | tf_op jit(solution)/shard_map/all_gather | solution.py:105
  70.6 4.3 %copy-start.8 = (f32[64]{0:T(128)S(1)}, f32[64]{0:T(128)}, u32[]{:S(2)}) copy-start(f32[64]{0:T(128)} %param.8) | copy-start | bytes 772
  70.6 17.2 %copy-start.7 = (bf16[64,64]{1,0:T(8,128)(2,1)S(1)}, bf16[64,64]{1,0:T(8,128)(2,1)}, u32[]{:S(2)}) copy-start(bf16[64,64]{1,0:T(8,128)(2,1)} %param.7) | copy-start | bytes 24580
  73.1 13.4 %collective-permute-start.2 = (bf16[16,126,128]{2,1,0:T(8,128)(2,1)}, bf16[16,126,128]{2,1,0:T(8,128)(2,1)}, u32[]{:S(2)}, u32[]{:S(2)}) collective-permute-start(bf16[16,126,128]{2,1,0:T(8,128)(2,1)} %shard_map.55), channel_id=1, source_target_pairs={{0,64},{16,80},{32,96},{48,112},{64,0},{80,16},{96,32},{112,48},{1... | collective-permute-start | bytes 1548296 | tf_op jit(solution)/shard_map/ppermute | solution.py:102
  73.9 16.1 %collective-permute-start = (bf16[16,126,128]{2,1,0:T(8,128)(2,1)}, bf16[16,126,128]{2,1,0:T(8,128)(2,1)S(1)}, u32[]{:S(2)}, u32[]{:S(2)}) collective-permute-start(bf16[16,126,128]{2,1,0:T(8,128)(2,1)} %shard_map.55), channel_id=1, source_target_pairs={{0,16},{16,0},{32,48},{48,32},{64,80},{80,64},{96,112},{112,96},{1... | collective-permute-start | bytes 1548296 | tf_op jit(solution)/shard_map/ppermute | solution.py:101
  86.6 9.1 %collective-permute-start.3 = (bf16[16,126,128]{2,1,0:T(8,128)(2,1)}, bf16[16,126,128]{2,1,0:T(8,128)(2,1)}, u32[]{:S(2)}, u32[]{:S(2)}) collective-permute-start(bf16[16,126,128]{2,1,0:T(8,128)(2,1)} %collective-permute-done.2), channel_id=1, source_target_pairs={{0,16},{16,0},{32,48},{48,32},{64,80},{80,64},{96,112},{112,96},{1... | collective-permute-start | bytes 1548296 | tf_op jit(solution)/shard_map/ppermute | solution.py:103
  90.0 5.6 %copy-start.2 = (bf16[16,126,504]{1,2,0:T(8,128)(2,1)S(1)}, bf16[16,126,504]{1,2,0:T(8,128)(2,1)}, u32[]{:S(2)}) copy-start(bf16[16,126,504]{1,2,0:T(8,128)(2,1)} %all-gather.4.cloned.1.call-done) | copy-start | bytes 6096388
  92.5 6.9 %copy-start.3 = (bf16[16,126,128]{2,1,0:T(8,128)(2,1)S(1)}, bf16[16,126,128]{2,1,0:T(8,128)(2,1)}, u32[]{:S(2)}) copy-start(bf16[16,126,128]{2,1,0:T(8,128)(2,1)} %shard_map.55) | copy-start | bytes 1548292
  92.5 13.2 %collective-permute-start.1 = (f32[504,128]{1,0:T(8,128)S(1)}, f32[504,128]{1,0:T(8,128)S(1)}, u32[]{:S(2)}, u32[]{:S(2)}) collective-permute-start(f32[504,128]{1,0:T(8,128)S(1)} %convolution_bitcast_fusion.1), channel_id=1, source_target_pairs={{0,16},{16,0},{32,48},{48,32},{64,80},{80,64},{96,112},{112,96},{1... | collective-permute-start | bytes 774152 | tf_op jit(solution)/shard_map/ppermute | solution.py:117
  97.6 5.0 %collective-permute-start.4 = (bf16[504,128]{1,0:T(8,128)(2,1)S(1)}, bf16[504,128]{1,0:T(8,128)(2,1)S(1)}, u32[]{:S(2)}, u32[]{:S(2)}) collective-permute-start(bf16[504,128]{1,0:T(8,128)(2,1)S(1)} %get-tuple-element.6), channel_id=1, source_target_pairs={{0,64},{16,80},{32,96},{48,112},{64,0},{80,16},{96,32},{112,48},{1... | collective-permute-start | bytes 387080 | tf_op jit(solution)/shard_map/ppermute | solution.py:113
  98.5 7.2 %collective-permute-start.5 = (bf16[504,128]{1,0:T(8,128)(2,1)S(1)}, bf16[504,128]{1,0:T(8,128)(2,1)S(1)}, u32[]{:S(2)}, u32[]{:S(2)}) collective-permute-start(bf16[504,128]{1,0:T(8,128)(2,1)S(1)} %get-tuple-element.5), channel_id=1, source_target_pairs={{0,80},{16,64},{32,112},{48,96},{64,16},{80,0},{96,48},{112,32},{1... | collective-permute-start | bytes 387080 | tf_op jit(solution)/shard_map/ppermute | solution.py:113
  100.8 8.6 %copy-start.1 = (f32[64,64,128]{2,0,1:T(8,128)S(1)}, f32[64,64,128]{2,0,1:T(8,128)}, u32[]{:S(2)}) copy-start(f32[64,64,128]{2,0,1:T(8,128)} %fusion.7) | copy-start | bytes 6291460
  102.7 3.0 %copy-start.5 = (bf16[504,128]{1,0:T(8,128)(2,1)}, bf16[504,128]{1,0:T(8,128)(2,1)S(1)}, u32[]{:S(2)}) copy-start(bf16[504,128]{1,0:T(8,128)(2,1)S(1)} %collective-permute-done.4.p2) | copy-start | bytes 387076
  105.7 0.6 copy-start.6
  105.7 0.8 copy-start.4
Sparse Core Ops, SparseCore 0:
  9.1 77.9 all-gather.3
